TPU v7x, 128 devices: a whole 4x4x4 slice. The times are simulated.
128 devices in a mesh: leaf: 4 (over z), panel: 32 (over x, y, core).
Axes of the slice: x: 4, y: 4, z: 4, core: 2. Of those that a mesh axis runs over, the one named last changes fastest.
Arguments:
- right_sides: float32 [4, 1024, 32, 256], P('leaf', 'panel'), may hold values from -6 to 6
- inverse: float32 [4, 1024, 256, 256], P('leaf', 'panel'), as said below
- coupling: float32 [4, 1024, 256, 256], P('leaf', 'panel'), may hold values from -0.25 to 0.25
- owner_map: int32 [4, 1024, 1], P('leaf', 'panel'), may hold values from 0 to 31; in each aligned block of 32 rows (0 to 31, 32 to 63, ..., all dimensions but the last counted through in order) at most 2 rows name the same one
- parent_slot: int32 [4, 1024], P('leaf', 'panel'), may hold values from 0 to 31
Outputs:
- forward_solution: float32 [4, 1024, 32, 256], P('leaf', 'panel')
- backward_solution: float32 [4, 1024, 32, 256], P('leaf', 'panel')
Inputs may be any that keep to these rules, and one draw needn't show every extreme that they name: `owner_map`: within the 32 supernodes of one device no owner is named more than 2 times, and some owner is named exactly that often; entries of the top level are not read. `inverse`: each block is upper triangular with a positive diagonal.
All inputs are finite; a program needn't handle non-finite values.
Results may differ from a plain program's by a relative error of at most 0.0001.
Values sent between devices are 32-bit elements; how exact they have to be, the bound alone decides.
No kernel may reach another device: no remote copies, remote signals or barrier semaphores. Data moves between devices by JAX's collectives and lax.ppermute only.
A program may use at most 128 MiB of HBM per device.

v0:
```python
import jax
import jax.numpy as jnp
from jax import lax
from jax.sharding import PartitionSpec as P


def from_behind(block, axis, distance):
    devices = range(lax.axis_size(axis))
    route = [(i - distance, i) for i in devices if i - distance in devices]
    return lax.ppermute(block, axis, route)


def put_block(whole, piece, active):
    return jnp.where(active, piece, whole)


def body(right_sides, inverse, coupling, owner_map, parent_slot):
    highest = lax.Precision.HIGHEST
    levels = lax.axis_size("leaf")
    panels = lax.axis_size("panel")
    level = lax.axis_index("leaf")
    node_count = right_sides.shape[1]
    total_cols = right_sides.shape[2]
    width = right_sides.shape[3]
    capacity = max(2, 2 * node_count // panels)
    slot_count = panels * capacity
    owners = owner_map[0, :, 0]
    positions = parent_slot[0]
    node_iota = jnp.arange(node_count, dtype=jnp.int32)
    same_owner = owners[:, None] == owners[None, :]
    before = node_iota[None, :] < node_iota[:, None]
    slot_rank = jnp.sum((same_owner & before).astype(jnp.int32), axis=1)
    dest_slot = owners * capacity + slot_rank
    slot_iota = jnp.arange(slot_count, dtype=jnp.int32)
    send_onehot = (slot_iota[:, None] == dest_slot[None, :]).astype(jnp.float32)
    send_ids = jnp.dot(send_onehot, (positions + 1).astype(jnp.float32), precision=highest) - 1.0
    node_float = node_iota.astype(jnp.float32)
    block_count = 1
    turns = levels + block_count - 1
    given = right_sides[0]
    diag_inverse = inverse[0]
    couple_block = coupling[0]
    incoming = jnp.zeros((node_count, total_cols, width), jnp.float32)
    solved = jnp.zeros((node_count, total_cols, width), jnp.float32)
    recv_onehot = jnp.zeros((node_count, slot_count), jnp.float32)
    for turn_index in range(turns):
        blk_index = turn_index - level
        active = (blk_index >= 0) & (blk_index < block_count)
        part_in = incoming
        forward_part = jnp.einsum("nrw,nwv->nrv", given - part_in, diag_inverse, precision=highest)
        solved = put_block(solved, forward_part, active)
        if turn_index < turns - 1:
            updates = jnp.einsum("nrw,nwv->nrv", forward_part, couple_block, precision=highest)
            buffer = jnp.einsum("ts,srw->trw", send_onehot, updates, precision=highest)
            arrived, arrived_ids = (
                lax.all_to_all(buffer, "panel", split_axis=0, concat_axis=0, tiled=True),
                lax.all_to_all(send_ids, "panel", split_axis=0, concat_axis=0, tiled=True),
            )
            arrived, arrived_ids = from_behind((arrived, arrived_ids), "leaf", 1)
            recv_onehot = (arrived_ids[None, :] == node_float[:, None]).astype(jnp.float32)
            summed = jnp.einsum("st,trw->srw", recv_onehot, arrived, precision=highest)
            next_index = blk_index + 1
            next_active = (next_index >= 0) & (next_index < block_count)
            incoming = put_block(incoming, summed, next_active)
    height = levels - 1 - level
    lowered = jnp.zeros((node_count, total_cols, width), jnp.float32)
    result = jnp.zeros((node_count, total_cols, width), jnp.float32)
    for turn_index in range(turns):
        blk_index = turn_index - height
        active = (blk_index >= 0) & (blk_index < block_count)
        part_low = lowered
        backward_part = jnp.einsum(
            "nrw,nvw->nrv", solved - part_low, diag_inverse, precision=highest
        )
        result = put_block(result, backward_part, active)
        if turn_index < turns - 1:
            buffer = jnp.einsum("st,srw->trw", recv_onehot, backward_part, precision=highest)
            arrived = from_behind(buffer, "leaf", -1)
            arrived = lax.all_to_all(arrived, "panel", split_axis=0, concat_axis=0, tiled=True)
            picked = jnp.einsum("ts,trw->srw", send_onehot, arrived, precision=highest)
            parent_terms = jnp.einsum("srv,swv->srw", picked, couple_block, precision=highest)
            next_index = blk_index + 1
            next_active = (next_index >= 0) & (next_index < block_count)
            lowered = put_block(lowered, parent_terms, next_active)
    return (solved[None], result[None])


def solution(mesh):
    in_specs = (
        P("leaf", "panel", None, None),
        P("leaf", "panel", None, None),
        P("leaf", "panel", None, None),
        P("leaf", "panel", None),
        P("leaf", "panel"),
    )
    out_specs = (P("leaf", "panel", None, None), P("leaf", "panel", None, None))
    return jax.shard_map(body, mesh=mesh, in_specs=in_specs, out_specs=out_specs, check_vma=False)
```

profile of v0, /device:TPU:1, one launch (start us, length us, event | category | flops | bytes accessed | tf_op | source)
XLA Modules:
  0.0 672.0 jit_solution(18022284892442814882)
XLA Ops:
  2.2 8.7 %fusion.26 = f32[32,32,256]{2,1,0:T(8,128)S(1)} fusion(f32[1,32,256,256]{3,2,1,0:T(8,128)} %param.6, f32[1,32,32,256]{3,2,1,0:T(8,128)} %param.5), kind=kOutput, calls=%fused_computation.26 | convolution fusion | flops 805306368 | bytes 10485760 | tf_op jit(solution)/shard_map/nrw,nwv->nrv/dot_general | solution.py:50
  18.8 36.5 %all_to_all.44 = f32[64,32,256]{2,1,0:T(8,128)S(1)} all-to-all(f32[64,32,256]{2,1,0:T(8,128)S(1)} %copy.55), channel_id=1, replica_groups=mesh['leaf'=4,'panel'=32] {'panel'}, dimensions={0} | all-to-all | bytes 4194304 | tf_op jit(solution)/shard_map/all_to_all | solution.py:56
  77.1 28.0 %collective-permute-done = f32[64]{0:T(128)S(1)} collective-permute-done((f32[64]{0:T(128)S(1)}, f32[64]{0:T(128)S(1)}, u32[]{:S(2)}, u32[]{:S(2)}) %collective-permute-start) | collective-permute-done | bytes 288 | tf_op jit(solution)/shard_map/ppermute | solution.py:10
  107.6 7.6 %fusion.24 = f32[32,32,256]{2,1,0:T(8,128)S(1)} fusion(f32[1,32,256,256]{3,2,1,0:T(8,128)} %param.6, f32[1,32,32,256]{3,2,1,0:T(8,128)S(1)} %copy-done.2, f32[32,32,256]{2,0,1:T(8,128)S(1)} %fusion.92, pred[]{:T(512)S(6)} %and.37), kind=kOutput, calls=%fused_computation.24 | convolution fusion | flops 805830656 | bytes 11534337 | tf_op jit(solution)/shard_map/nrw,nwv->nrv/dot_general | solution.py:50
  115.2 7.6 %fusion.8 = f32[32,32,256]{2,1,0:T(8,128)S(1)} fusion(f32[32,32,256]{2,1,0:T(8,128)S(1)} %fusion.24, f32[1,32,256,256]{3,2,1,0:T(8,128)} %param.7), kind=kOutput, calls=%fused_computation.8 | convolution fusion | flops 805306368 | bytes 10485760 | tf_op jit(solution)/shard_map/nrw,nwv->nrv/dot_general | solution.py:53
  125.7 32.4 %all_to_all.45 = f32[64,32,256]{2,1,0:T(8,128)S(1)} all-to-all(f32[64,32,256]{2,1,0:T(8,128)S(1)} %copy.59), channel_id=1, replica_groups=mesh['leaf'=4,'panel'=32] {'panel'}, dimensions={0} | all-to-all | bytes 4194304 | tf_op jit(solution)/shard_map/all_to_all | solution.py:56
  166.4 43.7 %collective-permute-done.2 = f32[64,32,256]{2,0,1:T(8,128)} collective-permute-done((f32[64,32,256]{2,0,1:T(8,128)}, f32[64,32,256]{2,0,1:T(8,128)}, u32[]{:S(2)}, u32[]{:S(2)}) %collective-permute-start.2) | collective-permute-done | bytes 2097184 | tf_op jit(solution)/shard_map/ppermute | solution.py:10
  212.7 8.8 %fusion.22 = f32[32,32,256]{2,1,0:T(8,128)S(1)} fusion(f32[1,32,256,256]{3,2,1,0:T(8,128)} %param.6, f32[1,32,32,256]{3,2,1,0:T(8,128)S(1)} %copy-done.2, f32[32,32,256]{2,0,1:T(8,128)S(1)} %fusion.90, f32[32,32,256]{2,0,1:T(8,128)S(1)} %fusion.92, pred[]{:T(512)S(6)} %and.37, pred[]{:T(512)S(6)} %and.36), kind=kOutput, calls=%fused_computation.22 | convolution fusion | flops 806092800 | bytes 12582914 | tf_op jit(solution)/shard_map/nrw,nwv->nrv/dot_general | solution.py:50
  229.4 32.4 %all_to_all.46 = f32[64,32,256]{2,1,0:T(8,128)S(1)} all-to-all(f32[64,32,256]{2,1,0:T(8,128)S(1)} %copy.63), channel_id=1, replica_groups=mesh['leaf'=4,'panel'=32] {'panel'}, dimensions={0} | all-to-all | bytes 4194304 | tf_op jit(solution)/shard_map/all_to_all | solution.py:56
  270.2 43.4 %collective-permute-done.3 = f32[64,32,256]{2,0,1:T(8,128)} collective-permute-done((f32[64,32,256]{2,0,1:T(8,128)}, f32[64,32,256]{2,0,1:T(8,128)}, u32[]{:S(2)}, u32[]{:S(2)}) %collective-permute-start.3) | collective-permute-done | bytes 2097184 | tf_op jit(solution)/shard_map/ppermute | solution.py:10
  316.3 10.8 %fusion.34 = f32[32,32,256]{2,1,0:T(8,128)S(1)} fusion(f32[1,32,256,256]{3,2,1,0:T(8,128)} %param.6, f32[1,32,32,256]{3,2,1,0:T(8,128)S(1)} %copy-done.2, f32[32,32,256]{2,0,1:T(8,128)S(1)} %fusion.88, f32[32,32,256]{2,1,0:T(8,128)} %copy-done.9, f32[32,32,256]{2,1,0:T(8,128)} %copy-done.8, f32[32,32,256]{2,1,0:T(8,128)} %copy-done.7, pred[]{:T(512)S(6)} %and.38, ...), kind=kOutput, calls=%fused_computation.34 | convolution fusion | flops 807403520 | bytes 16777220 | tf_op jit(solution)/shard_map/nrw,nwv->nrv/dot_general | solution.py:50
  327.1 7.9 %fusion.18 = f32[32,32,256]{2,1,0:T(8,128)S(1)} fusion(f32[32,32,256]{2,1,0:T(8,128)S(1)} %fusion.34, f32[1,32,256,256]{3,2,1,0:T(8,128)S(1)} %bitcast.98), kind=kOutput, calls=%fused_computation.18 | convolution fusion | flops 805306368 | bytes 10485760 | tf_op jit(solution)/shard_map/nrw,nvw->nrv/dot_general | solution.py:72
  338.0 47.8 %collective-permute-done.4 = f32[64,32,256]{2,0,1:T(8,128)S(1)} collective-permute-done((f32[64,32,256]{2,0,1:T(8,128)S(1)}, f32[64,32,256]{2,0,1:T(8,128)S(1)}, u32[]{:S(2)}, u32[]{:S(2)}) %collective-permute-start.4) | collective-permute-done | bytes 2097184 | tf_op jit(solution)/shard_map/ppermute | solution.py:10
  394.3 28.5 %all-to-all-done.4 = f32[64,32,256]{2,1,0:T(8,128)} async-done(((f32[64,32,256]{2,1,0:T(8,128)}), f32[64,32,256]{2,1,0:T(8,128)}, u32[]{:S(2)}, u32[]{:S(2)}) %all-to-all-start.4) | async-done | bytes 2097184 | tf_op jit(solution)/shard_map/all_to_all | solution.py:79
  426.3 10.3 %fusion.43 = f32[32,32,256]{2,1,0:T(8,128)S(1)} fusion(f32[1,32,256,256]{3,2,1,0:T(8,128)} %param.7, f32[32,32,256]{2,0,1:T(8,128)S(1)} %fusion.32, pred[]{:T(512)S(6)} %and.41), kind=kOutput, calls=%fused_computation.37 | convolution fusion | flops 805568512 | bytes 10485761 | tf_op jit(solution)/shard_map/srv,swv->srw/dot_general | solution.py:81
  436.6 10.4 %fusion.16 = f32[32,32,256]{2,1,0:T(8,128)S(1)} fusion(f32[1,32,256,256]{3,2,1,0:T(8,128)} %param.6, f32[32,32,256]{2,1,0:T(8,128)S(1)} %fusion.34, f32[32,32,256]{2,1,0:T(8,128)S(1)} %fusion.43), kind=kOutput, calls=%fused_computation.16 | convolution fusion | flops 805568512 | bytes 11534336 | tf_op jit(solution)/shard_map/nrw,nvw->nrv/dot_general | solution.py:72
  451.1 47.3 %collective-permute-done.5 = f32[64,32,256]{2,0,1:T(8,128)S(1)} collective-permute-done((f32[64,32,256]{2,0,1:T(8,128)S(1)}, f32[64,32,256]{2,0,1:T(8,128)S(1)}, u32[]{:S(2)}, u32[]{:S(2)}) %collective-permute-start.5) | collective-permute-done | bytes 2097184 | tf_op jit(solution)/shard_map/ppermute | solution.py:10
  507.4 28.3 %all-to-all-done.5 = f32[64,32,256]{2,1,0:T(8,128)} async-done(((f32[64,32,256]{2,1,0:T(8,128)}), f32[64,32,256]{2,1,0:T(8,128)}, u32[]{:S(2)}, u32[]{:S(2)}) %all-to-all-start.5) | async-done | bytes 2097184 | tf_op jit(solution)/shard_map/all_to_all | solution.py:79
  539.2 11.5 %fusion.46 = f32[32,32,256]{2,1,0:T(8,128)S(1)} fusion(f32[32,32,256]{2,1,0:T(8,128)} %copy-done.10, f32[1,32,256,256]{3,2,1,0:T(8,128)} %param.7, f32[32,32,256]{2,0,1:T(8,128)S(1)} %fusion.30, pred[]{:T(512)S(6)} %and.40), kind=kOutput, calls=%fused_computation.38 | convolution fusion | flops 805568512 | bytes 11534337 | tf_op jit(solution)/shard_map/srv,swv->srw/dot_general | solution.py:81
  550.8 10.0 %fusion.14 = f32[32,32,256]{2,1,0:T(8,128)S(1)} fusion(f32[1,32,256,256]{3,2,1,0:T(8,128)} %param.6, f32[32,32,256]{2,1,0:T(8,128)S(1)} %fusion.34, f32[32,32,256]{2,1,0:T(8,128)S(1)} %fusion.46), kind=kOutput, calls=%fused_computation.14 | convolution fusion | flops 805568512 | bytes 11534336 | tf_op jit(solution)/shard_map/nrw,nvw->nrv/dot_general | solution.py:72
  564.8 46.9 %collective-permute-done.6 = f32[64,32,256]{2,0,1:T(8,128)S(1)} collective-permute-done((f32[64,32,256]{2,0,1:T(8,128)S(1)}, f32[64,32,256]{2,0,1:T(8,128)S(1)}, u32[]{:S(2)}, u32[]{:S(2)}) %collective-permute-start.6) | collective-permute-done | bytes 2097184 | tf_op jit(solution)/shard_map/ppermute | solution.py:10
  620.7 28.3 %all-to-all-done.6 = f32[64,32,256]{2,1,0:T(8,128)} async-done(((f32[64,32,256]{2,1,0:T(8,128)}), f32[64,32,256]{2,1,0:T(8,128)}, u32[]{:S(2)}, u32[]{:S(2)}) %all-to-all-start.6) | async-done | bytes 2097184 | tf_op jit(solution)/shard_map/all_to_all | solution.py:79
  652.7 10.3 %fusion.52 = f32[32,32,256]{2,1,0:T(8,128)S(1)} fusion(f32[32,32,256]{2,1,0:T(8,128)S(1)} %fusion.34, f32[32,32,256]{2,1,0:T(8,128)S(1)} %fusion.46, f32[1,32,256,256]{3,2,1,0:T(8,128)} %param.7, f32[32,32,256]{2,0,1:T(8,128)S(1)} %fusion.28, pred[]{:T(512)S(6)} %and.39), kind=kOutput, calls=%fused_computation.40 | convolution fusion | flops 805830656 | bytes 12582913 | tf_op jit(solution)/shard_map/srv,swv->srw/dot_general | solution.py:81
  663.1 8.8 %fusion.40 = f32[1,32,32,256]{3,2,1,0:T(8,128)} fusion(f32[32,32,256]{2,1,0:T(8,128)S(1)} %fusion.52, f32[1,32,256,256]{3,2,1,0:T(8,128)S(1)} %bitcast.100, f32[32,32,256]{2,1,0:T(8,128)S(1)} %copy-done.6, f32[32,32,256]{2,1,0:T(8,128)S(1)} %copy-done.4, f32[32,32,256]{2,1,0:T(8,128)S(1)} %fusion.18, pred[]{:T(512)S(6)} %and.42, pred[]{:T(512)S(6)} %and.41, ...), kind=kOutput, calls=%fused_computation.36 | convolution fusion | flops 806354944 | bytes 13631492 | tf_op jit(solution)/shard_map/nrw,nvw->nrv/dot_general | solution.py:72
  (85 shorter events, 114.4 us)
Async XLA Ops:
  2.2 8.7 %copy-start = (f32[1,32,256,256]{3,2,1,0:T(8,128)S(1)}, f32[1,32,256,256]{3,2,1,0:T(8,128)}, u32[]{:S(2)}) copy-start(f32[1,32,256,256]{3,2,1,0:T(8,128)} %param.7) | copy-start | bytes 25165828
  56.5 51.1 %copy-start.2 = (f32[1,32,32,256]{3,2,1,0:T(8,128)S(1)}, f32[1,32,32,256]{3,2,1,0:T(8,128)}, u32[]{:S(2)}) copy-start(f32[1,32,32,256]{3,2,1,0:T(8,128)} %param.5) | copy-start | bytes 3145732
  56.5 48.6 %collective-permute-start.1 = (f32[64,32,256]{2,0,1:T(8,128)S(1)}, f32[64,32,256]{2,0,1:T(8,128)}, u32[]{:S(2)}, u32[]{:S(2)}) collective-permute-start(f32[64,32,256]{2,0,1:T(8,128)S(1)} %copy.56), channel_id=1, source_target_pairs={{0,32},{32,64},{64,96},{1,33},{33,65},{65,97},{2,34},{34,66},{66,9... | collective-permute-start | bytes 6291464 | tf_op jit(solution)/shard_map/ppermute | solution.py:10
  62.5 11.1 %all-to-all-start = ((f32[32,2,1]{1,2,0:T(1,128)}), f32[32,2,1]{1,2,0:T(1,128)S(1)}, u32[]{:S(2)}, u32[]{:S(2)}) async-start(f32[32,2,1]{1,2,0:T(1,128)} %bitcast.5), calls=%async_computation | async-start | bytes 32768 | tf_op jit(solution)/shard_map/all_to_all | solution.py:57
  74.9 30.2 %collective-permute-start = (f32[64]{0:T(128)S(1)}, f32[64]{0:T(128)S(1)}, u32[]{:S(2)}, u32[]{:S(2)}) collective-permute-start(f32[64]{0:T(128)S(1)} %all_to_all.30), channel_id=1, source_target_pairs={{0,32},{32,64},{64,96},{1,33},{33,65},{65,97},{2,34},{34,66},{66,9... | collective-permute-start | bytes 776 | tf_op jit(solution)/shard_map/ppermute | solution.py:10
  160.7 49.4 %collective-permute-start.2 = (f32[64,32,256]{2,0,1:T(8,128)}, f32[64,32,256]{2,0,1:T(8,128)}, u32[]{:S(2)}, u32[]{:S(2)}) collective-permute-start(f32[64,32,256]{2,0,1:T(8,128)} %copy.60), channel_id=1, source_target_pairs={{0,32},{32,64},{64,96},{1,33},{33,65},{65,97},{2,34},{34,66},{66,9... | collective-permute-start | bytes 6291464 | tf_op jit(solution)/shard_map/ppermute | solution.py:10
  210.0 11.5 %slice-start.4 = ((s8[8388608]{0:T(1024)(128)(4,1)}), s8[4194304]{0:T(1024)(128)(4,1)S(1)}, s32[]{:S(2)}) async-start(s8[8388608]{0:T(1024)(128)(4,1)} %bitcast.101), calls=%async_computation.11 | async-start | bytes 8388608
  212.6 8.9 %copy-start.11 = (f32[32,32,256]{2,0,1:T(8,128)}, f32[32,32,256]{2,0,1:T(8,128)S(1)}, u32[]{:S(2)}) copy-start(f32[32,32,256]{2,0,1:T(8,128)S(1)} %fusion.90) | copy-start | bytes 3145732
  212.7 8.9 %slice-start.5 = ((s8[8388608]{0:T(1024)(128)(4,1)}), s8[4194304]{0:T(1024)(128)(4,1)S(1)}, s32[]{:S(2)}) async-start(s8[8388608]{0:T(1024)(128)(4,1)} %bitcast.101), calls=%async_computation.12 | async-start | bytes 8388608
  264.4 49.3 %collective-permute-start.3 = (f32[64,32,256]{2,0,1:T(8,128)}, f32[64,32,256]{2,0,1:T(8,128)}, u32[]{:S(2)}, u32[]{:S(2)}) collective-permute-start(f32[64,32,256]{2,0,1:T(8,128)} %copy.64), channel_id=1, source_target_pairs={{0,32},{32,64},{64,96},{1,33},{33,65},{65,97},{2,34},{34,66},{66,9... | collective-permute-start | bytes 6291464 | tf_op jit(solution)/shard_map/ppermute | solution.py:10
  313.7 13.4 %slice-start = ((s8[8388608]{0:T(1024)(128)(4,1)}), s8[4194304]{0:T(1024)(128)(4,1)S(1)}, s32[]{:S(2)}) async-start(s8[8388608]{0:T(1024)(128)(4,1)} %bitcast.97), calls=%async_computation.7 | async-start | bytes 8388608
  316.3 10.8 %slice-start.1 = ((s8[8388608]{0:T(1024)(128)(4,1)}), s8[4194304]{0:T(1024)(128)(4,1)S(1)}, s32[]{:S(2)}) async-start(s8[8388608]{0:T(1024)(128)(4,1)} %bitcast.97), calls=%async_computation.8 | async-start | bytes 8388608
  327.1 325.6 %copy-start.1 = (f32[32,32,256]{2,1,0:T(8,128)}, f32[32,32,256]{2,1,0:T(8,128)S(1)}, u32[]{:S(2)}) copy-start(f32[32,32,256]{2,1,0:T(8,128)S(1)} %fusion.34) | copy-start | bytes 3145732
  336.7 49.1 %collective-permute-start.4 = (f32[64,32,256]{2,0,1:T(8,128)S(1)}, f32[64,32,256]{2,0,1:T(8,128)S(1)}, u32[]{:S(2)}, u32[]{:S(2)}) collective-permute-start(f32[64,32,256]{2,0,1:T(8,128)S(1)} %fusion.64), channel_id=1, source_target_pairs={{32,0},{64,32},{96,64},{33,1},{65,33},{97,65},{34,2},{66,34},{98,6... | collective-permute-start | bytes 6291464 | tf_op jit(solution)/shard_map/ppermute | solution.py:10
  388.4 34.4 %all-to-all-start.4 = ((f32[64,32,256]{2,1,0:T(8,128)}), f32[64,32,256]{2,1,0:T(8,128)}, u32[]{:S(2)}, u32[]{:S(2)}) async-start(f32[64,32,256]{2,1,0:T(8,128)} %copy.67), calls=%async_computation.4 | async-start | bytes 4194304 | tf_op jit(solution)/shard_map/all_to_all | solution.py:79
  436.6 10.5 %copy-start.10 = (f32[32,32,256]{2,1,0:T(8,128)}, f32[32,32,256]{2,1,0:T(8,128)S(1)}, u32[]{:S(2)}) copy-start(f32[32,32,256]{2,1,0:T(8,128)S(1)} %fusion.43) | copy-start | bytes 3145732
  449.8 48.6 %collective-permute-start.5 = (f32[64,32,256]{2,0,1:T(8,128)S(1)}, f32[64,32,256]{2,0,1:T(8,128)S(1)}, u32[]{:S(2)}, u32[]{:S(2)}) collective-permute-start(f32[64,32,256]{2,0,1:T(8,128)S(1)} %fusion.61), channel_id=1, source_target_pairs={{32,0},{64,32},{96,64},{33,1},{65,33},{97,65},{34,2},{66,34},{98,6... | collective-permute-start | bytes 6291464 | tf_op jit(solution)/shard_map/ppermute | solution.py:10
  500.9 34.7 %all-to-all-start.5 = ((f32[64,32,256]{2,1,0:T(8,128)}), f32[64,32,256]{2,1,0:T(8,128)}, u32[]{:S(2)}, u32[]{:S(2)}) async-start(f32[64,32,256]{2,1,0:T(8,128)} %copy.71), calls=%async_computation.5 | async-start | bytes 4194304 | tf_op jit(solution)/shard_map/all_to_all | solution.py:79
  563.5 48.2 %collective-permute-start.6 = (f32[64,32,256]{2,0,1:T(8,128)S(1)}, f32[64,32,256]{2,0,1:T(8,128)S(1)}, u32[]{:S(2)}, u32[]{:S(2)}) collective-permute-start(f32[64,32,256]{2,0,1:T(8,128)S(1)} %fusion.58), channel_id=1, source_target_pairs={{32,0},{64,32},{96,64},{33,1},{65,33},{97,65},{34,2},{66,34},{98,6... | collective-permute-start | bytes 6291464 | tf_op jit(solution)/shard_map/ppermute | solution.py:10
  614.3 34.7 %all-to-all-start.6 = ((f32[64,32,256]{2,1,0:T(8,128)}), f32[64,32,256]{2,1,0:T(8,128)}, u32[]{:S(2)}, u32[]{:S(2)}) async-start(f32[64,32,256]{2,1,0:T(8,128)} %copy.75), calls=%async_computation.6 | async-start | bytes 4194304 | tf_op jit(solution)/shard_map/all_to_all | solution.py:79
  648.9 14.1 %slice-start.2 = ((s8[8388608]{0:T(1024)(128)(4,1)}), s8[4194304]{0:T(1024)(128)(4,1)S(1)}, s32[]{:S(2)}) async-start(s8[8388608]{0:T(1024)(128)(4,1)} %bitcast.99), calls=%async_computation.9 | async-start | bytes 8388608
  652.7 10.4 %slice-start.3 = ((s8[8388608]{0:T(1024)(128)(4,1)}), s8[4194304]{0:T(1024)(128)(4,1)S(1)}, s32[]{:S(2)}) async-start(s8[8388608]{0:T(1024)(128)(4,1)} %bitcast.99), calls=%async_computation.10 | async-start | bytes 8388608
  652.7 10.4 %copy-start.4 = (f32[32,32,256]{2,1,0:T(8,128)S(1)}, f32[32,32,256]{2,1,0:T(8,128)}, u32[]{:S(2)}) copy-start(f32[32,32,256]{2,1,0:T(8,128)} %copy-done.3) | copy-start | bytes 3145732
  652.7 10.4 %copy-start.6 = (f32[32,32,256]{2,1,0:T(8,128)S(1)}, f32[32,32,256]{2,1,0:T(8,128)}, u32[]{:S(2)}) copy-start(f32[32,32,256]{2,1,0:T(8,128)} %copy-done.5) | copy-start | bytes 3145732
  (6 other events, 25.7 us)
where the time goes:
time: 681 us; the launch traced here: 672 us
  waiting for transfers between devices  349 us (51%)
  matrix products  151 us (22%)
  blocking collectives  101 us (15%)
  starting transfers between devices  45.6 us (7%)
  local copies, waits for them, and re-layouts  21.1 us (3%)
    ppermute x7, waiting for transfers between devices, from_behind(): return lax.ppermute(block, axis, route)  257 us
    all_to_all x3, blocking collectives, body(): lax.all_to_all(buffer, 'panel', split_axis=0, concat_axis=0, tiled=True)  101 us
    all_to_all x3, waiting for transfers between devices, body(): lax.all_to_all(arrived, 'panel', split_axis=0, concat_axis=0, tiled=True)  85 us
    dot_general x4, matrix products, body(): jnp.einsum('nrw,nvw->nrv', solved - part_low, diag_inverse, precision=hig...  37.1 us
    dot_general x4, matrix products, body(): jnp.einsum('nrw,nwv->nrv', given - part_in, diag_inverse, precision=highest)  35.9 us
    dot_general x3, matrix products, body(): jnp.einsum('srv,swv->srw', picked, couple_block, precision=highest)  32.1 us
    ppermute x7, starting transfers between devices, from_behind(): return lax.ppermute(block, axis, route)  22.6 us
    all_to_all x3, starting transfers between devices, body(): lax.all_to_all(arrived, 'panel', split_axis=0, concat_axis=0, tiled=True)  18.7 us
  transfers between devices with their start and end apart: 11, of which 10 were waited for; matrix products, arithmetic and copies ran while one was open for 0% of the time, Pallas kernels for 0%

commit v1 on v0

v1 whole, which is shorter than its diff:
```python
import jax
import jax.numpy as jnp
from jax import lax
from jax.sharding import PartitionSpec as P

CHUNKS = 1
MAIN_PRECISION = lax.Precision.HIGHEST


def shift_leaf(block, pairs):
    if not pairs:
        return jnp.zeros_like(block)
    return lax.ppermute(block, "leaf", pairs)


def pick_chunk(chunks, index):
    out = chunks[0]
    for j in range(1, len(chunks)):
        out = jnp.where(index == j, chunks[j], out)
    return out


def store_chunk(chunks, index, piece):
    return [jnp.where(index == j, piece, c) for j, c in enumerate(chunks)]


def body(right_sides, inverse, coupling, owner_map, parent_slot):
    highest = lax.Precision.HIGHEST
    main = MAIN_PRECISION
    levels = lax.axis_size("leaf")
    panels = lax.axis_size("panel")
    level = lax.axis_index("leaf")
    node_count = right_sides.shape[1]
    total_cols = right_sides.shape[2]
    width = right_sides.shape[3]
    capacity = max(2, 2 * node_count // panels)
    slot_count = panels * capacity
    owners = owner_map[0, :, 0]
    positions = parent_slot[0]
    node_iota = jnp.arange(node_count, dtype=jnp.int32)
    same_owner = owners[:, None] == owners[None, :]
    before = node_iota[None, :] < node_iota[:, None]
    slot_rank = jnp.sum((same_owner & before).astype(jnp.int32), axis=1)
    dest_slot = owners * capacity + slot_rank
    slot_iota = jnp.arange(slot_count, dtype=jnp.int32)
    send_onehot = (slot_iota[:, None] == dest_slot[None, :]).astype(jnp.float32)
    send_ids = jnp.dot(send_onehot, (positions + 1).astype(jnp.float32), precision=highest) - 1.0
    arrived_ids = lax.all_to_all(send_ids, "panel", split_axis=0, concat_axis=0, tiled=True)
    node_float = node_iota.astype(jnp.float32)
    recv_onehot = (arrived_ids[None, :] == node_float[:, None]).astype(jnp.float32)

    chunks = CHUNKS
    rows = total_cols // chunks
    given = [right_sides[0, :, j * rows:(j + 1) * rows] for j in range(chunks)]
    diag_inverse = inverse[0]
    couple_block = coupling[0]
    zero_chunk = jnp.zeros((node_count, rows, width), jnp.float32)
    solved = [zero_chunk] * chunks
    result = [zero_chunk] * chunks
    incoming = zero_chunk
    picked = zero_chunk
    top = levels - 1
    turns = 2 * top + chunks
    for turn in range(turns):
        fwd_levels = [l for l in range(levels) if 0 <= turn - l < chunks]
        bwd_levels = [l for l in range(levels) if 0 <= turn - 2 * top + l < chunks]
        if fwd_levels:
            f_index = turn - level
            f_active = (f_index >= 0) & (f_index < chunks)
            rhs = pick_chunk(given, f_index)
            forward_part = jnp.einsum("nrw,nwv->nrv", rhs - incoming, diag_inverse, precision=main)
            solved = store_chunk(solved, jnp.where(f_active, f_index, -1), forward_part)
        if bwd_levels:
            b_index = turn - 2 * top + level
            b_active = (b_index >= 0) & (b_index < chunks)
            source = pick_chunk(solved, b_index)
            if any(l < top for l in bwd_levels):
                lowered = jnp.einsum("nrv,nwv->nrw", picked, couple_block, precision=main)
                source = source - lowered
            backward_part = jnp.einsum("nrw,nvw->nrv", source, diag_inverse, precision=main)
            result = store_chunk(result, jnp.where(b_active, b_index, -1), backward_part)
        senders = [l for l in fwd_levels if l < top]
        if senders:
            updates = jnp.einsum("nrw,nwv->nrv", forward_part, couple_block, precision=main)
            buffer = jnp.einsum("ts,srw->trw", send_onehot, updates, precision=highest)
            arrived = lax.all_to_all(buffer, "panel", split_axis=0, concat_axis=0, tiled=True)
            summed = jnp.einsum("st,trw->srw", recv_onehot, arrived, precision=highest)
            incoming = shift_leaf(summed, [(l, l + 1) for l in senders])
        else:
            incoming = zero_chunk
        down = [l for l in bwd_levels if l > 0]
        if down:
            lowered_in = shift_leaf(backward_part, [(l, l - 1) for l in down])
            buffer = jnp.einsum("st,srw->trw", recv_onehot, lowered_in, precision=highest)
            arrived = lax.all_to_all(buffer, "panel", split_axis=0, concat_axis=0, tiled=True)
            picked = jnp.einsum("ts,trw->srw", send_onehot, arrived, precision=highest)
        else:
            picked = zero_chunk
    solved_all = jnp.concatenate(solved, axis=1)
    result_all = jnp.concatenate(result, axis=1)
    return (solved_all[None], result_all[None])


def solution(mesh):
    in_specs = (
        P("leaf", "panel", None, None),
        P("leaf", "panel", None, None),
        P("leaf", "panel", None, None),
        P("leaf", "panel", None),
        P("leaf", "panel"),
    )
    out_specs = (P("leaf", "panel", None, None), P("leaf", "panel", None, None))
    return jax.shard_map(body, mesh=mesh, in_specs=in_specs, out_specs=out_specs, check_vma=False)
```

time: 681 us -> 520 us (0.76)
  waiting for transfers between devices: 349 us -> 201 us
  blocking collectives: 101 us -> 129 us
  matrix products: 151 us -> 133 us
  starting transfers between devices: 45.6 us -> 29.6 us
  local copies, waits for them, and re-layouts: 21.1 us -> 11.8 us
    ppermute x7 -> x6, waiting for transfers between devices: 257 us -> 145 us  [shift_leaf(): return lax.ppermute(block, 'leaf', pairs)]
    all_to_all x3 -> x2, waiting for transfers between devices: 85 us -> 55.4 us  [body(): lax.all_to_all(buffer, 'panel', split_axis=0, concat_axis=0, tiled=True)]
    all_to_all x3 -> x4, blocking collectives: 101 us -> 129 us  [body(): lax.all_to_all(buffer, 'panel', split_axis=0, concat_axis=0, tiled=True)]
    dot_general x17, matrix products: 128 us -> 112 us  [the longest x4 35.9 us: body(): jnp.einsum('nrw,nvw->nrv', source, diag_inverse, precision=main)]
    ppermute x7 -> x6, starting transfers between devices: 22.6 us -> 9.2 us  [shift_leaf(): return lax.ppermute(block, 'leaf', pairs)]
    ppermute x3 -> x0, local copies, waits for them, and re-layouts: 7.65 us -> none  [from_behind(): return lax.ppermute(block, axis, route)]
    all_to_all x3 -> x2, starting transfers between devices: 18.7 us -> 11.8 us  [body(): lax.all_to_all(buffer, 'panel', split_axis=0, concat_axis=0, tiled=True)]
    all_to_all x1, waiting for transfers between devices: 6.88 us -> 0.01 us  [body(): lax.all_to_all(send_ids, 'panel', split_axis=0, concat_axis=0, tiled=True)]
  transfers between devices with their start and end apart: 11 -> 9, of which waited for: 10 -> 4; matrix products, arithmetic and copies ran while one was open for 0% -> 4% of each run, Pallas kernels for 0% -> 0%
where the time goes in v1:
time: 520 us; the launch traced here: 511 us
  waiting for transfers between devices  201 us (39%)
  matrix products  133 us (26%)
  blocking collectives  129 us (25%)
  starting transfers between devices  29.6 us (6%)
  local copies, waits for them, and re-layouts  11.8 us (2%)
  other arithmetic  5.57 us (1%)
    ppermute x6, waiting for transfers between devices, shift_leaf(): return lax.ppermute(block, 'leaf', pairs)  145 us
    all_to_all x4, blocking collectives, body(): lax.all_to_all(buffer, 'panel', split_axis=0, concat_axis=0, tiled=True)  129 us
    all_to_all x2, waiting for transfers between devices, body(): lax.all_to_all(buffer, 'panel', split_axis=0, concat_axis=0, tiled=True)  55.4 us
    dot_general x4, matrix products, body(): jnp.einsum('nrw,nvw->nrv', source, diag_inverse, precision=main)  35.9 us
    dot_general x4, matrix products, body(): jnp.einsum('nrw,nwv->nrv', rhs - incoming, diag_inverse, precision=main)  30.2 us
    dot_general x3, matrix products, body(): lowered = jnp.einsum('nrv,nwv->nrw', picked, couple_block, precision=main)  26.4 us
    dot_general x3, matrix products, body(): jnp.einsum('nrw,nwv->nrv', forward_part, couple_block, precision=main)  14.6 us
    all_to_all x2, starting transfers between devices, body(): lax.all_to_all(buffer, 'panel', split_axis=0, concat_axis=0, tiled=True)  11.8 us
  transfers between devices with their start and end apart: 9, of which 4 were waited for; matrix products, arithmetic and copies ran while one was open for 4% of the time, Pallas kernels for 0%

profile of v1, /device:TPU:1, one launch (start us, length us, event | category | flops | bytes accessed | tf_op | source)
XLA Modules:
  0.0 511.0 jit_solution(9089394296832107681)
XLA Ops:
  3.8 8.6 %all-to-all-start = ((f32[32,2,1]{1,2,0:T(1,128)}), f32[32,2,1]{1,2,0:T(1,128)S(1)}, u32[]{:S(2)}, u32[]{:S(2)}) async-start(f32[32,2,1]{1,2,0:T(1,128)} %bitcast.5), calls=%async_computation | async-start | bytes 32768 | tf_op jit(solution)/shard_map/all_to_all | solution.py:48
  12.4 8.7 %fusion.26 = f32[32,32,256]{2,1,0:T(8,128)S(1)} fusion(f32[1,32,256,256]{3,2,1,0:T(8,128)} %param.6, f32[1,32,32,256]{3,2,1,0:T(8,128)} %param.5), kind=kOutput, calls=%fused_computation.26 | convolution fusion | flops 805306368 | bytes 10485760 | tf_op jit(solution)/shard_map/nrw,nwv->nrv/dot_general | solution.py:71
  21.1 4.9 fusion.10
  30.2 7.4 %all-to-all-start.1 = ((f32[64,32,256]{2,1,0:T(8,128)}), f32[64,32,256]{2,1,0:T(8,128)}, u32[]{:S(2)}, u32[]{:S(2)}) async-start(f32[64,32,256]{2,1,0:T(8,128)} %copy.53), calls=%async_computation.1 | async-start | bytes 4194304 | tf_op jit(solution)/shard_map/all_to_all | solution.py:86
  39.0 27.1 %all-to-all-done.1 = f32[64,32,256]{2,1,0:T(8,128)} async-done(((f32[64,32,256]{2,1,0:T(8,128)}), f32[64,32,256]{2,1,0:T(8,128)}, u32[]{:S(2)}, u32[]{:S(2)}) %all-to-all-start.1) | async-done | bytes 2097184 | tf_op jit(solution)/shard_map/all_to_all | solution.py:86
  73.4 21.6 %collective-permute-done = f32[32,32,256]{2,0,1:T(8,128)S(1)} collective-permute-done((f32[32,32,256]{2,0,1:T(8,128)S(1)}, f32[32,32,256]{2,0,1:T(8,128)S(1)}, u32[]{:S(2)}, u32[]{:S(2)}) %collective-permute-start) | collective-permute-done | bytes 1048608 | tf_op jit(solution)/shard_map/ppermute | solution.py:13
  95.7 7.7 %fusion.24 = f32[32,32,256]{2,1,0:T(8,128)S(1)} fusion(f32[1,32,256,256]{3,2,1,0:T(8,128)} %param.6, f32[32,32,256]{2,0,1:T(8,128)S(1)} %bitcast_subtract_fusion.1), kind=kOutput, calls=%fused_computation.24 | convolution fusion | flops 805306368 | bytes 10485760 | tf_op jit(solution)/shard_map/nrw,nwv->nrv/dot_general | solution.py:71
  103.5 4.9 fusion.8
  111.3 33.0 %all_to_all.39 = f32[64,32,256]{2,1,0:T(8,128)S(1)} all-to-all(f32[64,32,256]{2,1,0:T(8,128)S(1)} %copy.57), channel_id=1, replica_groups=mesh['leaf'=4,'panel'=32] {'panel'}, dimensions={0} | all-to-all | bytes 4194304 | tf_op jit(solution)/shard_map/all_to_all | solution.py:86
  148.0 5.3 %fusion.22 = f32[32,32,256]{2,1,0:T(8,128)S(1)} fusion(f32[1,32,256,256]{3,2,1,0:T(8,128)S(1)} %bitcast.93, f32[32,32,256]{2,0,1:T(8,128)S(1)} %bitcast_subtract_fusion), kind=kOutput, calls=%fused_computation.22 | convolution fusion | flops 805306368 | bytes 10485760 | tf_op jit(solution)/shard_map/nrw,nwv->nrv/dot_general | solution.py:71
  153.3 4.9 fusion.6
  161.6 31.9 %all_to_all.40 = f32[64,32,256]{2,1,0:T(8,128)S(1)} all-to-all(f32[64,32,256]{2,1,0:T(8,128)S(1)} %copy.61), channel_id=1, replica_groups=mesh['leaf'=4,'panel'=32] {'panel'}, dimensions={0} | all-to-all | bytes 4194304 | tf_op jit(solution)/shard_map/all_to_all | solution.py:86
  200.2 8.5 %fusion.40 = f32[32,32,256]{2,1,0:T(8,128)S(1)} fusion(f32[1,32,256,256]{3,2,1,0:T(8,128)} %param.6, f32[32,32,256]{2,0,1:T(8,128)S(1)} %bitcast_subtract_fusion.2, f32[32,32,256]{2,1,0:T(8,128)S(1)} %copy-done.4, f32[32,32,256]{2,1,0:T(8,128)S(1)} %fusion.24, f32[32,32,256]{2,1,0:T(8,128)S(1)} %fusion.26, pred[]{:T(512)S(6)} %eq.78, pred[]{:T(512)S(6)} %eq.77, ...), kind=kOutput, calls=%fused_computation.40 | convolution fusion | flops 806354944 | bytes 13631492 | tf_op jit(solution)/shard_map/nrw,nwv->nrv/dot_general | solution.py:71
  208.8 7.8 %fusion.18 = f32[32,32,256]{2,1,0:T(8,128)S(1)} fusion(f32[32,32,256]{2,1,0:T(8,128)S(1)} %fusion.40, f32[1,32,256,256]{3,2,1,0:T(8,128)S(1)} %bitcast.95), kind=kOutput, calls=%fused_computation.18 | convolution fusion | flops 805306368 | bytes 10485760 | tf_op jit(solution)/shard_map/nrw,nvw->nrv/dot_general | solution.py:80
  220.6 31.9 %all_to_all.41 = f32[64,32,256]{2,1,0:T(8,128)S(1)} all-to-all(f32[64,32,256]{2,1,0:T(8,128)S(1)} %copy.65), channel_id=1, replica_groups=mesh['leaf'=4,'panel'=32] {'panel'}, dimensions={0} | all-to-all | bytes 4194304 | tf_op jit(solution)/shard_map/all_to_all | solution.py:95
  254.6 8.0 %fusion.49 = f32[32,32,256]{2,1,0:T(8,128)S(1)} fusion(f32[32,32,256]{2,1,0:T(8,128)S(1)} %fusion.40, f32[1,32,256,256]{3,2,1,0:T(8,128)S(1)} %bitcast.99, f32[32,32,256]{2,0,1:T(8,128)S(1)} %fusion.32), kind=kOutput, calls=%fused_computation.43 | convolution fusion | flops 805568512 | bytes 11534336 | tf_op jit(solution)/shard_map/nrv,nwv->nrw/dot_general | solution.py:78
  262.6 8.2 %fusion.16 = f32[32,32,256]{2,1,0:T(8,128)S(1)} fusion(f32[32,32,256]{2,1,0:T(8,128)S(1)} %fusion.49, f32[1,32,256,256]{3,2,1,0:T(8,128)S(1)} %bitcast.95), kind=kOutput, calls=%fused_computation.16 | convolution fusion | flops 805306368 | bytes 10485760 | tf_op jit(solution)/shard_map/nrw,nvw->nrv/dot_general | solution.py:80
  274.4 31.9 %all_to_all.42 = f32[64,32,256]{2,1,0:T(8,128)S(1)} all-to-all(f32[64,32,256]{2,1,0:T(8,128)S(1)} %copy.69), channel_id=1, replica_groups=mesh['leaf'=4,'panel'=32] {'panel'}, dimensions={0} | all-to-all | bytes 4194304 | tf_op jit(solution)/shard_map/all_to_all | solution.py:95
  308.4 8.0 %fusion.52 = f32[32,32,256]{2,1,0:T(8,128)S(1)} fusion(f32[32,32,256]{2,1,0:T(8,128)S(1)} %fusion.40, f32[1,32,256,256]{3,2,1,0:T(8,128)S(1)} %bitcast.99, f32[32,32,256]{2,0,1:T(8,128)S(1)} %fusion.30), kind=kOutput, calls=%fused_computation.44 | convolution fusion | flops 805568512 | bytes 11534336 | tf_op jit(solution)/shard_map/nrv,nwv->nrw/dot_general | solution.py:78
  316.4 7.9 %fusion.14 = f32[32,32,256]{2,1,0:T(8,128)S(1)} fusion(f32[32,32,256]{2,1,0:T(8,128)S(1)} %fusion.52, f32[1,32,256,256]{3,2,1,0:T(8,128)S(1)} %bitcast.95), kind=kOutput, calls=%fused_computation.14 | convolution fusion | flops 805306368 | bytes 10485760 | tf_op jit(solution)/shard_map/nrw,nvw->nrv/dot_general | solution.py:80
  325.7 123.5 %collective-permute-done.5 = f32[32,32,256]{2,1,0:T(8,128)S(1)} collective-permute-done((f32[32,32,256]{2,1,0:T(8,128)S(1)}, f32[32,32,256]{2,1,0:T(8,128)S(1)}, u32[]{:S(2)}, u32[]{:S(2)}) %collective-permute-start.5) | collective-permute-done | bytes 1048608 | tf_op jit(solution)/shard_map/ppermute | solution.py:13
  457.8 28.4 %all-to-all-done.6 = f32[64,32,256]{2,1,0:T(8,128)S(1)} async-done(((f32[64,32,256]{2,1,0:T(8,128)}), f32[64,32,256]{2,1,0:T(8,128)S(1)}, u32[]{:S(2)}, u32[]{:S(2)}) %all-to-all-start.6) | async-done | bytes 2097184 | tf_op jit(solution)/shard_map/all_to_all | solution.py:95
  488.4 10.4 %fusion.55 = f32[32,32,256]{2,1,0:T(8,128)S(1)} fusion(f32[32,32,256]{2,1,0:T(8,128)S(1)} %fusion.40, f32[1,32,256,256]{3,2,1,0:T(8,128)} %param.7, f32[32,32,256]{2,0,1:T(8,128)S(1)} %fusion.28), kind=kOutput, calls=%fused_computation.45 | convolution fusion | flops 805568512 | bytes 11534336 | tf_op jit(solution)/shard_map/nrv,nwv->nrw/dot_general | solution.py:78
  498.8 12.0 %fusion.46 = f32[1,32,32,256]{3,2,1,0:T(8,128)} fusion(f32[32,32,256]{2,1,0:T(8,128)S(1)} %fusion.55, f32[1,32,256,256]{3,2,1,0:T(8,128)} %param.6, f32[32,32,256]{2,1,0:T(8,128)S(1)} %copy-done.10, f32[32,32,256]{2,1,0:T(8,128)S(1)} %copy-done.8, f32[32,32,256]{2,1,0:T(8,128)S(1)} %copy-done.6, pred[]{:T(512)S(6)} %eq.82, pred[]{:T(512)S(6)} %eq.81, ...), kind=kOutput, calls=%fused_computation.42 | convolution fusion | flops 806354944 | bytes 13631492 | tf_op jit(solution)/shard_map/nrw,nvw->nrv/dot_general | solution.py:80
  (83 shorter events, 57.3 us)
Async XLA Ops:
  3.8 26.5 %all-to-all-start = ((f32[32,2,1]{1,2,0:T(1,128)}), f32[32,2,1]{1,2,0:T(1,128)S(1)}, u32[]{:S(2)}, u32[]{:S(2)}) async-start(f32[32,2,1]{1,2,0:T(1,128)} %bitcast.5), calls=%async_computation | async-start | bytes 32768 | tf_op jit(solution)/shard_map/all_to_all | solution.py:48
  12.4 8.7 %copy-start = (f32[1,32,256,256]{3,2,1,0:T(8,128)S(1)}, f32[1,32,256,256]{3,2,1,0:T(8,128)}, u32[]{:S(2)}) copy-start(f32[1,32,256,256]{3,2,1,0:T(8,128)} %param.7) | copy-start | bytes 25165828
  30.2 35.8 %all-to-all-start.1 = ((f32[64,32,256]{2,1,0:T(8,128)}), f32[64,32,256]{2,1,0:T(8,128)}, u32[]{:S(2)}, u32[]{:S(2)}) async-start(f32[64,32,256]{2,1,0:T(8,128)} %copy.53), calls=%async_computation.1 | async-start | bytes 4194304 | tf_op jit(solution)/shard_map/all_to_all | solution.py:86
  37.7 57.3 %copy-start.2 = (f32[1,32,32,256]{3,2,1,0:T(8,128)S(1)}, f32[1,32,32,256]{3,2,1,0:T(8,128)}, u32[]{:S(2)}) copy-start(f32[1,32,32,256]{3,2,1,0:T(8,128)} %param.5) | copy-start | bytes 3145732
  66.1 37.4 %slice-start.4 = ((s8[8388608]{0:T(1024)(128)(4,1)}), s8[4194304]{0:T(1024)(128)(4,1)S(1)}, s32[]{:S(2)}) async-start(s8[8388608]{0:T(1024)(128)(4,1)} %bitcast.96), calls=%async_computation.11 | async-start | bytes 8388608
  69.8 25.2 %collective-permute-start = (f32[32,32,256]{2,0,1:T(8,128)S(1)}, f32[32,32,256]{2,0,1:T(8,128)S(1)}, u32[]{:S(2)}, u32[]{:S(2)}) collective-permute-start(f32[32,32,256]{2,0,1:T(8,128)S(1)} %fusion.38), channel_id=1, source_target_pairs={{0,32},{1,33},{2,34},{3,35},{4,36},{5,37},{6,38},{7,39},{8,40},{9,... | collective-permute-start | bytes 3145736 | tf_op jit(solution)/shard_map/ppermute | solution.py:13
  95.7 7.8 %slice-start.5 = ((s8[8388608]{0:T(1024)(128)(4,1)}), s8[4194304]{0:T(1024)(128)(4,1)S(1)}, s32[]{:S(2)}) async-start(s8[8388608]{0:T(1024)(128)(4,1)} %bitcast.96), calls=%async_computation.12 | async-start | bytes 8388608
  108.3 39.6 %slice-start = ((s8[8388608]{0:T(1024)(128)(4,1)}), s8[4194304]{0:T(1024)(128)(4,1)S(1)}, s32[]{:S(2)}) async-start(s8[8388608]{0:T(1024)(128)(4,1)} %bitcast.92), calls=%async_computation.7 | async-start | bytes 8388608
  111.3 36.7 %slice-start.1 = ((s8[8388608]{0:T(1024)(128)(4,1)}), s8[4194304]{0:T(1024)(128)(4,1)S(1)}, s32[]{:S(2)}) async-start(s8[8388608]{0:T(1024)(128)(4,1)} %bitcast.92), calls=%async_computation.8 | async-start | bytes 8388608
  146.4 0.9 collective-permute-start.1
  153.3 4.9 copy-start.3
  196.5 1.6 collective-permute-start.2
  198.1 10.6 %slice-start.2 = ((s8[8388608]{0:T(1024)(128)(4,1)}), s8[4194304]{0:T(1024)(128)(4,1)S(1)}, s32[]{:S(2)}) async-start(s8[8388608]{0:T(1024)(128)(4,1)} %bitcast.94), calls=%async_computation.9 | async-start | bytes 8388608
  200.2 8.6 %slice-start.3 = ((s8[8388608]{0:T(1024)(128)(4,1)}), s8[4194304]{0:T(1024)(128)(4,1)S(1)}, s32[]{:S(2)}) async-start(s8[8388608]{0:T(1024)(128)(4,1)} %bitcast.94), calls=%async_computation.10 | async-start | bytes 8388608
  208.7 279.6 %copy-start.1 = (f32[32,32,256]{2,1,0:T(8,128)}, f32[32,32,256]{2,1,0:T(8,128)S(1)}, u32[]{:S(2)}) copy-start(f32[32,32,256]{2,1,0:T(8,128)S(1)} %fusion.40) | copy-start | bytes 3145732
  208.7 45.8 %slice-start.6 = ((s8[8388608]{0:T(1024)(128)(4,1)}), s8[4194304]{0:T(1024)(128)(4,1)S(1)}, s32[]{:S(2)}) async-start(s8[8388608]{0:T(1024)(128)(4,1)} %bitcast.98), calls=%async_computation.13 | async-start | bytes 8388608
  216.6 38.0 %slice-start.7 = ((s8[8388608]{0:T(1024)(128)(4,1)}), s8[4194304]{0:T(1024)(128)(4,1)S(1)}, s32[]{:S(2)}) async-start(s8[8388608]{0:T(1024)(128)(4,1)} %bitcast.98), calls=%async_computation.14 | async-start | bytes 8388608
  216.6 1.0 collective-permute-start.3
  270.7 0.7 collective-permute-start.4
  324.4 124.8 %collective-permute-start.5 = (f32[32,32,256]{2,1,0:T(8,128)S(1)}, f32[32,32,256]{2,1,0:T(8,128)S(1)}, u32[]{:S(2)}, u32[]{:S(2)}) collective-permute-start(f32[32,32,256]{2,1,0:T(8,128)S(1)} %fusion.14), channel_id=1, source_target_pairs={{32,0},{33,1},{34,2},{35,3},{36,4},{37,5},{38,6},{39,7},{40,8},{41... | collective-permute-start | bytes 3145736 | tf_op jit(solution)/shard_map/ppermute | solution.py:13
  453.4 32.8 %all-to-all-start.6 = ((f32[64,32,256]{2,1,0:T(8,128)}), f32[64,32,256]{2,1,0:T(8,128)S(1)}, u32[]{:S(2)}, u32[]{:S(2)}) async-start(f32[64,32,256]{2,1,0:T(8,128)} %copy.73), calls=%async_computation.6 | async-start | bytes 4194304 | tf_op jit(solution)/shard_map/all_to_all | solution.py:95
  488.4 10.4 %copy-start.6 = (f32[32,32,256]{2,1,0:T(8,128)S(1)}, f32[32,32,256]{2,1,0:T(8,128)}, u32[]{:S(2)}) copy-start(f32[32,32,256]{2,1,0:T(8,128)} %copy-done.5) | copy-start | bytes 3145732
  488.4 10.4 %copy-start.8 = (f32[32,32,256]{2,1,0:T(8,128)S(1)}, f32[32,32,256]{2,1,0:T(8,128)}, u32[]{:S(2)}) copy-start(f32[32,32,256]{2,1,0:T(8,128)} %copy-done.7) | copy-start | bytes 3145732
  488.4 10.4 %copy-start.10 = (f32[32,32,256]{2,1,0:T(8,128)S(1)}, f32[32,32,256]{2,1,0:T(8,128)}, u32[]{:S(2)}) copy-start(f32[32,32,256]{2,1,0:T(8,128)} %copy-done.9) | copy-start | bytes 3145732
  (4 other events, 11.1 us)

commit v2 on v1

--- a/solution.py
+++ b/solution.py
@@ -3,7 +3,7 @@
 from jax import lax
 from jax.sharding import PartitionSpec as P
 
-CHUNKS = 1
+CHUNKS = 2
 MAIN_PRECISION = lax.Precision.HIGHEST
 
 

time: 520 us -> 491 us (0.944)
  blocking collectives: 129 us -> 63 us
  matrix products: 133 us -> 160 us
  starting transfers between devices: 29.6 us -> 48.9 us
  waiting for transfers between devices: 201 us -> 188 us
    all_to_all x4 -> x3, blocking collectives: 129 us -> 63 us  [body(): lax.all_to_all(buffer, 'panel', split_axis=0, concat_axis=0, tiled=True)]
    ppermute x6 -> x8, waiting for transfers between devices: 145 us -> 106 us  [shift_leaf(): return lax.ppermute(block, 'leaf', pairs)]
    all_to_all x2 -> x5, waiting for transfers between devices: 55.4 us -> 81.8 us  [body(): lax.all_to_all(buffer, 'panel', split_axis=0, concat_axis=0, tiled=True)]
    all_to_all x2 -> x5, starting transfers between devices: 11.8 us -> 25.5 us  [body(): lax.all_to_all(buffer, 'panel', split_axis=0, concat_axis=0, tiled=True)]
    dot_general x3 -> x4, matrix products: 26.4 us -> 37.8 us  [body(): lowered = jnp.einsum('nrv,nwv->nrw', picked, couple_block, precision=main)]
    dot_general x4 -> x5, matrix products: 35.9 us -> 46.4 us  [body(): jnp.einsum('nrw,nvw->nrv', source, diag_inverse, precision=main)]
    dot_general x3 -> x4, matrix products: 14.6 us -> 23.4 us  [body(): jnp.einsum('nrw,nwv->nrv', forward_part, couple_block, precision=main)]
    ppermute x6 -> x8, starting transfers between devices: 9.2 us -> 14.9 us  [shift_leaf(): return lax.ppermute(block, 'leaf', pairs)]
  transfers between devices with their start and end apart: 9 -> 14, of which waited for: 4 -> 9; matrix products, arithmetic and copies ran while one was open for 4% -> 4% of each run, Pallas kernels for 0% -> 0%
where the time goes in v2:
time: 491 us; the launch traced here: 482 us
  waiting for transfers between devices  188 us (38%)
  matrix products  160 us (33%)
  blocking collectives  63 us (13%)
  starting transfers between devices  48.9 us (10%)
  local copies, waits for them, and re-layouts  12.4 us (3%)
  other arithmetic  8.45 us (2%)
    ppermute x8, waiting for transfers between devices, shift_leaf(): return lax.ppermute(block, 'leaf', pairs)  106 us
    all_to_all x5, waiting for transfers between devices, body(): lax.all_to_all(buffer, 'panel', split_axis=0, concat_axis=0, tiled=True)  81.8 us
    all_to_all x3, blocking collectives, body(): lax.all_to_all(buffer, 'panel', split_axis=0, concat_axis=0, tiled=True)  63 us
    dot_general x5, matrix products, body(): jnp.einsum('nrw,nvw->nrv', source, diag_inverse, precision=main)  46.4 us
    dot_general x4, matrix products, body(): lowered = jnp.einsum('nrv,nwv->nrw', picked, couple_block, precision=main)  37.8 us
    dot_general x5, matrix products, body(): jnp.einsum('nrw,nwv->nrv', rhs - incoming, diag_inverse, precision=main)  33.3 us
    all_to_all x5, starting transfers between devices, body(): lax.all_to_all(buffer, 'panel', split_axis=0, concat_axis=0, tiled=True)  25.5 us
    dot_general x4, matrix products, body(): jnp.einsum('nrw,nwv->nrv', forward_part, couple_block, precision=main)  23.4 us
  transfers between devices with their start and end apart: 14, of which 9 were waited for; matrix products, arithmetic and copies ran while one was open for 4% of the time, Pallas kernels for 0%

profile of v2, /device:TPU:1, one launch (start us, length us, event | category | flops | bytes accessed | tf_op | source)
XLA Modules:
  0.0 482.4 jit_solution(11132842327641891050)
XLA Ops:
  3.8 8.6 %all-to-all-start = ((f32[32,2,1]{1,2,0:T(1,128)}), f32[32,2,1]{1,2,0:T(1,128)S(1)}, u32[]{:S(2)}, u32[]{:S(2)}) async-start(f32[32,2,1]{1,2,0:T(1,128)} %bitcast.5), calls=%async_computation | async-start | bytes 32768 | tf_op jit(solution)/shard_map/all_to_all | solution.py:48
  14.3 6.9 %fusion.34 = f32[32,16,256]{2,1,0:T(8,128)S(1)} fusion(f32[1,32,256,256]{3,2,1,0:T(8,128)} %param.6, f32[32,16,256]{2,0,1:T(8,128)S(1)} %select_bitcast_fusion), kind=kOutput, calls=%fused_computation.34 | convolution fusion | flops 402653184 | bytes 9437184 | tf_op jit(solution)/shard_map/nrw,nwv->nrv/dot_general | solution.py:71
  27.8 7.4 %all-to-all-start.1 = ((f32[64,16,256]{2,1,0:T(8,128)}), f32[64,16,256]{2,1,0:T(8,128)S(1)}, u32[]{:S(2)}, u32[]{:S(2)}) async-start(f32[64,16,256]{2,1,0:T(8,128)} %copy.68), calls=%async_computation.1 | async-start | bytes 2097152 | tf_op jit(solution)/shard_map/all_to_all | solution.py:86
  36.5 15.6 %all-to-all-done.1 = f32[64,16,256]{2,1,0:T(8,128)S(1)} async-done(((f32[64,16,256]{2,1,0:T(8,128)}), f32[64,16,256]{2,1,0:T(8,128)S(1)}, u32[]{:S(2)}, u32[]{:S(2)}) %all-to-all-start.1) | async-done | bytes 1048608 | tf_op jit(solution)/shard_map/all_to_all | solution.py:86
  56.9 10.9 %collective-permute-done = f32[32,16,256]{2,0,1:T(8,128)S(1)} collective-permute-done((f32[32,16,256]{2,0,1:T(8,128)S(1)}, f32[32,16,256]{2,0,1:T(8,128)S(1)}, u32[]{:S(2)}, u32[]{:S(2)}) %collective-permute-start) | collective-permute-done | bytes 524320 | tf_op jit(solution)/shard_map/ppermute | solution.py:13
  83.1 21.2 %all_to_all.49 = f32[64,16,256]{2,1,0:T(8,128)S(1)} all-to-all(f32[64,16,256]{2,1,0:T(8,128)S(1)} %copy.72), channel_id=1, replica_groups=mesh['leaf'=4,'panel'=32] {'panel'}, dimensions={0} | all-to-all | bytes 2097152 | tf_op jit(solution)/shard_map/all_to_all | solution.py:86
  109.7 10.9 %collective-permute-done.1 = f32[32,16,256]{2,0,1:T(8,128)S(1)} collective-permute-done((f32[32,16,256]{2,0,1:T(8,128)S(1)}, f32[32,16,256]{2,0,1:T(8,128)S(1)}, u32[]{:S(2)}, u32[]{:S(2)}) %collective-permute-start.1) | collective-permute-done | bytes 524320 | tf_op jit(solution)/shard_map/ppermute | solution.py:13
  135.8 21.2 %all_to_all.50 = f32[64,16,256]{2,1,0:T(8,128)S(1)} all-to-all(f32[64,16,256]{2,1,0:T(8,128)S(1)} %copy.76), channel_id=1, replica_groups=mesh['leaf'=4,'panel'=32] {'panel'}, dimensions={0} | all-to-all | bytes 2097152 | tf_op jit(solution)/shard_map/all_to_all | solution.py:86
  175.1 20.6 %all_to_all.51 = f32[64,16,256]{2,1,0:T(8,128)S(1)} all-to-all(f32[64,16,256]{2,1,0:T(8,128)S(1)} %copy.80), channel_id=1, replica_groups=mesh['leaf'=4,'panel'=32] {'panel'}, dimensions={0} | all-to-all | bytes 2097152 | tf_op jit(solution)/shard_map/all_to_all | solution.py:86
  207.9 9.3 %fusion.24 = f32[32,16,256]{2,1,0:T(8,128)S(1)} fusion(f32[1,32,256,256]{3,2,1,0:T(8,128)} %param.6, f32[32,16,256]{2,1,0:T(8,128)S(1)} %get-tuple-element.9, f32[32,16,256]{2,1,0:T(8,128)S(1)} %get-tuple-element.3, pred[]{:T(512)S(6)} %eq.161), kind=kOutput, calls=%fused_computation.24 | convolution fusion | flops 402784256 | bytes 9961473 | tf_op jit(solution)/shard_map/nrw,nvw->nrv/dot_general | solution.py:80
  224.6 16.8 %all-to-all-done.5 = f32[64,16,256]{2,1,0:T(8,128)S(1)} async-done(((f32[64,16,256]{2,1,0:T(8,128)}), f32[64,16,256]{2,1,0:T(8,128)S(1)}, u32[]{:S(2)}, u32[]{:S(2)}) %all-to-all-start.5) | async-done | bytes 1048608 | tf_op jit(solution)/shard_map/all_to_all | solution.py:95
  242.5 9.4 %fusion.6 = f32[32,16,256]{2,1,0:T(8,128)S(1)} fusion(f32[1,32,256,256]{3,2,1,0:T(8,128)} %param.7, f32[32,16,256]{2,0,1:T(8,128)S(1)} %fusion.43), kind=kOutput, calls=%fused_computation.6 | convolution fusion | flops 402653184 | bytes 9437184 | tf_op jit(solution)/shard_map/nrv,nwv->nrw/dot_general | solution.py:78
  252.0 9.3 %fusion.22 = f32[32,16,256]{2,1,0:T(8,128)S(1)} fusion(f32[1,32,256,256]{3,2,1,0:T(8,128)} %param.6, f32[32,16,256]{2,1,0:T(8,128)S(1)} %fusion.6, f32[32,16,256]{2,1,0:T(8,128)S(1)} %get-tuple-element.8, f32[32,16,256]{2,1,0:T(8,128)S(1)} %get-tuple-element.2, pred[]{:T(512)S(6)} %eq.160), kind=kOutput, calls=%fused_computation.22 | convolution fusion | flops 402915328 | bytes 10485761 | tf_op jit(solution)/shard_map/nrw,nvw->nrv/dot_general | solution.py:80
  268.7 16.8 %all-to-all-done.6 = f32[64,16,256]{2,1,0:T(8,128)S(1)} async-done(((f32[64,16,256]{2,1,0:T(8,128)}), f32[64,16,256]{2,1,0:T(8,128)S(1)}, u32[]{:S(2)}, u32[]{:S(2)}) %all-to-all-start.6) | async-done | bytes 1048608 | tf_op jit(solution)/shard_map/all_to_all | solution.py:95
  286.7 9.4 %fusion.4 = f32[32,16,256]{2,1,0:T(8,128)S(1)} fusion(f32[1,32,256,256]{3,2,1,0:T(8,128)} %param.7, f32[32,16,256]{2,0,1:T(8,128)S(1)} %fusion.41), kind=kOutput, calls=%fused_computation.4 | convolution fusion | flops 402653184 | bytes 9437184 | tf_op jit(solution)/shard_map/nrv,nwv->nrw/dot_general | solution.py:78
  296.1 9.3 %fusion.20 = f32[32,16,256]{2,1,0:T(8,128)S(1)} fusion(f32[1,32,256,256]{3,2,1,0:T(8,128)} %param.6, f32[32,16,256]{2,1,0:T(8,128)S(1)} %fusion.4, f32[32,16,256]{2,1,0:T(8,128)S(1)} %get-tuple-element.8, f32[32,16,256]{2,1,0:T(8,128)S(1)} %get-tuple-element.2, pred[]{:T(512)S(6)} %eq.159), kind=kOutput, calls=%fused_computation.20 | convolution fusion | flops 402915328 | bytes 10485761 | tf_op jit(solution)/shard_map/nrw,nvw->nrv/dot_general | solution.py:80
  306.7 70.6 %collective-permute-done.6 = f32[32,16,256]{2,1,0:T(8,128)S(1)} collective-permute-done((f32[32,16,256]{2,1,0:T(8,128)S(1)}, f32[32,16,256]{2,1,0:T(8,128)S(1)}, u32[]{:S(2)}, u32[]{:S(2)}) %collective-permute-start.6) | collective-permute-done | bytes 524320 | tf_op jit(solution)/shard_map/ppermute | solution.py:13
  384.5 16.9 %all-to-all-done.7 = f32[64,16,256]{2,1,0:T(8,128)S(1)} async-done(((f32[64,16,256]{2,1,0:T(8,128)}), f32[64,16,256]{2,1,0:T(8,128)S(1)}, u32[]{:S(2)}, u32[]{:S(2)}) %all-to-all-start.7) | async-done | bytes 1048608 | tf_op jit(solution)/shard_map/all_to_all | solution.py:95
  402.5 9.4 %fusion.2 = f32[32,16,256]{2,1,0:T(8,128)S(1)} fusion(f32[1,32,256,256]{3,2,1,0:T(8,128)} %param.7, f32[32,16,256]{2,0,1:T(8,128)S(1)} %fusion.39), kind=kOutput, calls=%fused_computation.2 | convolution fusion | flops 402653184 | bytes 9437184 | tf_op jit(solution)/shard_map/nrv,nwv->nrw/dot_general | solution.py:78
  412.0 9.3 %fusion.18 = f32[32,16,256]{2,1,0:T(8,128)S(1)} fusion(f32[1,32,256,256]{3,2,1,0:T(8,128)} %param.6, f32[32,16,256]{2,1,0:T(8,128)S(1)} %fusion.2, f32[32,16,256]{2,1,0:T(8,128)S(1)} %get-tuple-element.8, f32[32,16,256]{2,1,0:T(8,128)S(1)} %get-tuple-element.2, pred[]{:T(512)S(6)} %eq.158), kind=kOutput, calls=%fused_computation.18 | convolution fusion | flops 402915328 | bytes 10485761 | tf_op jit(solution)/shard_map/nrw,nvw->nrv/dot_general | solution.py:80
  422.6 14.0 %collective-permute-done.7 = f32[32,16,256]{2,1,0:T(8,128)S(1)} collective-permute-done((f32[32,16,256]{2,1,0:T(8,128)S(1)}, f32[32,16,256]{2,1,0:T(8,128)S(1)}, u32[]{:S(2)}, u32[]{:S(2)}) %collective-permute-start.7) | collective-permute-done | bytes 524320 | tf_op jit(solution)/shard_map/ppermute | solution.py:13
  445.2 15.8 %all-to-all-done.8 = f32[64,16,256]{2,1,0:T(8,128)S(1)} async-done(((f32[64,16,256]{2,1,0:T(8,128)}), f32[64,16,256]{2,1,0:T(8,128)S(1)}, u32[]{:S(2)}, u32[]{:S(2)}) %all-to-all-start.8) | async-done | bytes 1048608 | tf_op jit(solution)/shard_map/all_to_all | solution.py:95
  462.1 9.4 %fusion = f32[32,16,256]{2,1,0:T(8,128)S(1)} fusion(f32[1,32,256,256]{3,2,1,0:T(8,128)} %param.7, f32[32,16,256]{2,0,1:T(8,128)S(1)} %fusion.37), kind=kOutput, calls=%fused_computation | convolution fusion | flops 402653184 | bytes 9437184 | tf_op jit(solution)/shard_map/nrv,nwv->nrw/dot_general | solution.py:78
  471.5 9.3 %select_select_fusion.1 = (f32[32,16,256]{2,1,0:T(8,128)S(1)}, f32[32,16,256]{2,1,0:T(8,128)S(1)}) fusion(f32[32,16,256]{2,1,0:T(8,128)S(1)} %copy-done.4, f32[32,16,256]{2,1,0:T(8,128)S(1)} %copy-done.2, f32[32,16,256]{2,1,0:T(8,128)S(1)} %fusion.22, f32[32,16,256]{2,1,0:T(8,128)S(1)} %fusion.24, pred[]{:T(512)S(6)} %eq.165, pred[]{:T(512)S(6)} %eq.164, ...), kind=kOutput, calls=%fused_computation.86 | convolution fusion | flops 404226048 | bytes 13107211 | tf_op jit(solution)/shard_map/nrw,nvw->nrv/dot_general | solution.py:80
  (75 shorter events, 122.5 us)
Async XLA Ops:
  3.8 24.0 %all-to-all-start = ((f32[32,2,1]{1,2,0:T(1,128)}), f32[32,2,1]{1,2,0:T(1,128)S(1)}, u32[]{:S(2)}, u32[]{:S(2)}) async-start(f32[32,2,1]{1,2,0:T(1,128)} %bitcast.5), calls=%async_computation | async-start | bytes 32768 | tf_op jit(solution)/shard_map/all_to_all | solution.py:48
  13.7 7.5 %copy-start = (f32[1,32,256,256]{3,2,1,0:T(8,128)S(1)}, f32[1,32,256,256]{3,2,1,0:T(8,128)}, u32[]{:S(2)}) copy-start(f32[1,32,256,256]{3,2,1,0:T(8,128)} %param.7) | copy-start | bytes 25165828
  27.8 24.3 %all-to-all-start.1 = ((f32[64,16,256]{2,1,0:T(8,128)}), f32[64,16,256]{2,1,0:T(8,128)S(1)}, u32[]{:S(2)}, u32[]{:S(2)}) async-start(f32[64,16,256]{2,1,0:T(8,128)} %copy.68), calls=%async_computation.1 | async-start | bytes 2097152 | tf_op jit(solution)/shard_map/all_to_all | solution.py:86
  53.2 14.7 %collective-permute-start = (f32[32,16,256]{2,0,1:T(8,128)S(1)}, f32[32,16,256]{2,0,1:T(8,128)S(1)}, u32[]{:S(2)}, u32[]{:S(2)}) collective-permute-start(f32[32,16,256]{2,0,1:T(8,128)S(1)} %fusion.51), channel_id=1, source_target_pairs={{0,32},{1,33},{2,34},{3,35},{4,36},{5,37},{6,38},{7,39},{8,40},{9,... | collective-permute-start | bytes 1572872 | tf_op jit(solution)/shard_map/ppermute | solution.py:13
  105.4 15.3 %collective-permute-start.1 = (f32[32,16,256]{2,0,1:T(8,128)S(1)}, f32[32,16,256]{2,0,1:T(8,128)S(1)}, u32[]{:S(2)}, u32[]{:S(2)}) collective-permute-start(f32[32,16,256]{2,0,1:T(8,128)S(1)} %fusion.49), channel_id=1, source_target_pairs={{0,32},{32,64},{1,33},{33,65},{2,34},{34,66},{3,35},{35,67},{4,36}... | collective-permute-start | bytes 1572872 | tf_op jit(solution)/shard_map/ppermute | solution.py:13
  158.9 1.0 collective-permute-start.2
  197.6 2.0 collective-permute-start.3
  217.2 0.7 collective-permute-start.4
  220.4 21.0 %all-to-all-start.5 = ((f32[64,16,256]{2,1,0:T(8,128)}), f32[64,16,256]{2,1,0:T(8,128)S(1)}, u32[]{:S(2)}, u32[]{:S(2)}) async-start(f32[64,16,256]{2,1,0:T(8,128)} %copy.84), calls=%async_computation.5 | async-start | bytes 2097152 | tf_op jit(solution)/shard_map/all_to_all | solution.py:95
  261.3 0.7 collective-permute-start.5
  264.5 21.0 %all-to-all-start.6 = ((f32[64,16,256]{2,1,0:T(8,128)}), f32[64,16,256]{2,1,0:T(8,128)S(1)}, u32[]{:S(2)}, u32[]{:S(2)}) async-start(f32[64,16,256]{2,1,0:T(8,128)} %copy.88), calls=%async_computation.6 | async-start | bytes 2097152 | tf_op jit(solution)/shard_map/all_to_all | solution.py:95
  305.4 74.5 %copy-start.1 = (f32[32,16,256]{2,1,0:T(8,128)}, f32[32,16,256]{2,1,0:T(8,128)S(1)}, u32[]{:S(2)}) copy-start(f32[32,16,256]{2,1,0:T(8,128)S(1)} %fusion.20) | copy-start | bytes 1572868
  305.4 71.9 %collective-permute-start.6 = (f32[32,16,256]{2,1,0:T(8,128)S(1)}, f32[32,16,256]{2,1,0:T(8,128)S(1)}, u32[]{:S(2)}, u32[]{:S(2)}) collective-permute-start(f32[32,16,256]{2,1,0:T(8,128)S(1)} %fusion.20), channel_id=1, source_target_pairs={{32,0},{64,32},{33,1},{65,33},{34,2},{66,34},{35,3},{67,35},{36,4}... | collective-permute-start | bytes 1572872 | tf_op jit(solution)/shard_map/ppermute | solution.py:13
  379.9 21.6 %all-to-all-start.7 = ((f32[64,16,256]{2,1,0:T(8,128)}), f32[64,16,256]{2,1,0:T(8,128)S(1)}, u32[]{:S(2)}, u32[]{:S(2)}) async-start(f32[64,16,256]{2,1,0:T(8,128)} %copy.92), calls=%async_computation.7 | async-start | bytes 2097152 | tf_op jit(solution)/shard_map/all_to_all | solution.py:95
  421.3 17.8 %copy-start.3 = (f32[32,16,256]{2,1,0:T(8,128)}, f32[32,16,256]{2,1,0:T(8,128)S(1)}, u32[]{:S(2)}) copy-start(f32[32,16,256]{2,1,0:T(8,128)S(1)} %fusion.18) | copy-start | bytes 1572868
  421.3 15.3 %collective-permute-start.7 = (f32[32,16,256]{2,1,0:T(8,128)S(1)}, f32[32,16,256]{2,1,0:T(8,128)S(1)}, u32[]{:S(2)}, u32[]{:S(2)}) collective-permute-start(f32[32,16,256]{2,1,0:T(8,128)S(1)} %fusion.18), channel_id=1, source_target_pairs={{32,0},{33,1},{34,2},{35,3},{36,4},{37,5},{38,6},{39,7},{40,8},{41... | collective-permute-start | bytes 1572872 | tf_op jit(solution)/shard_map/ppermute | solution.py:13
  439.1 21.9 %all-to-all-start.8 = ((f32[64,16,256]{2,1,0:T(8,128)}), f32[64,16,256]{2,1,0:T(8,128)S(1)}, u32[]{:S(2)}, u32[]{:S(2)}) async-start(f32[64,16,256]{2,1,0:T(8,128)} %copy.96), calls=%async_computation.8 | async-start | bytes 2097152 | tf_op jit(solution)/shard_map/all_to_all | solution.py:95
  460.9 10.6 %copy-start.2 = (f32[32,16,256]{2,1,0:T(8,128)S(1)}, f32[32,16,256]{2,1,0:T(8,128)}, u32[]{:S(2)}) copy-start(f32[32,16,256]{2,1,0:T(8,128)} %copy-done.1) | copy-start | bytes 1572868
  460.9 10.6 %copy-start.4 = (f32[32,16,256]{2,1,0:T(8,128)S(1)}, f32[32,16,256]{2,1,0:T(8,128)}, u32[]{:S(2)}) copy-start(f32[32,16,256]{2,1,0:T(8,128)} %copy-done.3) | copy-start | bytes 1572868

commit v3 on v2

--- a/solution.py
+++ b/solution.py
@@ -4,7 +4,7 @@
 from jax.sharding import PartitionSpec as P
 
 CHUNKS = 2
-MAIN_PRECISION = lax.Precision.HIGHEST
+MAIN_PRECISION = lax.Precision.HIGH
 
 
 def shift_leaf(block, pairs):

time: 491 us -> 459 us (0.935)
  matrix products: 160 us -> 128 us
    dot_general x5, matrix products: 46.4 us -> 33.8 us  [body(): jnp.einsum('nrw,nvw->nrv', source, diag_inverse, precision=main)]
    dot_general x4, matrix products: 37.8 us -> 27.1 us  [body(): lowered = jnp.einsum('nrv,nwv->nrw', picked, couple_block, precision=main)]
  transfers between devices with their start and end apart: 14 -> 14, of which waited for: 9 -> 9; matrix products, arithmetic and copies ran while one was open for 4% -> 3% of each run, Pallas kernels for 0% -> 0%
where the time goes in v3:
time: 459 us; the launch traced here: 451 us
  waiting for transfers between devices  188 us (41%)
  matrix products  128 us (28%)
  blocking collectives  62.9 us (14%)
  starting transfers between devices  49.2 us (11%)
  local copies, waits for them, and re-layouts  12.4 us (3%)
  other arithmetic  8.45 us (2%)
    ppermute x8, waiting for transfers between devices, shift_leaf(): return lax.ppermute(block, 'leaf', pairs)  106 us
    all_to_all x5, waiting for transfers between devices, body(): lax.all_to_all(buffer, 'panel', split_axis=0, concat_axis=0, tiled=True)  81.8 us
    all_to_all x3, blocking collectives, body(): lax.all_to_all(buffer, 'panel', split_axis=0, concat_axis=0, tiled=True)  62.9 us
    dot_general x5, matrix products, body(): jnp.einsum('nrw,nvw->nrv', source, diag_inverse, precision=main)  33.8 us
    dot_general x5, matrix products, body(): jnp.einsum('nrw,nwv->nrv', rhs - incoming, diag_inverse, precision=main)  29.2 us
    dot_general x4, matrix products, body(): lowered = jnp.einsum('nrv,nwv->nrw', picked, couple_block, precision=main)  27.1 us
    all_to_all x5, starting transfers between devices, body(): lax.all_to_all(buffer, 'panel', split_axis=0, concat_axis=0, tiled=True)  25.6 us
    dot_general x4, matrix products, body(): jnp.einsum('nrw,nwv->nrv', forward_part, couple_block, precision=main)  19.1 us
  transfers between devices with their start and end apart: 14, of which 9 were waited for; matrix products, arithmetic and copies ran while one was open for 3% of the time, Pallas kernels for 0%

profile of v3, /device:TPU:1, one launch (start us, length us, event | category | flops | bytes accessed | tf_op | source)
XLA Modules:
  0.0 450.6 jit_solution(14772341179408255910)
XLA Ops:
  3.8 8.6 %all-to-all-start = ((f32[32,2,1]{1,2,0:T(1,128)}), f32[32,2,1]{1,2,0:T(1,128)S(1)}, u32[]{:S(2)}, u32[]{:S(2)}) async-start(f32[32,2,1]{1,2,0:T(1,128)} %bitcast.5), calls=%async_computation | async-start | bytes 32768 | tf_op jit(solution)/shard_map/all_to_all | solution.py:48
  14.3 6.0 %fusion.34 = f32[32,16,256]{2,1,0:T(8,128)S(1)} fusion(f32[1,32,256,256]{3,2,1,0:T(8,128)} %param.6, f32[32,16,256]{2,0,1:T(8,128)S(1)} %select_bitcast_fusion), kind=kOutput, calls=%fused_computation.34 | convolution fusion | flops 201326592 | bytes 9437184 | tf_op jit(solution)/shard_map/nrw,nwv->nrv/dot_general | solution.py:71
  25.1 7.4 %all-to-all-start.1 = ((f32[64,16,256]{2,1,0:T(8,128)}), f32[64,16,256]{2,1,0:T(8,128)S(1)}, u32[]{:S(2)}, u32[]{:S(2)}) async-start(f32[64,16,256]{2,1,0:T(8,128)} %copy.68), calls=%async_computation.1 | async-start | bytes 2097152 | tf_op jit(solution)/shard_map/all_to_all | solution.py:86
  33.8 15.6 %all-to-all-done.1 = f32[64,16,256]{2,1,0:T(8,128)S(1)} async-done(((f32[64,16,256]{2,1,0:T(8,128)}), f32[64,16,256]{2,1,0:T(8,128)S(1)}, u32[]{:S(2)}, u32[]{:S(2)}) %all-to-all-start.1) | async-done | bytes 1048608 | tf_op jit(solution)/shard_map/all_to_all | solution.py:86
  54.6 10.6 %collective-permute-done = f32[32,16,256]{2,0,1:T(8,128)S(1)} collective-permute-done((f32[32,16,256]{2,0,1:T(8,128)S(1)}, f32[32,16,256]{2,0,1:T(8,128)S(1)}, u32[]{:S(2)}, u32[]{:S(2)}) %collective-permute-start) | collective-permute-done | bytes 524320 | tf_op jit(solution)/shard_map/ppermute | solution.py:13
  78.7 21.2 %all_to_all.49 = f32[64,16,256]{2,1,0:T(8,128)S(1)} all-to-all(f32[64,16,256]{2,1,0:T(8,128)S(1)} %copy.72), channel_id=1, replica_groups=mesh['leaf'=4,'panel'=32] {'panel'}, dimensions={0} | all-to-all | bytes 2097152 | tf_op jit(solution)/shard_map/all_to_all | solution.py:86
  105.4 10.9 %collective-permute-done.1 = f32[32,16,256]{2,0,1:T(8,128)S(1)} collective-permute-done((f32[32,16,256]{2,0,1:T(8,128)S(1)}, f32[32,16,256]{2,0,1:T(8,128)S(1)}, u32[]{:S(2)}, u32[]{:S(2)}) %collective-permute-start.1) | collective-permute-done | bytes 524320 | tf_op jit(solution)/shard_map/ppermute | solution.py:13
  129.9 21.2 %all_to_all.50 = f32[64,16,256]{2,1,0:T(8,128)S(1)} all-to-all(f32[64,16,256]{2,1,0:T(8,128)S(1)} %copy.76), channel_id=1, replica_groups=mesh['leaf'=4,'panel'=32] {'panel'}, dimensions={0} | all-to-all | bytes 2097152 | tf_op jit(solution)/shard_map/all_to_all | solution.py:86
  167.4 20.6 %all_to_all.51 = f32[64,16,256]{2,1,0:T(8,128)S(1)} all-to-all(f32[64,16,256]{2,1,0:T(8,128)S(1)} %copy.80), channel_id=1, replica_groups=mesh['leaf'=4,'panel'=32] {'panel'}, dimensions={0} | all-to-all | bytes 2097152 | tf_op jit(solution)/shard_map/all_to_all | solution.py:86
  199.2 6.8 %fusion.24 = f32[32,16,256]{2,1,0:T(8,128)S(1)} fusion(f32[1,32,256,256]{3,2,1,0:T(8,128)} %param.6, f32[32,16,256]{2,1,0:T(8,128)S(1)} %get-tuple-element.9, f32[32,16,256]{2,1,0:T(8,128)S(1)} %get-tuple-element.3, pred[]{:T(512)S(6)} %eq.161), kind=kOutput, calls=%fused_computation.24 | convolution fusion | flops 201457664 | bytes 9961473 | tf_op jit(solution)/shard_map/nrw,nvw->nrv/dot_general | solution.py:80
  213.7 16.8 %all-to-all-done.5 = f32[64,16,256]{2,1,0:T(8,128)S(1)} async-done(((f32[64,16,256]{2,1,0:T(8,128)}), f32[64,16,256]{2,1,0:T(8,128)S(1)}, u32[]{:S(2)}, u32[]{:S(2)}) %all-to-all-start.5) | async-done | bytes 1048608 | tf_op jit(solution)/shard_map/all_to_all | solution.py:95
  231.6 6.8 %fusion.6 = f32[32,16,256]{2,1,0:T(8,128)S(1)} fusion(f32[1,32,256,256]{3,2,1,0:T(8,128)} %param.7, f32[32,16,256]{2,0,1:T(8,128)S(1)} %fusion.43), kind=kOutput, calls=%fused_computation.6 | convolution fusion | flops 201326592 | bytes 9437184 | tf_op jit(solution)/shard_map/nrv,nwv->nrw/dot_general | solution.py:78
  238.4 6.7 %fusion.22 = f32[32,16,256]{2,1,0:T(8,128)S(1)} fusion(f32[1,32,256,256]{3,2,1,0:T(8,128)} %param.6, f32[32,16,256]{2,1,0:T(8,128)S(1)} %fusion.6, f32[32,16,256]{2,1,0:T(8,128)S(1)} %get-tuple-element.8, f32[32,16,256]{2,1,0:T(8,128)S(1)} %get-tuple-element.2, pred[]{:T(512)S(6)} %eq.160), kind=kOutput, calls=%fused_computation.22 | convolution fusion | flops 201588736 | bytes 10485761 | tf_op jit(solution)/shard_map/nrw,nvw->nrv/dot_general | solution.py:80
  252.6 16.8 %all-to-all-done.6 = f32[64,16,256]{2,1,0:T(8,128)S(1)} async-done(((f32[64,16,256]{2,1,0:T(8,128)}), f32[64,16,256]{2,1,0:T(8,128)S(1)}, u32[]{:S(2)}, u32[]{:S(2)}) %all-to-all-start.6) | async-done | bytes 1048608 | tf_op jit(solution)/shard_map/all_to_all | solution.py:95
  270.5 6.8 %fusion.4 = f32[32,16,256]{2,1,0:T(8,128)S(1)} fusion(f32[1,32,256,256]{3,2,1,0:T(8,128)} %param.7, f32[32,16,256]{2,0,1:T(8,128)S(1)} %fusion.41), kind=kOutput, calls=%fused_computation.4 | convolution fusion | flops 201326592 | bytes 9437184 | tf_op jit(solution)/shard_map/nrv,nwv->nrw/dot_general | solution.py:78
  277.3 6.7 %fusion.20 = f32[32,16,256]{2,1,0:T(8,128)S(1)} fusion(f32[1,32,256,256]{3,2,1,0:T(8,128)} %param.6, f32[32,16,256]{2,1,0:T(8,128)S(1)} %fusion.4, f32[32,16,256]{2,1,0:T(8,128)S(1)} %get-tuple-element.8, f32[32,16,256]{2,1,0:T(8,128)S(1)} %get-tuple-element.2, pred[]{:T(512)S(6)} %eq.159), kind=kOutput, calls=%fused_computation.20 | convolution fusion | flops 201588736 | bytes 10485761 | tf_op jit(solution)/shard_map/nrw,nvw->nrv/dot_general | solution.py:80
  285.4 70.9 %collective-permute-done.6 = f32[32,16,256]{2,1,0:T(8,128)S(1)} collective-permute-done((f32[32,16,256]{2,1,0:T(8,128)S(1)}, f32[32,16,256]{2,1,0:T(8,128)S(1)}, u32[]{:S(2)}, u32[]{:S(2)}) %collective-permute-start.6) | collective-permute-done | bytes 524320 | tf_op jit(solution)/shard_map/ppermute | solution.py:13
  363.4 16.9 %all-to-all-done.7 = f32[64,16,256]{2,1,0:T(8,128)S(1)} async-done(((f32[64,16,256]{2,1,0:T(8,128)}), f32[64,16,256]{2,1,0:T(8,128)S(1)}, u32[]{:S(2)}, u32[]{:S(2)}) %all-to-all-start.7) | async-done | bytes 1048608 | tf_op jit(solution)/shard_map/all_to_all | solution.py:95
  381.5 6.8 %fusion.2 = f32[32,16,256]{2,1,0:T(8,128)S(1)} fusion(f32[1,32,256,256]{3,2,1,0:T(8,128)} %param.7, f32[32,16,256]{2,0,1:T(8,128)S(1)} %fusion.39), kind=kOutput, calls=%fused_computation.2 | convolution fusion | flops 201326592 | bytes 9437184 | tf_op jit(solution)/shard_map/nrv,nwv->nrw/dot_general | solution.py:78
  388.2 6.7 %fusion.18 = f32[32,16,256]{2,1,0:T(8,128)S(1)} fusion(f32[1,32,256,256]{3,2,1,0:T(8,128)} %param.6, f32[32,16,256]{2,1,0:T(8,128)S(1)} %fusion.2, f32[32,16,256]{2,1,0:T(8,128)S(1)} %get-tuple-element.8, f32[32,16,256]{2,1,0:T(8,128)S(1)} %get-tuple-element.2, pred[]{:T(512)S(6)} %eq.158), kind=kOutput, calls=%fused_computation.18 | convolution fusion | flops 201588736 | bytes 10485761 | tf_op jit(solution)/shard_map/nrw,nvw->nrv/dot_general | solution.py:80
  396.3 13.9 %collective-permute-done.7 = f32[32,16,256]{2,1,0:T(8,128)S(1)} collective-permute-done((f32[32,16,256]{2,1,0:T(8,128)S(1)}, f32[32,16,256]{2,1,0:T(8,128)S(1)}, u32[]{:S(2)}, u32[]{:S(2)}) %collective-permute-start.7) | collective-permute-done | bytes 524320 | tf_op jit(solution)/shard_map/ppermute | solution.py:13
  418.8 15.8 %all-to-all-done.8 = f32[64,16,256]{2,1,0:T(8,128)S(1)} async-done(((f32[64,16,256]{2,1,0:T(8,128)}), f32[64,16,256]{2,1,0:T(8,128)S(1)}, u32[]{:S(2)}, u32[]{:S(2)}) %all-to-all-start.8) | async-done | bytes 1048608 | tf_op jit(solution)/shard_map/all_to_all | solution.py:95
  435.7 6.8 %fusion = f32[32,16,256]{2,1,0:T(8,128)S(1)} fusion(f32[1,32,256,256]{3,2,1,0:T(8,128)} %param.7, f32[32,16,256]{2,0,1:T(8,128)S(1)} %fusion.37), kind=kOutput, calls=%fused_computation | convolution fusion | flops 201326592 | bytes 9437184 | tf_op jit(solution)/shard_map/nrv,nwv->nrw/dot_general | solution.py:78
  442.5 6.8 %select_select_fusion.1 = (f32[32,16,256]{2,1,0:T(8,128)S(1)}, f32[32,16,256]{2,1,0:T(8,128)S(1)}) fusion(f32[32,16,256]{2,1,0:T(8,128)S(1)} %copy-done.4, f32[32,16,256]{2,1,0:T(8,128)S(1)} %copy-done.2, f32[32,16,256]{2,1,0:T(8,128)S(1)} %fusion.22, f32[32,16,256]{2,1,0:T(8,128)S(1)} %fusion.24, pred[]{:T(512)S(6)} %eq.165, pred[]{:T(512)S(6)} %eq.164, ...), kind=kOutput, calls=%fused_computation.86 | convolution fusion | flops 202899456 | bytes 13107211 | tf_op jit(solution)/shard_map/nrw,nvw->nrv/dot_general | solution.py:80
  (75 shorter events, 115.1 us)
Async XLA Ops:
  3.8 21.3 %all-to-all-start = ((f32[32,2,1]{1,2,0:T(1,128)}), f32[32,2,1]{1,2,0:T(1,128)S(1)}, u32[]{:S(2)}, u32[]{:S(2)}) async-start(f32[32,2,1]{1,2,0:T(1,128)} %bitcast.5), calls=%async_computation | async-start | bytes 32768 | tf_op jit(solution)/shard_map/all_to_all | solution.py:48
  13.7 6.6 %copy-start = (f32[1,32,256,256]{3,2,1,0:T(8,128)S(1)}, f32[1,32,256,256]{3,2,1,0:T(8,128)}, u32[]{:S(2)}) copy-start(f32[1,32,256,256]{3,2,1,0:T(8,128)} %param.7) | copy-start | bytes 25165828
  25.1 24.3 %all-to-all-start.1 = ((f32[64,16,256]{2,1,0:T(8,128)}), f32[64,16,256]{2,1,0:T(8,128)S(1)}, u32[]{:S(2)}, u32[]{:S(2)}) async-start(f32[64,16,256]{2,1,0:T(8,128)} %copy.68), calls=%async_computation.1 | async-start | bytes 2097152 | tf_op jit(solution)/shard_map/all_to_all | solution.py:86
  50.5 14.7 %collective-permute-start = (f32[32,16,256]{2,0,1:T(8,128)S(1)}, f32[32,16,256]{2,0,1:T(8,128)S(1)}, u32[]{:S(2)}, u32[]{:S(2)}) collective-permute-start(f32[32,16,256]{2,0,1:T(8,128)S(1)} %fusion.51), channel_id=1, source_target_pairs={{0,32},{1,33},{2,34},{3,35},{4,36},{5,37},{6,38},{7,39},{8,40},{9,... | collective-permute-start | bytes 1572872 | tf_op jit(solution)/shard_map/ppermute | solution.py:13
  101.0 15.3 %collective-permute-start.1 = (f32[32,16,256]{2,0,1:T(8,128)S(1)}, f32[32,16,256]{2,0,1:T(8,128)S(1)}, u32[]{:S(2)}, u32[]{:S(2)}) collective-permute-start(f32[32,16,256]{2,0,1:T(8,128)S(1)} %fusion.49), channel_id=1, source_target_pairs={{0,32},{32,64},{1,33},{33,65},{2,34},{34,66},{3,35},{35,67},{4,36}... | collective-permute-start | bytes 1572872 | tf_op jit(solution)/shard_map/ppermute | solution.py:13
  152.9 0.9 collective-permute-start.2
  189.9 1.8 collective-permute-start.3
  206.0 0.7 collective-permute-start.4
  209.2 21.3 %all-to-all-start.5 = ((f32[64,16,256]{2,1,0:T(8,128)}), f32[64,16,256]{2,1,0:T(8,128)S(1)}, u32[]{:S(2)}, u32[]{:S(2)}) async-start(f32[64,16,256]{2,1,0:T(8,128)} %copy.84), calls=%async_computation.5 | async-start | bytes 2097152 | tf_op jit(solution)/shard_map/all_to_all | solution.py:95
  245.2 0.7 collective-permute-start.5
  248.4 21.0 %all-to-all-start.6 = ((f32[64,16,256]{2,1,0:T(8,128)}), f32[64,16,256]{2,1,0:T(8,128)S(1)}, u32[]{:S(2)}, u32[]{:S(2)}) async-start(f32[64,16,256]{2,1,0:T(8,128)} %copy.88), calls=%async_computation.6 | async-start | bytes 2097152 | tf_op jit(solution)/shard_map/all_to_all | solution.py:95
  284.1 74.7 %copy-start.1 = (f32[32,16,256]{2,1,0:T(8,128)}, f32[32,16,256]{2,1,0:T(8,128)S(1)}, u32[]{:S(2)}) copy-start(f32[32,16,256]{2,1,0:T(8,128)S(1)} %fusion.20) | copy-start | bytes 1572868
  284.1 72.2 %collective-permute-start.6 = (f32[32,16,256]{2,1,0:T(8,128)S(1)}, f32[32,16,256]{2,1,0:T(8,128)S(1)}, u32[]{:S(2)}, u32[]{:S(2)}) collective-permute-start(f32[32,16,256]{2,1,0:T(8,128)S(1)} %fusion.20), channel_id=1, source_target_pairs={{32,0},{64,32},{33,1},{65,33},{34,2},{66,34},{35,3},{67,35},{36,4}... | collective-permute-start | bytes 1572872 | tf_op jit(solution)/shard_map/ppermute | solution.py:13
  358.8 21.5 %all-to-all-start.7 = ((f32[64,16,256]{2,1,0:T(8,128)}), f32[64,16,256]{2,1,0:T(8,128)S(1)}, u32[]{:S(2)}, u32[]{:S(2)}) async-start(f32[64,16,256]{2,1,0:T(8,128)} %copy.92), calls=%async_computation.7 | async-start | bytes 2097152 | tf_op jit(solution)/shard_map/all_to_all | solution.py:95
  395.0 17.8 %copy-start.3 = (f32[32,16,256]{2,1,0:T(8,128)}, f32[32,16,256]{2,1,0:T(8,128)S(1)}, u32[]{:S(2)}) copy-start(f32[32,16,256]{2,1,0:T(8,128)S(1)} %fusion.18) | copy-start | bytes 1572868
  395.0 15.2 %collective-permute-start.7 = (f32[32,16,256]{2,1,0:T(8,128)S(1)}, f32[32,16,256]{2,1,0:T(8,128)S(1)}, u32[]{:S(2)}, u32[]{:S(2)}) collective-permute-start(f32[32,16,256]{2,1,0:T(8,128)S(1)} %fusion.18), channel_id=1, source_target_pairs={{32,0},{33,1},{34,2},{35,3},{36,4},{37,5},{38,6},{39,7},{40,8},{41... | collective-permute-start | bytes 1572872 | tf_op jit(solution)/shard_map/ppermute | solution.py:13
  412.8 21.9 %all-to-all-start.8 = ((f32[64,16,256]{2,1,0:T(8,128)}), f32[64,16,256]{2,1,0:T(8,128)S(1)}, u32[]{:S(2)}, u32[]{:S(2)}) async-start(f32[64,16,256]{2,1,0:T(8,128)} %copy.96), calls=%async_computation.8 | async-start | bytes 2097152 | tf_op jit(solution)/shard_map/all_to_all | solution.py:95
  434.6 7.9 %copy-start.2 = (f32[32,16,256]{2,1,0:T(8,128)S(1)}, f32[32,16,256]{2,1,0:T(8,128)}, u32[]{:S(2)}) copy-start(f32[32,16,256]{2,1,0:T(8,128)} %copy-done.1) | copy-start | bytes 1572868
  434.6 7.9 %copy-start.4 = (f32[32,16,256]{2,1,0:T(8,128)S(1)}, f32[32,16,256]{2,1,0:T(8,128)}, u32[]{:S(2)}) copy-start(f32[32,16,256]{2,1,0:T(8,128)} %copy-done.3) | copy-start | bytes 1572868

commit v4 on v2

--- a/solution.py
+++ b/solution.py
@@ -2,6 +2,7 @@
 import jax.numpy as jnp
 from jax import lax
 from jax.sharding import PartitionSpec as P
+from jax.experimental.layout import Layout, with_layout_constraint
 
 CHUNKS = 2
 MAIN_PRECISION = lax.Precision.HIGHEST
@@ -54,6 +55,9 @@
     given = [right_sides[0, :, j * rows:(j + 1) * rows] for j in range(chunks)]
     diag_inverse = inverse[0]
     couple_block = coupling[0]
+    row_major = Layout(major_to_minor=(0, 1, 2))
+    inverse_t = with_layout_constraint(jnp.swapaxes(diag_inverse, 1, 2), row_major)
+    couple_t = with_layout_constraint(jnp.swapaxes(couple_block, 1, 2), row_major)
     zero_chunk = jnp.zeros((node_count, rows, width), jnp.float32)
     solved = [zero_chunk] * chunks
     result = [zero_chunk] * chunks
@@ -75,9 +79,9 @@
             b_active = (b_index >= 0) & (b_index < chunks)
             source = pick_chunk(solved, b_index)
             if any(l < top for l in bwd_levels):
-                lowered = jnp.einsum("nrv,nwv->nrw", picked, couple_block, precision=main)
+                lowered = jnp.einsum("nrv,nvw->nrw", picked, couple_t, precision=main)
                 source = source - lowered
-            backward_part = jnp.einsum("nrw,nvw->nrv", source, diag_inverse, precision=main)
+            backward_part = jnp.einsum("nrw,nwv->nrv", source, inverse_t, precision=main)
             result = store_chunk(result, jnp.where(b_active, b_index, -1), backward_part)
         senders = [l for l in fwd_levels if l < top]
         if senders:

time: 491 us -> 464 us (0.945)
  matrix products: 160 us -> 132 us
  local copies, waits for them, and re-layouts: 12.4 us -> 30.4 us
  waiting for transfers between devices: 188 us -> 170 us
    dot_general x9, matrix products: 84.2 us -> 56.4 us  [the longest x5 30 us: body(): jnp.einsum('nrw,nwv->nrv', source, inverse_t, precision=main)]
    unnamed x10 -> x16, local copies, waits for them, and re-layouts: 0.04 us -> 18.1 us
    ppermute x8, waiting for transfers between devices: 106 us -> 97.1 us  [shift_leaf(): return lax.ppermute(block, 'leaf', pairs)]
    all_to_all x5, waiting for transfers between devices: 81.8 us -> 72.9 us  [body(): lax.all_to_all(buffer, 'panel', split_axis=0, concat_axis=0, tiled=True)]
  transfers between devices with their start and end apart: 14 -> 14, of which waited for: 9 -> 9; matrix products, arithmetic and copies ran while one was open for 4% -> 8% of each run, Pallas kernels for 0% -> 0%
where the time goes in v4:
time: 464 us; the launch traced here: 455 us
  waiting for transfers between devices  170 us (37%)
  matrix products  132 us (28%)
  blocking collectives  63 us (14%)
  starting transfers between devices  49.2 us (11%)
  local copies, waits for them, and re-layouts  30.4 us (7%)
  other arithmetic  8.6 us (2%)
    ppermute x8, waiting for transfers between devices, shift_leaf(): return lax.ppermute(block, 'leaf', pairs)  97.1 us
    all_to_all x5, waiting for transfers between devices, body(): lax.all_to_all(buffer, 'panel', split_axis=0, concat_axis=0, tiled=True)  72.9 us
    all_to_all x3, blocking collectives, body(): lax.all_to_all(buffer, 'panel', split_axis=0, concat_axis=0, tiled=True)  63 us
    dot_general x5, matrix products, body(): jnp.einsum('nrw,nwv->nrv', rhs - incoming, diag_inverse, precision=main)  33.5 us
    dot_general x5, matrix products, body(): jnp.einsum('nrw,nwv->nrv', source, inverse_t, precision=main)  30 us
    dot_general x4, matrix products, body(): lowered = jnp.einsum('nrv,nvw->nrw', picked, couple_t, precision=main)  26.4 us
    all_to_all x5, starting transfers between devices, body(): lax.all_to_all(buffer, 'panel', split_axis=0, concat_axis=0, tiled=True)  25.6 us
    dot_general x4, matrix products, body(): jnp.einsum('nrw,nwv->nrv', forward_part, couple_block, precision=main)  23.4 us
  transfers between devices with their start and end apart: 14, of which 9 were waited for; matrix products, arithmetic and copies ran while one was open for 8% of the time, Pallas kernels for 0%

profile of v4, /device:TPU:1, one launch (start us, length us, event | category | flops | bytes accessed | tf_op | source)
XLA Modules:
  0.0 454.7 jit_solution(7245533550313312238)
XLA Ops:
  3.8 8.6 %all-to-all-start = ((f32[32,2,1]{1,2,0:T(1,128)}), f32[32,2,1]{1,2,0:T(1,128)S(1)}, u32[]{:S(2)}, u32[]{:S(2)}) async-start(f32[32,2,1]{1,2,0:T(1,128)} %bitcast.5), calls=%async_computation | async-start | bytes 32768 | tf_op jit(solution)/shard_map/all_to_all | solution.py:49
  14.3 6.9 %fusion.32 = f32[32,16,256]{2,1,0:T(8,128)S(1)} fusion(f32[1,32,256,256]{3,2,1,0:T(8,128)} %param.6, f32[32,16,256]{2,0,1:T(8,128)S(1)} %select_bitcast_fusion), kind=kOutput, calls=%fused_computation.32 | convolution fusion | flops 402653184 | bytes 9437184 | tf_op jit(solution)/shard_map/nrw,nwv->nrv/dot_general | solution.py:75
  27.8 7.4 %all-to-all-start.1 = ((f32[64,16,256]{2,1,0:T(8,128)}), f32[64,16,256]{2,1,0:T(8,128)S(1)}, u32[]{:S(2)}, u32[]{:S(2)}) async-start(f32[64,16,256]{2,1,0:T(8,128)} %copy.108), calls=%async_computation.1 | async-start | bytes 2097152 | tf_op jit(solution)/shard_map/all_to_all | solution.py:90
  36.5 15.6 %all-to-all-done.1 = f32[64,16,256]{2,1,0:T(8,128)S(1)} async-done(((f32[64,16,256]{2,1,0:T(8,128)}), f32[64,16,256]{2,1,0:T(8,128)S(1)}, u32[]{:S(2)}, u32[]{:S(2)}) %all-to-all-start.1) | async-done | bytes 1048608 | tf_op jit(solution)/shard_map/all_to_all | solution.py:90
  57.3 10.6 %collective-permute-done = f32[32,16,256]{2,0,1:T(8,128)S(1)} collective-permute-done((f32[32,16,256]{2,0,1:T(8,128)S(1)}, f32[32,16,256]{2,0,1:T(8,128)S(1)}, u32[]{:S(2)}, u32[]{:S(2)}) %collective-permute-start) | collective-permute-done | bytes 524320 | tf_op jit(solution)/shard_map/ppermute | solution.py:14
  68.5 6.6 %fusion.30 = f32[32,16,256]{2,1,0:T(8,128)S(1)} fusion(f32[1,32,256,256]{3,2,1,0:T(8,128)} %param.6, f32[32,16,256]{2,0,1:T(8,128)S(1)} %bitcast_subtract_fusion), kind=kOutput, calls=%fused_computation.30 | convolution fusion | flops 402653184 | bytes 9437184 | tf_op jit(solution)/shard_map/nrw,nwv->nrv/dot_general | solution.py:75
  83.1 21.2 %all_to_all.49 = f32[64,16,256]{2,1,0:T(8,128)S(1)} all-to-all(f32[64,16,256]{2,1,0:T(8,128)S(1)} %copy.114), channel_id=1, replica_groups=mesh['leaf'=4,'panel'=32] {'panel'}, dimensions={0} | all-to-all | bytes 2097152 | tf_op jit(solution)/shard_map/all_to_all | solution.py:90
  109.7 10.9 %collective-permute-done.1 = f32[32,16,256]{2,0,1:T(8,128)S(1)} collective-permute-done((f32[32,16,256]{2,0,1:T(8,128)S(1)}, f32[32,16,256]{2,0,1:T(8,128)S(1)}, u32[]{:S(2)}, u32[]{:S(2)}) %collective-permute-start.1) | collective-permute-done | bytes 524320 | tf_op jit(solution)/shard_map/ppermute | solution.py:14
  121.2 6.6 %fusion.28 = f32[32,16,256]{2,1,0:T(8,128)S(1)} fusion(f32[1,32,256,256]{3,2,1,0:T(8,128)} %param.6, f32[32,16,256]{2,0,1:T(8,128)S(1)} %bitcast_subtract_fusion.1), kind=kOutput, calls=%fused_computation.28 | convolution fusion | flops 402653184 | bytes 9437184 | tf_op jit(solution)/shard_map/nrw,nwv->nrv/dot_general | solution.py:75
  135.8 21.2 %all_to_all.50 = f32[64,16,256]{2,1,0:T(8,128)S(1)} all-to-all(f32[64,16,256]{2,1,0:T(8,128)S(1)} %copy.120), channel_id=1, replica_groups=mesh['leaf'=4,'panel'=32] {'panel'}, dimensions={0} | all-to-all | bytes 2097152 | tf_op jit(solution)/shard_map/all_to_all | solution.py:90
  160.5 6.6 %fusion.26 = f32[32,16,256]{2,1,0:T(8,128)S(1)} fusion(f32[1,32,256,256]{3,2,1,0:T(8,128)} %param.6, f32[32,16,256]{2,0,1:T(8,128)S(1)} %bitcast_subtract_fusion.2), kind=kOutput, calls=%fused_computation.26 | convolution fusion | flops 402653184 | bytes 9437184 | tf_op jit(solution)/shard_map/nrw,nwv->nrv/dot_general | solution.py:75
  175.0 20.6 %all_to_all.51 = f32[64,16,256]{2,1,0:T(8,128)S(1)} all-to-all(f32[64,16,256]{2,1,0:T(8,128)S(1)} %copy.126), channel_id=1, replica_groups=mesh['leaf'=4,'panel'=32] {'panel'}, dimensions={0} | all-to-all | bytes 2097152 | tf_op jit(solution)/shard_map/all_to_all | solution.py:90
  199.4 9.0 %copy.102 = f32[1,32,256,256]{2,3,1,0:T(8,128)} copy(f32[1,32,256,256]{3,2,1,0:T(8,128)} %param.6) | data formatting | bytes 16777216 | tf_op args[1]
  210.3 6.8 %broadcast_select_fusion.1 = (f32[32,16,256]{2,1,0:T(8,128)S(1)}, f32[32,16,256]{2,1,0:T(8,128)S(1)}, f32[32,16,256]{2,1,0:T(8,128)S(1)}, f32[32,16,256]{2,1,0:T(8,128)S(1)}) fusion(pred[]{:T(512)S(6)} %eq.131, f32[32,16,256]{2,1,0:T(8,128)S(1)} %fusion.26, f32[32,16,256]{2,1,0:T(8,128)S(1)} %fusion.28, f32[32,16,256]{2,1,0:T(8,128)S(1)} %fusion.30, ...), kind=kOutput, calls=%fused_computation.105 | convolution fusion | flops 403963904 | bytes 13107210 | tf_op jit(solution)/shard_map/nrw,nwv->nrv/dot_general | solution.py:75
  228.9 9.0 %copy.105 = f32[1,32,256,256]{2,3,1,0:T(8,128)} copy(f32[1,32,256,256]{3,2,1,0:T(8,128)} %param.7) | data formatting | bytes 16777216 | tf_op args[2]
  237.9 7.8 %all-to-all-done.5 = f32[64,16,256]{2,1,0:T(8,128)S(1)} async-done(((f32[64,16,256]{2,1,0:T(8,128)}), f32[64,16,256]{2,1,0:T(8,128)S(1)}, u32[]{:S(2)}, u32[]{:S(2)}) %all-to-all-start.5) | async-done | bytes 1048608 | tf_op jit(solution)/shard_map/all_to_all | solution.py:99
  246.9 6.6 %fusion.4 = f32[32,16,256]{2,1,0:T(8,128)S(1)} fusion(f32[1,32,256,256]{2,3,1,0:T(8,128)} %copy.105, f32[32,16,256]{2,0,1:T(8,128)S(1)} %fusion.43), kind=kOutput, calls=%fused_computation.4 | convolution fusion | flops 402653184 | bytes 9437184 | tf_op jit(solution)/shard_map/nrv,nvw->nrw/dot_general | solution.py:82
  267.4 16.8 %all-to-all-done.6 = f32[64,16,256]{2,1,0:T(8,128)S(1)} async-done(((f32[64,16,256]{2,1,0:T(8,128)}), f32[64,16,256]{2,1,0:T(8,128)S(1)}, u32[]{:S(2)}, u32[]{:S(2)}) %all-to-all-start.6) | async-done | bytes 1048608 | tf_op jit(solution)/shard_map/all_to_all | solution.py:99
  285.3 6.6 %fusion.2 = f32[32,16,256]{2,1,0:T(8,128)S(1)} fusion(f32[1,32,256,256]{2,3,1,0:T(8,128)} %copy.105, f32[32,16,256]{2,0,1:T(8,128)S(1)} %fusion.41), kind=kOutput, calls=%fused_computation.2 | convolution fusion | flops 402653184 | bytes 9437184 | tf_op jit(solution)/shard_map/nrv,nvw->nrw/dot_general | solution.py:82
  299.7 61.7 %collective-permute-done.6 = f32[32,16,256]{2,1,0:T(8,128)S(1)} collective-permute-done((f32[32,16,256]{2,1,0:T(8,128)S(1)}, f32[32,16,256]{2,1,0:T(8,128)S(1)}, u32[]{:S(2)}, u32[]{:S(2)}) %collective-permute-start.6) | collective-permute-done | bytes 524320 | tf_op jit(solution)/shard_map/ppermute | solution.py:14
  368.5 16.9 %all-to-all-done.7 = f32[64,16,256]{2,1,0:T(8,128)S(1)} async-done(((f32[64,16,256]{2,1,0:T(8,128)}), f32[64,16,256]{2,1,0:T(8,128)S(1)}, u32[]{:S(2)}, u32[]{:S(2)}) %all-to-all-start.7) | async-done | bytes 1048608 | tf_op jit(solution)/shard_map/all_to_all | solution.py:99
  386.5 6.6 %fusion = f32[32,16,256]{2,1,0:T(8,128)S(1)} fusion(f32[1,32,256,256]{2,3,1,0:T(8,128)} %copy.105, f32[32,16,256]{2,0,1:T(8,128)S(1)} %fusion.39), kind=kOutput, calls=%fused_computation | convolution fusion | flops 402653184 | bytes 9437184 | tf_op jit(solution)/shard_map/nrv,nvw->nrw/dot_general | solution.py:82
  400.9 13.9 %collective-permute-done.7 = f32[32,16,256]{2,1,0:T(8,128)S(1)} collective-permute-done((f32[32,16,256]{2,1,0:T(8,128)S(1)}, f32[32,16,256]{2,1,0:T(8,128)S(1)}, u32[]{:S(2)}, u32[]{:S(2)}) %collective-permute-start.7) | collective-permute-done | bytes 524320 | tf_op jit(solution)/shard_map/ppermute | solution.py:14
  423.4 15.8 %all-to-all-done.8 = f32[64,16,256]{2,1,0:T(8,128)S(1)} async-done(((f32[64,16,256]{2,1,0:T(8,128)}), f32[64,16,256]{2,1,0:T(8,128)S(1)}, u32[]{:S(2)}, u32[]{:S(2)}) %all-to-all-start.8) | async-done | bytes 1048608 | tf_op jit(solution)/shard_map/all_to_all | solution.py:99
  (82 shorter events, 133.0 us)
Async XLA Ops:
  3.8 24.0 %all-to-all-start = ((f32[32,2,1]{1,2,0:T(1,128)}), f32[32,2,1]{1,2,0:T(1,128)S(1)}, u32[]{:S(2)}, u32[]{:S(2)}) async-start(f32[32,2,1]{1,2,0:T(1,128)} %bitcast.5), calls=%async_computation | async-start | bytes 32768 | tf_op jit(solution)/shard_map/all_to_all | solution.py:49
  13.7 7.5 %copy-start = (f32[1,32,256,256]{3,2,1,0:T(8,128)S(1)}, f32[1,32,256,256]{3,2,1,0:T(8,128)}, u32[]{:S(2)}) copy-start(f32[1,32,256,256]{3,2,1,0:T(8,128)} %param.7) | copy-start | bytes 25165828
  27.8 24.3 %all-to-all-start.1 = ((f32[64,16,256]{2,1,0:T(8,128)}), f32[64,16,256]{2,1,0:T(8,128)S(1)}, u32[]{:S(2)}, u32[]{:S(2)}) async-start(f32[64,16,256]{2,1,0:T(8,128)} %copy.108), calls=%async_computation.1 | async-start | bytes 2097152 | tf_op jit(solution)/shard_map/all_to_all | solution.py:90
  53.2 14.7 %collective-permute-start = (f32[32,16,256]{2,0,1:T(8,128)S(1)}, f32[32,16,256]{2,0,1:T(8,128)S(1)}, u32[]{:S(2)}, u32[]{:S(2)}) collective-permute-start(f32[32,16,256]{2,0,1:T(8,128)S(1)} %fusion.51), channel_id=1, source_target_pairs={{0,32},{1,33},{2,34},{3,35},{4,36},{5,37},{6,38},{7,39},{8,40},{9,... | collective-permute-start | bytes 1572872 | tf_op jit(solution)/shard_map/ppermute | solution.py:14
  105.4 15.3 %collective-permute-start.1 = (f32[32,16,256]{2,0,1:T(8,128)S(1)}, f32[32,16,256]{2,0,1:T(8,128)S(1)}, u32[]{:S(2)}, u32[]{:S(2)}) collective-permute-start(f32[32,16,256]{2,0,1:T(8,128)S(1)} %fusion.49), channel_id=1, source_target_pairs={{0,32},{32,64},{1,33},{33,65},{2,34},{34,66},{3,35},{35,67},{4,36}... | collective-permute-start | bytes 1572872 | tf_op jit(solution)/shard_map/ppermute | solution.py:14
  158.9 0.9 collective-permute-start.2
  197.6 10.9 %collective-permute-start.3 = (f32[32,16,256]{2,0,1:T(8,128)}, f32[32,16,256]{2,0,1:T(8,128)}, u32[]{:S(2)}, u32[]{:S(2)}) collective-permute-start(f32[32,16,256]{2,0,1:T(8,128)} %fusion.45), channel_id=1, source_target_pairs={{64,96},{65,97},{66,98},{67,99},{68,100},{69,101},{70,102},{71,103... | collective-permute-start | bytes 1572872 | tf_op jit(solution)/shard_map/ppermute | solution.py:14
  208.5 8.6 %slice-start = ((s8[8388608]{0:T(1024)(128)(4,1)}), s8[4194304]{0:T(1024)(128)(4,1)S(1)}, s32[]{:S(2)}) async-start(s8[8388608]{0:T(1024)(128)(4,1)} %bitcast.112), calls=%async_computation.9 | async-start | bytes 8388608
  210.3 6.8 %slice-start.1 = ((s8[8388608]{0:T(1024)(128)(4,1)}), s8[4194304]{0:T(1024)(128)(4,1)S(1)}, s32[]{:S(2)}) async-start(s8[8388608]{0:T(1024)(128)(4,1)} %bitcast.112), calls=%async_computation.10 | async-start | bytes 8388608
  221.2 0.7 collective-permute-start.4
  224.4 21.3 %all-to-all-start.5 = ((f32[64,16,256]{2,1,0:T(8,128)}), f32[64,16,256]{2,1,0:T(8,128)S(1)}, u32[]{:S(2)}, u32[]{:S(2)}) async-start(f32[64,16,256]{2,1,0:T(8,128)} %copy.131), calls=%async_computation.5 | async-start | bytes 2097152 | tf_op jit(solution)/shard_map/all_to_all | solution.py:99
  259.9 0.7 collective-permute-start.5
  263.2 21.0 %all-to-all-start.6 = ((f32[64,16,256]{2,1,0:T(8,128)}), f32[64,16,256]{2,1,0:T(8,128)S(1)}, u32[]{:S(2)}, u32[]{:S(2)}) async-start(f32[64,16,256]{2,1,0:T(8,128)} %copy.135), calls=%async_computation.6 | async-start | bytes 2097152 | tf_op jit(solution)/shard_map/all_to_all | solution.py:99
  298.3 65.5 %copy-start.1 = (f32[32,16,256]{2,1,0:T(8,128)}, f32[32,16,256]{2,1,0:T(8,128)S(1)}, u32[]{:S(2)}) copy-start(f32[32,16,256]{2,1,0:T(8,128)S(1)} %fusion.10) | copy-start | bytes 1572868
  298.4 63.0 %collective-permute-start.6 = (f32[32,16,256]{2,1,0:T(8,128)S(1)}, f32[32,16,256]{2,1,0:T(8,128)S(1)}, u32[]{:S(2)}, u32[]{:S(2)}) collective-permute-start(f32[32,16,256]{2,1,0:T(8,128)S(1)} %fusion.10), channel_id=1, source_target_pairs={{32,0},{64,32},{33,1},{65,33},{34,2},{66,34},{35,3},{67,35},{36,4}... | collective-permute-start | bytes 1572872 | tf_op jit(solution)/shard_map/ppermute | solution.py:14
  363.8 21.5 %all-to-all-start.7 = ((f32[64,16,256]{2,1,0:T(8,128)}), f32[64,16,256]{2,1,0:T(8,128)S(1)}, u32[]{:S(2)}, u32[]{:S(2)}) async-start(f32[64,16,256]{2,1,0:T(8,128)} %copy.139), calls=%async_computation.7 | async-start | bytes 2097152 | tf_op jit(solution)/shard_map/all_to_all | solution.py:99
  399.5 17.8 %copy-start.3 = (f32[32,16,256]{2,1,0:T(8,128)}, f32[32,16,256]{2,1,0:T(8,128)S(1)}, u32[]{:S(2)}) copy-start(f32[32,16,256]{2,1,0:T(8,128)S(1)} %fusion.8) | copy-start | bytes 1572868
  399.6 15.2 %collective-permute-start.7 = (f32[32,16,256]{2,1,0:T(8,128)S(1)}, f32[32,16,256]{2,1,0:T(8,128)S(1)}, u32[]{:S(2)}, u32[]{:S(2)}) collective-permute-start(f32[32,16,256]{2,1,0:T(8,128)S(1)} %fusion.8), channel_id=1, source_target_pairs={{32,0},{33,1},{34,2},{35,3},{36,4},{37,5},{38,6},{39,7},{40,8},{41... | collective-permute-start | bytes 1572872 | tf_op jit(solution)/shard_map/ppermute | solution.py:14
  417.3 21.8 %all-to-all-start.8 = ((f32[64,16,256]{2,1,0:T(8,128)}), f32[64,16,256]{2,1,0:T(8,128)S(1)}, u32[]{:S(2)}, u32[]{:S(2)}) async-start(f32[64,16,256]{2,1,0:T(8,128)} %copy.143), calls=%async_computation.8 | async-start | bytes 2097152 | tf_op jit(solution)/shard_map/all_to_all | solution.py:99
  439.2 7.7 %copy-start.2 = (f32[32,16,256]{2,1,0:T(8,128)S(1)}, f32[32,16,256]{2,1,0:T(8,128)}, u32[]{:S(2)}) copy-start(f32[32,16,256]{2,1,0:T(8,128)} %copy-done.1) | copy-start | bytes 1572868
  439.2 7.7 %copy-start.4 = (f32[32,16,256]{2,1,0:T(8,128)S(1)}, f32[32,16,256]{2,1,0:T(8,128)}, u32[]{:S(2)}) copy-start(f32[32,16,256]{2,1,0:T(8,128)} %copy-done.3) | copy-start | bytes 1572868

commit v5 on v4

--- a/solution.py
+++ b/solution.py
@@ -4,14 +4,16 @@
 from jax.sharding import PartitionSpec as P
 from jax.experimental.layout import Layout, with_layout_constraint
 
-CHUNKS = 2
+CHUNKS = 4
 MAIN_PRECISION = lax.Precision.HIGHEST
 
 
 def shift_leaf(block, pairs):
-    if not pairs:
-        return jnp.zeros_like(block)
     return lax.ppermute(block, "leaf", pairs)
+
+
+def exchange(buffer):
+    return lax.all_to_all(buffer, "panel", split_axis=0, concat_axis=0, tiled=True)
 
 
 def pick_chunk(chunks, index):
@@ -46,7 +48,7 @@
     slot_iota = jnp.arange(slot_count, dtype=jnp.int32)
     send_onehot = (slot_iota[:, None] == dest_slot[None, :]).astype(jnp.float32)
     send_ids = jnp.dot(send_onehot, (positions + 1).astype(jnp.float32), precision=highest) - 1.0
-    arrived_ids = lax.all_to_all(send_ids, "panel", split_axis=0, concat_axis=0, tiled=True)
+    arrived_ids = exchange(send_ids)
     node_float = node_iota.astype(jnp.float32)
     recv_onehot = (arrived_ids[None, :] == node_float[:, None]).astype(jnp.float32)
 
@@ -84,20 +86,27 @@
             backward_part = jnp.einsum("nrw,nwv->nrv", source, inverse_t, precision=main)
             result = store_chunk(result, jnp.where(b_active, b_index, -1), backward_part)
         senders = [l for l in fwd_levels if l < top]
+        down = [l for l in bwd_levels if l > 0]
         if senders:
             updates = jnp.einsum("nrw,nwv->nrv", forward_part, couple_block, precision=main)
-            buffer = jnp.einsum("ts,srw->trw", send_onehot, updates, precision=highest)
-            arrived = lax.all_to_all(buffer, "panel", split_axis=0, concat_axis=0, tiled=True)
-            summed = jnp.einsum("st,trw->srw", recv_onehot, arrived, precision=highest)
+            fwd_buffer = jnp.einsum("ts,srw->trw", send_onehot, updates, precision=highest)
+        if down:
+            lowered_in = shift_leaf(backward_part, [(l, l - 1) for l in down])
+            bwd_buffer = jnp.einsum("st,srw->trw", recv_onehot, lowered_in, precision=highest)
+        if senders and down:
+            arrived = exchange(jnp.concatenate([fwd_buffer, bwd_buffer], axis=1))
+            fwd_arrived, bwd_arrived = arrived[:, :rows], arrived[:, rows:]
+        elif senders:
+            fwd_arrived = exchange(fwd_buffer)
+        elif down:
+            bwd_arrived = exchange(bwd_buffer)
+        if senders:
+            summed = jnp.einsum("st,trw->srw", recv_onehot, fwd_arrived, precision=highest)
             incoming = shift_leaf(summed, [(l, l + 1) for l in senders])
         else:
             incoming = zero_chunk
-        down = [l for l in bwd_levels if l > 0]
         if down:
-            lowered_in = shift_leaf(backward_part, [(l, l - 1) for l in down])
-            buffer = jnp.einsum("st,srw->trw", recv_onehot, lowered_in, precision=highest)
-            arrived = lax.all_to_all(buffer, "panel", split_axis=0, concat_axis=0, tiled=True)
-            picked = jnp.einsum("ts,trw->srw", send_onehot, arrived, precision=highest)
+            picked = jnp.einsum("ts,trw->srw", send_onehot, bwd_arrived, precision=highest)
         else:
             picked = zero_chunk
     solved_all = jnp.concatenate(solved, axis=1)

time: 464 us -> 448 us (0.966)
  waiting for transfers between devices: 170 us -> 135 us
  matrix products: 132 us -> 164 us
  blocking collectives: 63 us -> 31 us
  starting transfers between devices: 49.2 us -> 66.4 us
    ppermute x8 -> x12, waiting for transfers between devices: 97.1 us -> 49.5 us  [shift_leaf(): return lax.ppermute(block, 'leaf', pairs)]
    all_to_all x3 -> x2, blocking collectives: 63 us -> 31 us  [exchange(): lax.all_to_all(buffer, 'panel', split_axis=0, concat_axis=0, tiled=True)]
    all_to_all x6 -> x8, waiting for transfers between devices: 72.9 us -> 85.9 us  [exchange(): lax.all_to_all(buffer, 'panel', split_axis=0, concat_axis=0, tiled=True)]
    dot_general x5 -> x7, matrix products: 33.5 us -> 46.3 us  [body(): jnp.einsum('nrw,nwv->nrv', rhs - incoming, diag_inverse, precision=main)]
    dot_general x4 -> x6, matrix products: 26.4 us -> 39 us  [body(): lowered = jnp.einsum('nrv,nvw->nrw', picked, couple_t, precision=main)]
    all_to_all x6 -> x8, starting transfers between devices: 34.2 us -> 43.2 us  [exchange(): lax.all_to_all(buffer, 'panel', split_axis=0, concat_axis=0, tiled=True)]
    ppermute x8 -> x12, starting transfers between devices: 15 us -> 23.1 us  [shift_leaf(): return lax.ppermute(block, 'leaf', pairs)]
    dot_general x4 -> x6, matrix products: 23.4 us -> 31.3 us  [body(): jnp.einsum('nrw,nwv->nrv', forward_part, couple_block, precision=main)]
  transfers between devices with their start and end apart: 14 -> 20, of which waited for: 9 -> 13; matrix products, arithmetic and copies ran while one was open for 8% -> 16% of each run, Pallas kernels for 0% -> 0%
where the time goes in v5:
time: 448 us; the launch traced here: 440 us
  matrix products  164 us (37%)
  waiting for transfers between devices  135 us (30%)
  starting transfers between devices  66.4 us (15%)
  local copies, waits for them, and re-layouts  33.2 us (7%)
  blocking collectives  31 us (7%)
  other arithmetic  7.35 us (2%)
    all_to_all x8, waiting for transfers between devices, exchange(): lax.all_to_all(buffer, 'panel', split_axis=0, concat_axis=0, tiled=True)  85.9 us
    ppermute x12, waiting for transfers between devices, shift_leaf(): return lax.ppermute(block, 'leaf', pairs)  49.5 us
    dot_general x7, matrix products, body(): jnp.einsum('nrw,nwv->nrv', rhs - incoming, diag_inverse, precision=main)  46.3 us
    all_to_all x8, starting transfers between devices, exchange(): lax.all_to_all(buffer, 'panel', split_axis=0, concat_axis=0, tiled=True)  43.2 us
    dot_general x6, matrix products, body(): lowered = jnp.einsum('nrv,nvw->nrw', picked, couple_t, precision=main)  39 us
    dot_general x7, matrix products, body(): jnp.einsum('nrw,nwv->nrv', source, inverse_t, precision=main)  35.7 us
    dot_general x6, matrix products, body(): jnp.einsum('nrw,nwv->nrv', forward_part, couple_block, precision=main)  31.3 us
    all_to_all x2, blocking collectives, exchange(): lax.all_to_all(buffer, 'panel', split_axis=0, concat_axis=0, tiled=True)  31 us
  transfers between devices with their start and end apart: 20, of which 13 were waited for; matrix products, arithmetic and copies ran while one was open for 16% of the time, Pallas kernels for 0%

profile of v5, /device:TPU:1, one launch (start us, length us, event | category | flops | bytes accessed | tf_op | source)
XLA Modules:
  0.0 439.9 jit_solution(15465954833485361116)
XLA Ops:
  3.8 8.6 %all-to-all-start = ((f32[32,2,1]{1,2,0:T(1,128)}), f32[32,2,1]{1,2,0:T(1,128)S(1)}, u32[]{:S(2)}, u32[]{:S(2)}) async-start(f32[32,2,1]{1,2,0:T(1,128)} %bitcast.5), calls=%async_computation | async-start | bytes 32768 | tf_op jit(solution)/shard_map/all_to_all | solution.py:16
  14.1 6.8 %fusion.48 = f32[32,8,256]{2,1,0:T(8,128)S(1)} fusion(f32[1,32,256,256]{3,2,1,0:T(8,128)} %param.6, f32[32,8,256]{2,0,1:T(8,128)S(1)} %select_bitcast_fusion), kind=kOutput, calls=%fused_computation.48 | convolution fusion | flops 201326592 | bytes 8912896 | tf_op jit(solution)/shard_map/nrw,nwv->nrv/dot_general | solution.py:77
  26.6 7.4 %all-to-all-start.1 = ((f32[64,8,256]{2,1,0:T(8,128)}), f32[64,8,256]{2,1,0:T(8,128)S(1)}, u32[]{:S(2)}, u32[]{:S(2)}) async-start(f32[64,8,256]{2,1,0:T(8,128)} %copy.162), calls=%async_computation.1 | async-start | bytes 1048576 | tf_op jit(solution)/shard_map/all_to_all | solution.py:16
  35.3 10.3 %all-to-all-done.1 = f32[64,8,256]{2,1,0:T(8,128)S(1)} async-done(((f32[64,8,256]{2,1,0:T(8,128)}), f32[64,8,256]{2,1,0:T(8,128)S(1)}, u32[]{:S(2)}, u32[]{:S(2)}) %all-to-all-start.1) | async-done | bytes 524320 | tf_op jit(solution)/shard_map/all_to_all | solution.py:16
  69.5 15.3 %all_to_all.54 = f32[64,8,256]{2,1,0:T(8,128)S(1)} all-to-all(f32[64,8,256]{2,1,0:T(8,128)S(1)} %copy.168), channel_id=1, replica_groups=mesh['leaf'=4,'panel'=32] {'panel'}, dimensions={0} | all-to-all | bytes 1048576 | tf_op jit(solution)/shard_map/all_to_all | solution.py:16
  109.3 15.7 %all_to_all.55 = f32[64,8,256]{2,1,0:T(8,128)S(1)} all-to-all(f32[64,8,256]{2,1,0:T(8,128)S(1)} %copy.174), channel_id=1, replica_groups=mesh['leaf'=4,'panel'=32] {'panel'}, dimensions={0} | all-to-all | bytes 1048576 | tf_op jit(solution)/shard_map/all_to_all | solution.py:16
  129.7 9.0 %copy.156 = f32[1,32,256,256]{2,3,1,0:T(8,128)} copy(f32[1,32,256,256]{3,2,1,0:T(8,128)} %param.6) | data formatting | bytes 16777216 | tf_op args[1]
  139.0 6.6 %select_select_fusion.7 = (f32[32,8,256]{2,1,0:T(8,128)S(1)}, f32[32,8,256]{2,1,0:T(8,128)S(1)}) fusion(f32[32,8,256]{2,1,0:T(8,128)S(1)} %fusion.44, f32[32,8,256]{2,1,0:T(8,128)S(1)} %fusion.46, f32[32,8,256]{2,1,0:T(8,128)S(1)} %fusion.48, pred[]{:T(512)S(6)} %eq.371, pred[]{:T(512)S(6)} %eq.370, pred[]{:T(512)S(6)} %eq.369, pred[]{:T(512)S(6)} %eq.368, ...), kind=kOutput, calls=%fused_computation.160 | convolution fusion | flops 201588736 | bytes 9961476 | tf_op jit(solution)/shard_map/nrw,nwv->nrv/dot_general | solution.py:77
  164.2 9.0 %copy.159 = f32[1,32,256,256]{2,3,1,0:T(8,128)} copy(f32[1,32,256,256]{3,2,1,0:T(8,128)} %param.7) | data formatting | bytes 16777216 | tf_op args[2]
  173.2 7.9 %all-to-all-done.4 = f32[64,16,256]{2,1,0:T(8,128)} async-done(((f32[64,16,256]{2,1,0:T(8,128)}), f32[64,16,256]{2,1,0:T(8,128)}, u32[]{:S(2)}, u32[]{:S(2)}) %all-to-all-start.4) | async-done | bytes 1048608 | tf_op jit(solution)/shard_map/all_to_all | solution.py:16
  192.3 6.6 %fusion.40 = f32[32,8,256]{2,1,0:T(8,128)S(1)} fusion(f32[1,32,256,256]{3,2,1,0:T(8,128)} %param.6, f32[32,8,256]{2,0,1:T(8,128)S(1)} %bitcast_subtract_fusion.3), kind=kOutput, calls=%fused_computation.40 | convolution fusion | flops 201326592 | bytes 8912896 | tf_op jit(solution)/shard_map/nrw,nwv->nrv/dot_general | solution.py:77
  215.5 17.0 %all-to-all-done.5 = f32[64,16,256]{2,1,0:T(8,128)} async-done(((f32[64,16,256]{2,1,0:T(8,128)}), f32[64,16,256]{2,1,0:T(8,128)}, u32[]{:S(2)}, u32[]{:S(2)}) %all-to-all-start.5) | async-done | bytes 1048608 | tf_op jit(solution)/shard_map/all_to_all | solution.py:16
  235.7 6.6 %fusion.6 = f32[32,8,256]{2,1,0:T(8,128)S(1)} fusion(f32[1,32,256,256]{2,3,1,0:T(8,128)} %copy.159, f32[32,8,256]{2,0,1:T(8,128)S(1)} %fusion.57), kind=kOutput, calls=%fused_computation.6 | convolution fusion | flops 201326592 | bytes 8912896 | tf_op jit(solution)/shard_map/nrv,nvw->nrw/dot_general | solution.py:84
  242.6 6.7 %broadcast_select_fusion.3 = (f32[32,8,256]{2,1,0:T(8,128)S(1)}, f32[32,8,256]{2,1,0:T(8,128)S(1)}, f32[32,8,256]{2,1,0:T(8,128)S(1)}, f32[32,8,256]{2,1,0:T(8,128)S(1)}, f32[32,8,256]{2,1,0:T(8,128)S(1)}) fusion(pred[]{:T(512)S(6)} %eq.399, f32[32,8,256]{2,1,0:T(8,128)S(1)} %fusion.40, f32[32,8,256]{2,1,0:T(8,128)S(1)} %get-tuple-element.8, ...), kind=kOutput, calls=%fused_computation.177 | convolution fusion | flops 201850880 | bytes 11272200 | tf_op jit(solution)/shard_map/nrw,nwv->nrv/dot_general | solution.py:77
  259.8 12.0 %collective-permute-done.7 = f32[32,8,256]{2,1,0:T(8,128)S(1)} collective-permute-done((f32[32,8,256]{2,1,0:T(8,128)S(1)}, f32[32,8,256]{2,1,0:T(8,128)S(1)}, u32[]{:S(2)}, u32[]{:S(2)}) %collective-permute-start.7) | collective-permute-done | bytes 262176 | tf_op jit(solution)/shard_map/ppermute | solution.py:12
  278.6 17.0 %all-to-all-done.6 = f32[64,16,256]{2,1,0:T(8,128)S(1)} async-done(((f32[64,16,256]{2,1,0:T(8,128)}), f32[64,16,256]{2,1,0:T(8,128)S(1)}, u32[]{:S(2)}, u32[]{:S(2)}) %all-to-all-start.6) | async-done | bytes 1048608 | tf_op jit(solution)/shard_map/all_to_all | solution.py:16
  297.5 6.6 %fusion.4 = f32[32,8,256]{2,1,0:T(8,128)S(1)} fusion(f32[1,32,256,256]{2,3,1,0:T(8,128)} %copy.159, f32[32,8,256]{2,0,1:T(8,128)S(1)} %fusion.53), kind=kOutput, calls=%fused_computation.4 | convolution fusion | flops 201326592 | bytes 8912896 | tf_op jit(solution)/shard_map/nrv,nvw->nrw/dot_general | solution.py:84
  304.4 6.6 %broadcast_select_fusion.11 = (f32[32,8,256]{2,1,0:T(8,128)S(1)}, f32[32,8,256]{2,1,0:T(8,128)S(1)}, f32[32,8,256]{2,1,0:T(8,128)S(1)}, f32[32,8,256]{2,1,0:T(8,128)S(1)}) fusion(f32[32,8,256]{2,1,0:T(8,128)S(1)} %get-tuple-element.15, pred[]{:T(512)S(6)} %eq.335, f32[32,8,256]{2,1,0:T(8,128)S(1)} %copy-done.5, pred[]{:T(512)S(6)} %eq.402, ...), kind=kOutput, calls=%fused_computation.194 | convolution fusion | flops 201588736 | bytes 10747908 | tf_op jit(solution)/shard_map/nrw,nwv->nrv/dot_general | solution.py:77
  316.5 8.3 %collective-permute-done.9 = f32[32,8,256]{2,1,0:T(8,128)S(1)} collective-permute-done((f32[32,8,256]{2,1,0:T(8,128)S(1)}, f32[32,8,256]{2,1,0:T(8,128)S(1)}, u32[]{:S(2)}, u32[]{:S(2)}) %collective-permute-start.9) | collective-permute-done | bytes 262176 | tf_op jit(solution)/shard_map/ppermute | solution.py:12
  331.3 11.6 %all-to-all-done.7 = f32[64,8,256]{2,1,0:T(8,128)S(1)} async-done(((f32[64,8,256]{2,1,0:T(8,128)}), f32[64,8,256]{2,1,0:T(8,128)S(1)}, u32[]{:S(2)}, u32[]{:S(2)}) %all-to-all-start.7) | async-done | bytes 524320 | tf_op jit(solution)/shard_map/all_to_all | solution.py:16
  357.5 8.7 %collective-permute-done.10 = f32[32,8,256]{2,1,0:T(8,128)S(1)} collective-permute-done((f32[32,8,256]{2,1,0:T(8,128)S(1)}, f32[32,8,256]{2,1,0:T(8,128)S(1)}, u32[]{:S(2)}, u32[]{:S(2)}) %collective-permute-start.10) | collective-permute-done | bytes 262176 | tf_op jit(solution)/shard_map/ppermute | solution.py:12
  371.9 11.7 %all-to-all-done.8 = f32[64,8,256]{2,1,0:T(8,128)S(1)} async-done(((f32[64,8,256]{2,1,0:T(8,128)}), f32[64,8,256]{2,1,0:T(8,128)S(1)}, u32[]{:S(2)}, u32[]{:S(2)}) %all-to-all-start.8) | async-done | bytes 524320 | tf_op jit(solution)/shard_map/all_to_all | solution.py:16
  398.3 8.8 %collective-permute-done.11 = f32[32,8,256]{2,1,0:T(8,128)S(1)} collective-permute-done((f32[32,8,256]{2,1,0:T(8,128)S(1)}, f32[32,8,256]{2,1,0:T(8,128)S(1)}, u32[]{:S(2)}, u32[]{:S(2)}) %collective-permute-start.11) | collective-permute-done | bytes 262176 | tf_op jit(solution)/shard_map/ppermute | solution.py:12
  414.3 10.4 %all-to-all-done.9 = f32[64,8,256]{2,1,0:T(8,128)S(1)} async-done(((f32[64,8,256]{2,1,0:T(8,128)}), f32[64,8,256]{2,1,0:T(8,128)S(1)}, u32[]{:S(2)}, u32[]{:S(2)}) %all-to-all-start.9) | async-done | bytes 524320 | tf_op jit(solution)/shard_map/all_to_all | solution.py:16
  (144 shorter events, 202.5 us)
Async XLA Ops:
  3.8 22.8 %all-to-all-start = ((f32[32,2,1]{1,2,0:T(1,128)}), f32[32,2,1]{1,2,0:T(1,128)S(1)}, u32[]{:S(2)}, u32[]{:S(2)}) async-start(f32[32,2,1]{1,2,0:T(1,128)} %bitcast.5), calls=%async_computation | async-start | bytes 32768 | tf_op jit(solution)/shard_map/all_to_all | solution.py:16
  26.6 19.0 %all-to-all-start.1 = ((f32[64,8,256]{2,1,0:T(8,128)}), f32[64,8,256]{2,1,0:T(8,128)S(1)}, u32[]{:S(2)}, u32[]{:S(2)}) async-start(f32[64,8,256]{2,1,0:T(8,128)} %copy.162), calls=%async_computation.1 | async-start | bytes 1048576 | tf_op jit(solution)/shard_map/all_to_all | solution.py:16
  46.1 9.5 %collective-permute-start = (f32[32,8,256]{2,0,1:T(8,128)S(1)}, f32[32,8,256]{2,0,1:T(8,128)S(1)}, u32[]{:S(2)}, u32[]{:S(2)}) collective-permute-start(f32[32,8,256]{2,0,1:T(8,128)S(1)} %fusion.75), channel_id=1, source_target_pairs={{0,32},{1,33},{2,34},{3,35},{4,36},{5,37},{6,38},{7,39},{8,40},{9,... | collective-permute-start | bytes 786440 | tf_op jit(solution)/shard_map/ppermute | solution.py:12
  85.3 10.0 %collective-permute-start.1 = (f32[32,8,256]{2,0,1:T(8,128)S(1)}, f32[32,8,256]{2,0,1:T(8,128)S(1)}, u32[]{:S(2)}, u32[]{:S(2)}) collective-permute-start(f32[32,8,256]{2,0,1:T(8,128)S(1)} %fusion.73), channel_id=1, source_target_pairs={{0,32},{32,64},{1,33},{33,65},{2,34},{34,66},{3,35},{35,67},{4,36}... | collective-permute-start | bytes 786440 | tf_op jit(solution)/shard_map/ppermute | solution.py:12
  125.5 13.2 %collective-permute-start.2 = (f32[32,8,256]{2,0,1:T(8,128)S(1)}, f32[32,8,256]{2,0,1:T(8,128)S(1)}, u32[]{:S(2)}, u32[]{:S(2)}) collective-permute-start(f32[32,8,256]{2,0,1:T(8,128)S(1)} %fusion.71), channel_id=1, source_target_pairs={{0,32},{32,64},{64,96},{1,33},{33,65},{65,97},{2,34},{34,66},{66,9... | collective-permute-start | bytes 786440 | tf_op jit(solution)/shard_map/ppermute | solution.py:12
  149.8 7.6 %collective-permute-start.3 = (f32[32,8,256]{2,1,0:T(8,128)S(1)}, f32[32,8,256]{2,1,0:T(8,128)S(1)}, u32[]{:S(2)}, u32[]{:S(2)}) collective-permute-start(f32[32,8,256]{2,1,0:T(8,128)S(1)} %fusion.22), channel_id=1, source_target_pairs={{96,64},{97,65},{98,66},{99,67},{100,68},{101,69},{102,70},{103,71... | collective-permute-start | bytes 786440 | tf_op jit(solution)/shard_map/ppermute | solution.py:12
  159.5 21.5 %all-to-all-start.4 = ((f32[64,16,256]{2,1,0:T(8,128)}), f32[64,16,256]{2,1,0:T(8,128)}, u32[]{:S(2)}, u32[]{:S(2)}) async-start(f32[64,16,256]{2,1,0:T(8,128)} %copy.181), calls=%async_computation.4 | async-start | bytes 2097152 | tf_op jit(solution)/shard_map/all_to_all | solution.py:16
  183.3 15.6 %slice-start = ((s8[8388608]{0:T(1024)(128)(4,1)}), s8[4194304]{0:T(1024)(128)(4,1)S(1)}, s32[]{:S(2)}) async-start(s8[8388608]{0:T(1024)(128)(4,1)} %bitcast.154), calls=%async_computation.10 | async-start | bytes 8388608
  183.3 8.7 %collective-permute-start.4 = (f32[32,8,256]{2,0,1:T(8,128)S(1)}, f32[32,8,256]{2,0,1:T(8,128)S(1)}, u32[]{:S(2)}, u32[]{:S(2)}) collective-permute-start(f32[32,8,256]{2,0,1:T(8,128)S(1)} %fusion.63), channel_id=1, source_target_pairs={{0,32},{32,64},{64,96},{1,33},{33,65},{65,97},{2,34},{34,66},{66,9... | collective-permute-start | bytes 786440 | tf_op jit(solution)/shard_map/ppermute | solution.py:12
  203.1 5.5 %collective-permute-start.5 = (f32[32,8,256]{2,1,0:T(8,128)S(1)}, f32[32,8,256]{2,1,0:T(8,128)S(1)}, u32[]{:S(2)}, u32[]{:S(2)}) collective-permute-start(f32[32,8,256]{2,1,0:T(8,128)S(1)} %fusion.20), channel_id=1, source_target_pairs={{64,32},{96,64},{65,33},{97,65},{66,34},{98,66},{67,35},{99,67},{6... | collective-permute-start | bytes 786440 | tf_op jit(solution)/shard_map/ppermute | solution.py:12
  210.8 21.7 %all-to-all-start.5 = ((f32[64,16,256]{2,1,0:T(8,128)}), f32[64,16,256]{2,1,0:T(8,128)}, u32[]{:S(2)}, u32[]{:S(2)}) async-start(f32[64,16,256]{2,1,0:T(8,128)} %copy.190), calls=%async_computation.5 | async-start | bytes 2097152 | tf_op jit(solution)/shard_map/all_to_all | solution.py:16
  234.7 7.6 %collective-permute-start.6 = (f32[32,8,256]{2,0,1:T(8,128)S(1)}, f32[32,8,256]{2,0,1:T(8,128)S(1)}, u32[]{:S(2)}, u32[]{:S(2)}) collective-permute-start(f32[32,8,256]{2,0,1:T(8,128)S(1)} %fusion.59), channel_id=1, source_target_pairs={{32,64},{64,96},{33,65},{65,97},{34,66},{66,98},{35,67},{67,99},{3... | collective-permute-start | bytes 786440 | tf_op jit(solution)/shard_map/ppermute | solution.py:12
  235.7 13.7 %slice-start.2 = ((s8[8388608]{0:T(1024)(128)(4,1)}), s8[4194304]{0:T(1024)(128)(4,1)S(1)}, s32[]{:S(2)}) async-start(s8[8388608]{0:T(1024)(128)(4,1)} %bitcast.156), calls=%async_computation.12 | async-start | bytes 8388608
  242.3 13.0 %slice-start.8 = ((s8[8388608]{0:T(1024)(128)(4,1)}), s8[4194304]{0:T(1024)(128)(4,1)S(1)}, s32[]{:S(2)}) async-start(s8[8388608]{0:T(1024)(128)(4,1)} %bitcast.162), calls=%async_computation.18 | async-start | bytes 8388608
  253.5 18.3 %collective-permute-start.7 = (f32[32,8,256]{2,1,0:T(8,128)S(1)}, f32[32,8,256]{2,1,0:T(8,128)S(1)}, u32[]{:S(2)}, u32[]{:S(2)}) collective-permute-start(f32[32,8,256]{2,1,0:T(8,128)S(1)} %fusion.18), channel_id=1, source_target_pairs={{32,0},{64,32},{96,64},{33,1},{65,33},{97,65},{34,2},{66,34},{98,6... | collective-permute-start | bytes 786440 | tf_op jit(solution)/shard_map/ppermute | solution.py:12
  274.0 21.6 %all-to-all-start.6 = ((f32[64,16,256]{2,1,0:T(8,128)}), f32[64,16,256]{2,1,0:T(8,128)S(1)}, u32[]{:S(2)}, u32[]{:S(2)}) async-start(f32[64,16,256]{2,1,0:T(8,128)} %copy.199), calls=%async_computation.6 | async-start | bytes 2097152 | tf_op jit(solution)/shard_map/all_to_all | solution.py:16
  296.6 7.5 %collective-permute-start.8 = (f32[32,8,256]{2,0,1:T(8,128)S(1)}, f32[32,8,256]{2,0,1:T(8,128)S(1)}, u32[]{:S(2)}, u32[]{:S(2)}) collective-permute-start(f32[32,8,256]{2,0,1:T(8,128)S(1)} %fusion.55), channel_id=1, source_target_pairs={{64,96},{65,97},{66,98},{67,99},{68,100},{69,101},{70,102},{71,103... | collective-permute-start | bytes 786440 | tf_op jit(solution)/shard_map/ppermute | solution.py:12
  297.5 13.6 %slice-start.4 = ((s8[8388608]{0:T(1024)(128)(4,1)}), s8[4194304]{0:T(1024)(128)(4,1)S(1)}, s32[]{:S(2)}) async-start(s8[8388608]{0:T(1024)(128)(4,1)} %bitcast.158), calls=%async_computation.14 | async-start | bytes 8388608
  315.2 9.6 %collective-permute-start.9 = (f32[32,8,256]{2,1,0:T(8,128)S(1)}, f32[32,8,256]{2,1,0:T(8,128)S(1)}, u32[]{:S(2)}, u32[]{:S(2)}) collective-permute-start(f32[32,8,256]{2,1,0:T(8,128)S(1)} %fusion.16), channel_id=1, source_target_pairs={{32,0},{64,32},{96,64},{33,1},{65,33},{97,65},{34,2},{66,34},{98,6... | collective-permute-start | bytes 786440 | tf_op jit(solution)/shard_map/ppermute | solution.py:12
  326.4 16.4 %all-to-all-start.7 = ((f32[64,8,256]{2,1,0:T(8,128)}), f32[64,8,256]{2,1,0:T(8,128)S(1)}, u32[]{:S(2)}, u32[]{:S(2)}) async-start(f32[64,8,256]{2,1,0:T(8,128)} %copy.206), calls=%async_computation.7 | async-start | bytes 1048576 | tf_op jit(solution)/shard_map/all_to_all | solution.py:16
  356.2 10.0 %collective-permute-start.10 = (f32[32,8,256]{2,1,0:T(8,128)S(1)}, f32[32,8,256]{2,1,0:T(8,128)S(1)}, u32[]{:S(2)}, u32[]{:S(2)}) collective-permute-start(f32[32,8,256]{2,1,0:T(8,128)S(1)} %fusion.14), channel_id=1, source_target_pairs={{32,0},{64,32},{33,1},{65,33},{34,2},{66,34},{35,3},{67,35},{36,4}... | collective-permute-start | bytes 786440 | tf_op jit(solution)/shard_map/ppermute | solution.py:12
  367.8 15.8 %all-to-all-start.8 = ((f32[64,8,256]{2,1,0:T(8,128)}), f32[64,8,256]{2,1,0:T(8,128)S(1)}, u32[]{:S(2)}, u32[]{:S(2)}) async-start(f32[64,8,256]{2,1,0:T(8,128)} %copy.210), calls=%async_computation.8 | async-start | bytes 1048576 | tf_op jit(solution)/shard_map/all_to_all | solution.py:16
  397.0 10.0 %collective-permute-start.11 = (f32[32,8,256]{2,1,0:T(8,128)S(1)}, f32[32,8,256]{2,1,0:T(8,128)S(1)}, u32[]{:S(2)}, u32[]{:S(2)}) collective-permute-start(f32[32,8,256]{2,1,0:T(8,128)S(1)} %fusion.12), channel_id=1, source_target_pairs={{32,0},{33,1},{34,2},{35,3},{36,4},{37,5},{38,6},{39,7},{40,8},{41... | collective-permute-start | bytes 786440 | tf_op jit(solution)/shard_map/ppermute | solution.py:12
  408.6 16.1 %all-to-all-start.9 = ((f32[64,8,256]{2,1,0:T(8,128)}), f32[64,8,256]{2,1,0:T(8,128)S(1)}, u32[]{:S(2)}, u32[]{:S(2)}) async-start(f32[64,8,256]{2,1,0:T(8,128)} %copy.214), calls=%async_computation.9 | async-start | bytes 1048576 | tf_op jit(solution)/shard_map/all_to_all | solution.py:16
  (12 other events, 103.1 us)

commit v6 on v5

--- a/solution.py
+++ b/solution.py
@@ -5,7 +5,6 @@
 from jax.experimental.layout import Layout, with_layout_constraint
 
 CHUNKS = 4
-MAIN_PRECISION = lax.Precision.HIGHEST
 
 
 def shift_leaf(block, pairs):
@@ -14,6 +13,27 @@
 
 def exchange(buffer):
     return lax.all_to_all(buffer, "panel", split_axis=0, concat_axis=0, tiled=True)
+
+
+def split3(a):
+    rounded = lambda v: lax.reduce_precision(v, exponent_bits=8, mantissa_bits=7)
+    hi = rounded(a)
+    rest = a - hi
+    mid = rounded(rest)
+    lo = rest - mid
+    return tuple(p.astype(jnp.bfloat16) for p in (hi, mid, lo))
+
+
+def product(x, parts):
+    hi, mid, lo = parts
+    rows = x.shape[1]
+    xh, xm, xl = split3(x)
+    mul = lambda a, w: jnp.einsum("nrw,nwv->nrv", a, w, preferred_element_type=jnp.float32)
+    first = mul(jnp.concatenate([xh, xm, xl], axis=1), hi)
+    second = mul(jnp.concatenate([xh, xm], axis=1), mid)
+    third = mul(xh, lo)
+    small = (first[:, 2 * rows:] + second[:, rows:] + third) + (first[:, rows:2 * rows] + second[:, :rows])
+    return small + first[:, :rows]
 
 
 def pick_chunk(chunks, index):
@@ -29,7 +49,6 @@
 
 def body(right_sides, inverse, coupling, owner_map, parent_slot):
     highest = lax.Precision.HIGHEST
-    main = MAIN_PRECISION
     levels = lax.axis_size("leaf")
     panels = lax.axis_size("panel")
     level = lax.axis_index("leaf")
@@ -60,6 +79,10 @@
     row_major = Layout(major_to_minor=(0, 1, 2))
     inverse_t = with_layout_constraint(jnp.swapaxes(diag_inverse, 1, 2), row_major)
     couple_t = with_layout_constraint(jnp.swapaxes(couple_block, 1, 2), row_major)
+    inverse_parts = split3(diag_inverse)
+    couple_parts = split3(couple_block)
+    inverse_t_parts = split3(inverse_t)
+    couple_t_parts = split3(couple_t)
     zero_chunk = jnp.zeros((node_count, rows, width), jnp.float32)
     solved = [zero_chunk] * chunks
     result = [zero_chunk] * chunks
@@ -74,21 +97,21 @@
             f_index = turn - level
             f_active = (f_index >= 0) & (f_index < chunks)
             rhs = pick_chunk(given, f_index)
-            forward_part = jnp.einsum("nrw,nwv->nrv", rhs - incoming, diag_inverse, precision=main)
+            forward_part = product(rhs - incoming, inverse_parts)
             solved = store_chunk(solved, jnp.where(f_active, f_index, -1), forward_part)
         if bwd_levels:
             b_index = turn - 2 * top + level
             b_active = (b_index >= 0) & (b_index < chunks)
             source = pick_chunk(solved, b_index)
             if any(l < top for l in bwd_levels):
-                lowered = jnp.einsum("nrv,nvw->nrw", picked, couple_t, precision=main)
+                lowered = product(picked, couple_t_parts)
                 source = source - lowered
-            backward_part = jnp.einsum("nrw,nwv->nrv", source, inverse_t, precision=main)
+            backward_part = product(source, inverse_t_parts)
             result = store_chunk(result, jnp.where(b_active, b_index, -1), backward_part)
         senders = [l for l in fwd_levels if l < top]
         down = [l for l in bwd_levels if l > 0]
         if senders:
-            updates = jnp.einsum("nrw,nwv->nrv", forward_part, couple_block, precision=main)
+            updates = product(forward_part, couple_parts)
             fwd_buffer = jnp.einsum("ts,srw->trw", send_onehot, updates, precision=highest)
         if down:
             lowered_in = shift_leaf(backward_part, [(l, l - 1) for l in down])

time: 448 us -> 457 us (1.020)
  matrix products: 164 us -> 103 us
  other arithmetic: 7.35 us -> 34.9 us
  local copies, waits for them, and re-layouts: 33.2 us -> 54.2 us
  waiting for transfers between devices: 135 us -> 156 us
    dot_general x26 -> x78, matrix products: 152 us -> 90.5 us  [product(): jnp.einsum('nrw,nwv->nrv', a, w, preferred_element_type=jnp.float32)]
    convert_element_type x0 -> x20, other arithmetic: none -> 30.1 us  [split3(): return tuple((p.astype(jnp.bfloat16) for p in (hi, mid, lo)))]
    unnamed x34 -> x182, local copies, waits for them, and re-layouts: 18 us -> 42 us
    ppermute x12, waiting for transfers between devices: 49.5 us -> 68.2 us  [shift_leaf(): return lax.ppermute(block, 'leaf', pairs)]
  transfers between devices with their start and end apart: 20 -> 20, of which waited for: 13 -> 14; matrix products, arithmetic and copies ran while one was open for 16% -> 15% of each run, Pallas kernels for 0% -> 0%
where the time goes in v6:
time: 457 us; the launch traced here: 449 us
  waiting for transfers between devices  156 us (34%)
  matrix products  103 us (23%)
  starting transfers between devices  67.6 us (15%)
  local copies, waits for them, and re-layouts  54.2 us (12%)
  other arithmetic  34.9 us (8%)
  blocking collectives  30.7 us (7%)
    dot_general x78, matrix products, product(): jnp.einsum('nrw,nwv->nrv', a, w, preferred_element_type=jnp.float32)  90.5 us
    all_to_all x8, waiting for transfers between devices, exchange(): lax.all_to_all(buffer, 'panel', split_axis=0, concat_axis=0, tiled=True)  88.1 us
    ppermute x12, waiting for transfers between devices, shift_leaf(): return lax.ppermute(block, 'leaf', pairs)  68.2 us
    all_to_all x8, starting transfers between devices, exchange(): lax.all_to_all(buffer, 'panel', split_axis=0, concat_axis=0, tiled=True)  42.2 us
    unnamed x182, local copies, waits for them, and re-layouts  42 us
    all_to_all x2, blocking collectives, exchange(): lax.all_to_all(buffer, 'panel', split_axis=0, concat_axis=0, tiled=True)  30.7 us
    convert_element_type x20, other arithmetic, split3(): return tuple((p.astype(jnp.bfloat16) for p in (hi, mid, lo)))  30.1 us
    ppermute x12, starting transfers between devices, shift_leaf(): return lax.ppermute(block, 'leaf', pairs)  25.4 us
  transfers between devices with their start and end apart: 20, of which 14 were waited for; matrix products, arithmetic and copies ran while one was open for 15% of the time, Pallas kernels for 0%

profile of v6, /device:TPU:1, one launch (start us, length us, event | category | flops | bytes accessed | tf_op | source)
XLA Modules:
  0.0 449.4 jit_solution(7476564511845899109)
XLA Ops:
  3.8 8.6 %all-to-all-start = ((f32[32,2,1]{1,2,0:T(1,128)}), f32[32,2,1]{1,2,0:T(1,128)S(1)}, u32[]{:S(2)}, u32[]{:S(2)}) async-start(f32[32,2,1]{1,2,0:T(1,128)} %bitcast.5), calls=%async_computation | async-start | bytes 32768 | tf_op jit(solution)/shard_map/all_to_all | solution.py:15
  13.7 9.0 %copy.237 = f32[1,32,256,256]{2,3,1,0:T(8,128)} copy(f32[1,32,256,256]{3,2,1,0:T(8,128)} %param.6) | data formatting | bytes 16777216 | tf_op args[1]
  22.7 9.0 %copy.241 = f32[1,32,256,256]{2,3,1,0:T(8,128)} copy(f32[1,32,256,256]{3,2,1,0:T(8,128)} %param.7) | data formatting | bytes 16777216 | tf_op args[2]
  36.4 9.0 %reduce-precision_convert_fusion.6 = (bf16[32,256,256]{1,2,0:T(8,128)(2,1)S(1)}, bf16[32,256,256]{1,2,0:T(8,128)(2,1)S(1)}, bf16[32,256,256]{1,2,0:T(8,128)(2,1)S(1)}) fusion(f32[1,32,256,256]{2,3,1,0:T(8,128)} %copy.237), kind=kLoop, calls=%fused_computation.13 | loop fusion | flops 14680064 | bytes 20971520 | tf_op jit(solution)/shard_map/convert_element_type | solution.py:24
  56.0 7.4 %all-to-all-start.1 = ((f32[64,8,256]{2,1,0:T(8,128)}), f32[64,8,256]{2,1,0:T(8,128)S(1)}, u32[]{:S(2)}, u32[]{:S(2)}) async-start(f32[64,8,256]{2,1,0:T(8,128)} %copy.246), calls=%async_computation.1 | async-start | bytes 1048576 | tf_op jit(solution)/shard_map/all_to_all | solution.py:15
  64.6 10.4 %all-to-all-done.1 = f32[64,8,256]{2,1,0:T(8,128)S(1)} async-done(((f32[64,8,256]{2,1,0:T(8,128)}), f32[64,8,256]{2,1,0:T(8,128)S(1)}, u32[]{:S(2)}, u32[]{:S(2)}) %all-to-all-start.1) | async-done | bytes 524320 | tf_op jit(solution)/shard_map/all_to_all | solution.py:15
  79.4 5.7 %collective-permute-done = f32[32,8,256]{2,1,0:T(8,128)S(1)} collective-permute-done((f32[32,8,256]{2,1,0:T(8,128)S(1)}, f32[32,8,256]{2,1,0:T(8,128)S(1)}, u32[]{:S(2)}, u32[]{:S(2)}) %collective-permute-start) | collective-permute-done | bytes 262176 | tf_op jit(solution)/shard_map/ppermute | solution.py:11
  96.4 15.3 %all_to_all.54 = f32[64,8,256]{2,1,0:T(8,128)S(1)} all-to-all(f32[64,8,256]{2,1,0:T(8,128)S(1)} %copy.256), channel_id=1, replica_groups=mesh['leaf'=4,'panel'=32] {'panel'}, dimensions={0} | all-to-all | bytes 1048576 | tf_op jit(solution)/shard_map/all_to_all | solution.py:15
  116.5 5.9 %collective-permute-done.1 = f32[32,8,256]{2,1,0:T(8,128)S(1)} collective-permute-done((f32[32,8,256]{2,1,0:T(8,128)S(1)}, f32[32,8,256]{2,1,0:T(8,128)S(1)}, u32[]{:S(2)}, u32[]{:S(2)}) %collective-permute-start.1) | collective-permute-done | bytes 262176 | tf_op jit(solution)/shard_map/ppermute | solution.py:11
  133.7 15.3 %all_to_all.55 = f32[64,8,256]{2,1,0:T(8,128)S(1)} all-to-all(f32[64,8,256]{2,1,0:T(8,128)S(1)} %copy.266), channel_id=1, replica_groups=mesh['leaf'=4,'panel'=32] {'panel'}, dimensions={0} | all-to-all | bytes 1048576 | tf_op jit(solution)/shard_map/all_to_all | solution.py:15
  154.0 6.1 %reduce-precision_convert_fusion.2 = (bf16[32,256,256]{2,1,0:T(8,128)(2,1)}, bf16[32,256,256]{2,1,0:T(8,128)(2,1)}, bf16[32,256,256]{2,1,0:T(8,128)(2,1)}) fusion(f32[1,32,256,256]{2,3,1,0:T(8,128)S(1)} %bitcast.221), kind=kLoop, calls=%fused_computation.5 | loop fusion | flops 14680064 | bytes 20971520 | tf_op jit(solution)/shard_map/convert_element_type | solution.py:24
  181.8 8.0 %reduce-precision_convert_fusion = (bf16[32,256,256]{2,1,0:T(8,128)(2,1)}, bf16[32,256,256]{2,1,0:T(8,128)(2,1)}, bf16[32,256,256]{2,1,0:T(8,128)(2,1)}) fusion(f32[1,32,256,256]{2,3,1,0:T(8,128)} %copy.241), kind=kLoop, calls=%fused_computation.1 | loop fusion | flops 14680064 | bytes 20971520 | tf_op jit(solution)/shard_map/convert_element_type | solution.py:24
  189.8 8.9 %all-to-all-done.4 = f32[64,16,256]{2,1,0:T(8,128)S(1)} async-done(((f32[64,16,256]{2,1,0:T(8,128)}), f32[64,16,256]{2,1,0:T(8,128)S(1)}, u32[]{:S(2)}, u32[]{:S(2)}) %all-to-all-start.4) | async-done | bytes 1048608 | tf_op jit(solution)/shard_map/all_to_all | solution.py:15
  199.4 4.7 %collective-permute-start.4 = (f32[32,8,256]{2,1,0:T(8,128)S(1)}, f32[32,8,256]{2,1,0:T(8,128)S(1)}, u32[]{:S(2)}, u32[]{:S(2)}) collective-permute-start(f32[32,8,256]{2,1,0:T(8,128)S(1)} %copy.279), channel_id=1, source_target_pairs={{0,32},{32,64},{64,96},{1,33},{33,65},{65,97},{2,34},{34,66},{66,9... | collective-permute-start | bytes 786440 | tf_op jit(solution)/shard_map/ppermute | solution.py:11
  230.2 17.0 %all-to-all-done.5 = f32[64,16,256]{2,1,0:T(8,128)S(1)} async-done(((f32[64,16,256]{2,1,0:T(8,128)}), f32[64,16,256]{2,1,0:T(8,128)S(1)}, u32[]{:S(2)}, u32[]{:S(2)}) %all-to-all-start.5) | async-done | bytes 1048608 | tf_op jit(solution)/shard_map/all_to_all | solution.py:15
  269.4 24.3 %collective-permute-done.7 = f32[32,8,256]{2,1,0:T(8,128)S(1)} collective-permute-done((f32[32,8,256]{2,1,0:T(8,128)S(1)}, f32[32,8,256]{2,1,0:T(8,128)S(1)}, u32[]{:S(2)}, u32[]{:S(2)}) %collective-permute-start.7) | collective-permute-done | bytes 262176 | tf_op jit(solution)/shard_map/ppermute | solution.py:11
  295.8 5.1 %all-to-all-start.6 = ((f32[64,16,256]{2,1,0:T(8,128)}), f32[64,16,256]{2,1,0:T(8,128)S(1)}, u32[]{:S(2)}, u32[]{:S(2)}) async-start(f32[64,16,256]{2,1,0:T(8,128)} %copy.307), calls=%async_computation.6 | async-start | bytes 2097152 | tf_op jit(solution)/shard_map/all_to_all | solution.py:15
  301.0 17.0 %all-to-all-done.6 = f32[64,16,256]{2,1,0:T(8,128)S(1)} async-done(((f32[64,16,256]{2,1,0:T(8,128)}), f32[64,16,256]{2,1,0:T(8,128)S(1)}, u32[]{:S(2)}, u32[]{:S(2)}) %all-to-all-start.6) | async-done | bytes 1048608 | tf_op jit(solution)/shard_map/all_to_all | solution.py:15
  334.5 9.4 %collective-permute-done.9 = f32[32,8,256]{2,1,0:T(8,128)S(1)} collective-permute-done((f32[32,8,256]{2,1,0:T(8,128)S(1)}, f32[32,8,256]{2,1,0:T(8,128)S(1)}, u32[]{:S(2)}, u32[]{:S(2)}) %collective-permute-start.9) | collective-permute-done | bytes 262176 | tf_op jit(solution)/shard_map/ppermute | solution.py:11
  349.7 11.7 %all-to-all-done.7 = f32[64,8,256]{2,1,0:T(8,128)S(1)} async-done(((f32[64,8,256]{2,1,0:T(8,128)}), f32[64,8,256]{2,1,0:T(8,128)S(1)}, u32[]{:S(2)}, u32[]{:S(2)}) %all-to-all-start.7) | async-done | bytes 524320 | tf_op jit(solution)/shard_map/all_to_all | solution.py:15
  372.1 11.3 %collective-permute-done.10 = f32[32,8,256]{2,1,0:T(8,128)S(1)} collective-permute-done((f32[32,8,256]{2,1,0:T(8,128)S(1)}, f32[32,8,256]{2,1,0:T(8,128)S(1)}, u32[]{:S(2)}, u32[]{:S(2)}) %collective-permute-start.10) | collective-permute-done | bytes 262176 | tf_op jit(solution)/shard_map/ppermute | solution.py:11
  389.2 11.6 %all-to-all-done.8 = f32[64,8,256]{2,1,0:T(8,128)S(1)} async-done(((f32[64,8,256]{2,1,0:T(8,128)}), f32[64,8,256]{2,1,0:T(8,128)S(1)}, u32[]{:S(2)}, u32[]{:S(2)}) %all-to-all-start.8) | async-done | bytes 524320 | tf_op jit(solution)/shard_map/all_to_all | solution.py:15
  411.4 8.7 %collective-permute-done.11 = f32[32,8,256]{2,1,0:T(8,128)S(1)} collective-permute-done((f32[32,8,256]{2,1,0:T(8,128)S(1)}, f32[32,8,256]{2,1,0:T(8,128)S(1)}, u32[]{:S(2)}, u32[]{:S(2)}) %collective-permute-start.11) | collective-permute-done | bytes 262176 | tf_op jit(solution)/shard_map/ppermute | solution.py:11
  426.0 11.6 %all-to-all-done.9 = f32[64,8,256]{2,1,0:T(8,128)S(1)} async-done(((f32[64,8,256]{2,1,0:T(8,128)}), f32[64,8,256]{2,1,0:T(8,128)S(1)}, u32[]{:S(2)}, u32[]{:S(2)}) %all-to-all-start.9) | async-done | bytes 524320 | tf_op jit(solution)/shard_map/all_to_all | solution.py:15
  (368 shorter events, 195.8 us)
Async XLA Ops:
  3.8 52.2 %all-to-all-start = ((f32[32,2,1]{1,2,0:T(1,128)}), f32[32,2,1]{1,2,0:T(1,128)S(1)}, u32[]{:S(2)}, u32[]{:S(2)}) async-start(f32[32,2,1]{1,2,0:T(1,128)} %bitcast.5), calls=%async_computation | async-start | bytes 32768 | tf_op jit(solution)/shard_map/all_to_all | solution.py:15
  53.2 31.9 %copy-start.72 = (f32[1,32,32,256]{3,2,1,0:T(8,128)S(1)}, f32[1,32,32,256]{3,2,1,0:T(8,128)}, u32[]{:S(2)}) copy-start(f32[1,32,32,256]{3,2,1,0:T(8,128)} %param.5) | copy-start | bytes 3145732
  56.0 19.0 %all-to-all-start.1 = ((f32[64,8,256]{2,1,0:T(8,128)}), f32[64,8,256]{2,1,0:T(8,128)S(1)}, u32[]{:S(2)}, u32[]{:S(2)}) async-start(f32[64,8,256]{2,1,0:T(8,128)} %copy.246), calls=%async_computation.1 | async-start | bytes 1048576 | tf_op jit(solution)/shard_map/all_to_all | solution.py:15
  75.6 9.5 %collective-permute-start = (f32[32,8,256]{2,1,0:T(8,128)S(1)}, f32[32,8,256]{2,1,0:T(8,128)S(1)}, u32[]{:S(2)}, u32[]{:S(2)}) collective-permute-start(f32[32,8,256]{2,1,0:T(8,128)S(1)} %copy.248), channel_id=1, source_target_pairs={{0,32},{1,33},{2,34},{3,35},{4,36},{5,37},{6,38},{7,39},{8,40},{9,... | collective-permute-start | bytes 786440 | tf_op jit(solution)/shard_map/ppermute | solution.py:11
  112.3 10.0 %collective-permute-start.1 = (f32[32,8,256]{2,1,0:T(8,128)S(1)}, f32[32,8,256]{2,1,0:T(8,128)S(1)}, u32[]{:S(2)}, u32[]{:S(2)}) collective-permute-start(f32[32,8,256]{2,1,0:T(8,128)S(1)} %copy.258), channel_id=1, source_target_pairs={{0,32},{32,64},{1,33},{33,65},{2,34},{34,66},{3,35},{35,67},{4,36}... | collective-permute-start | bytes 786440 | tf_op jit(solution)/shard_map/ppermute | solution.py:11
  149.6 10.4 %collective-permute-start.2 = (f32[32,8,256]{2,1,0:T(8,128)S(1)}, f32[32,8,256]{2,1,0:T(8,128)S(1)}, u32[]{:S(2)}, u32[]{:S(2)}) collective-permute-start(f32[32,8,256]{2,1,0:T(8,128)S(1)} %copy.268), channel_id=1, source_target_pairs={{0,32},{32,64},{64,96},{1,33},{33,65},{65,97},{2,34},{34,66},{66,9... | collective-permute-start | bytes 786440 | tf_op jit(solution)/shard_map/ppermute | solution.py:11
  166.3 49.3 %copy-start.77 = (f32[32,8,256]{2,1,0:T(8,128)}, f32[32,8,256]{2,1,0:T(8,128)S(1)}, u32[]{:S(2)}) copy-start(f32[32,8,256]{2,1,0:T(8,128)S(1)} %get-tuple-element.11) | copy-start | bytes 786436
  166.3 49.3 %copy-start.79 = (f32[32,8,256]{2,1,0:T(8,128)}, f32[32,8,256]{2,1,0:T(8,128)S(1)}, u32[]{:S(2)}) copy-start(f32[32,8,256]{2,1,0:T(8,128)S(1)} %get-tuple-element.12) | copy-start | bytes 786436
  166.3 49.3 %copy-start.81 = (f32[32,8,256]{2,1,0:T(8,128)}, f32[32,8,256]{2,1,0:T(8,128)S(1)}, u32[]{:S(2)}) copy-start(f32[32,8,256]{2,1,0:T(8,128)S(1)} %get-tuple-element.13) | copy-start | bytes 786436
  173.3 2.4 collective-permute-start.3
  177.9 20.8 %all-to-all-start.4 = ((f32[64,16,256]{2,1,0:T(8,128)}), f32[64,16,256]{2,1,0:T(8,128)S(1)}, u32[]{:S(2)}, u32[]{:S(2)}) async-start(f32[64,16,256]{2,1,0:T(8,128)} %copy.277), calls=%async_computation.4 | async-start | bytes 2097152 | tf_op jit(solution)/shard_map/all_to_all | solution.py:15
  199.4 9.9 %collective-permute-start.4 = (f32[32,8,256]{2,1,0:T(8,128)S(1)}, f32[32,8,256]{2,1,0:T(8,128)S(1)}, u32[]{:S(2)}, u32[]{:S(2)}) collective-permute-start(f32[32,8,256]{2,1,0:T(8,128)S(1)} %copy.279), channel_id=1, source_target_pairs={{0,32},{32,64},{64,96},{1,33},{33,65},{65,97},{2,34},{34,66},{66,9... | collective-permute-start | bytes 786440 | tf_op jit(solution)/shard_map/ppermute | solution.py:11
  221.1 2.4 collective-permute-start.5
  225.6 21.6 %all-to-all-start.5 = ((f32[64,16,256]{2,1,0:T(8,128)}), f32[64,16,256]{2,1,0:T(8,128)S(1)}, u32[]{:S(2)}, u32[]{:S(2)}) async-start(f32[64,16,256]{2,1,0:T(8,128)} %copy.292), calls=%async_computation.5 | async-start | bytes 2097152 | tf_op jit(solution)/shard_map/all_to_all | solution.py:15
  247.9 3.6 collective-permute-start.6
  266.4 27.2 %collective-permute-start.7 = (f32[32,8,256]{2,1,0:T(8,128)S(1)}, f32[32,8,256]{2,1,0:T(8,128)S(1)}, u32[]{:S(2)}, u32[]{:S(2)}) collective-permute-start(f32[32,8,256]{2,1,0:T(8,128)S(1)} %fusion.23), channel_id=1, source_target_pairs={{32,0},{64,32},{96,64},{33,1},{65,33},{97,65},{34,2},{66,34},{98,6... | collective-permute-start | bytes 786440 | tf_op jit(solution)/shard_map/ppermute | solution.py:11
  295.8 22.1 %all-to-all-start.6 = ((f32[64,16,256]{2,1,0:T(8,128)}), f32[64,16,256]{2,1,0:T(8,128)S(1)}, u32[]{:S(2)}, u32[]{:S(2)}) async-start(f32[64,16,256]{2,1,0:T(8,128)} %copy.307), calls=%async_computation.6 | async-start | bytes 2097152 | tf_op jit(solution)/shard_map/all_to_all | solution.py:15
  319.3 3.0 collective-permute-start.8
  333.2 10.7 %collective-permute-start.9 = (f32[32,8,256]{2,1,0:T(8,128)S(1)}, f32[32,8,256]{2,1,0:T(8,128)S(1)}, u32[]{:S(2)}, u32[]{:S(2)}) collective-permute-start(f32[32,8,256]{2,1,0:T(8,128)S(1)} %fusion.17), channel_id=1, source_target_pairs={{32,0},{64,32},{96,64},{33,1},{65,33},{97,65},{34,2},{66,34},{98,6... | collective-permute-start | bytes 786440 | tf_op jit(solution)/shard_map/ppermute | solution.py:11
  345.5 15.9 %all-to-all-start.7 = ((f32[64,8,256]{2,1,0:T(8,128)}), f32[64,8,256]{2,1,0:T(8,128)S(1)}, u32[]{:S(2)}, u32[]{:S(2)}) async-start(f32[64,8,256]{2,1,0:T(8,128)} %copy.318), calls=%async_computation.7 | async-start | bytes 1048576 | tf_op jit(solution)/shard_map/all_to_all | solution.py:15
  370.8 12.6 %collective-permute-start.10 = (f32[32,8,256]{2,1,0:T(8,128)S(1)}, f32[32,8,256]{2,1,0:T(8,128)S(1)}, u32[]{:S(2)}, u32[]{:S(2)}) collective-permute-start(f32[32,8,256]{2,1,0:T(8,128)S(1)} %fusion.13), channel_id=1, source_target_pairs={{32,0},{64,32},{33,1},{65,33},{34,2},{66,34},{35,3},{67,35},{36,4}... | collective-permute-start | bytes 786440 | tf_op jit(solution)/shard_map/ppermute | solution.py:11
  384.9 15.9 %all-to-all-start.8 = ((f32[64,8,256]{2,1,0:T(8,128)}), f32[64,8,256]{2,1,0:T(8,128)S(1)}, u32[]{:S(2)}, u32[]{:S(2)}) async-start(f32[64,8,256]{2,1,0:T(8,128)} %copy.324), calls=%async_computation.8 | async-start | bytes 1048576 | tf_op jit(solution)/shard_map/all_to_all | solution.py:15
  410.1 10.0 %collective-permute-start.11 = (f32[32,8,256]{2,1,0:T(8,128)S(1)}, f32[32,8,256]{2,1,0:T(8,128)S(1)}, u32[]{:S(2)}, u32[]{:S(2)}) collective-permute-start(f32[32,8,256]{2,1,0:T(8,128)S(1)} %fusion.9), channel_id=1, source_target_pairs={{32,0},{33,1},{34,2},{35,3},{36,4},{37,5},{38,6},{39,7},{40,8},{41... | collective-permute-start | bytes 786440 | tf_op jit(solution)/shard_map/ppermute | solution.py:11
  421.8 15.8 %all-to-all-start.9 = ((f32[64,8,256]{2,1,0:T(8,128)}), f32[64,8,256]{2,1,0:T(8,128)S(1)}, u32[]{:S(2)}, u32[]{:S(2)}) async-start(f32[64,8,256]{2,1,0:T(8,128)} %copy.330), calls=%async_computation.9 | async-start | bytes 1048576 | tf_op jit(solution)/shard_map/all_to_all | solution.py:15
  (86 other events, 362.4 us)

commit v7 on v5

--- a/solution.py
+++ b/solution.py
@@ -103,6 +103,8 @@
         if senders:
             summed = jnp.einsum("st,trw->srw", recv_onehot, fwd_arrived, precision=highest)
             incoming = shift_leaf(summed, [(l, l + 1) for l in senders])
+            if turn == 0:
+                incoming, inverse_t, couple_t = lax.optimization_barrier((incoming, inverse_t, couple_t))
         else:
             incoming = zero_chunk
         if down:

time: 448 us -> 459 us (1.025)
  waiting for transfers between devices: 135 us -> 146 us
    all_to_all x8, waiting for transfers between devices: 85.9 us -> 95 us  [exchange(): lax.all_to_all(buffer, 'panel', split_axis=0, concat_axis=0, tiled=True)]
    unnamed x34 -> x36, local copies, waits for them, and re-layouts: 18 us -> 18.1 us
  transfers between devices with their start and end apart: 20 -> 20, of which waited for: 13 -> 13; matrix products, arithmetic and copies ran while one was open for 16% -> 15% of each run, Pallas kernels for 0% -> 0%
where the time goes in v7:
time: 459 us; the launch traced here: 451 us
  matrix products  165 us (36%)
  waiting for transfers between devices  146 us (32%)
  starting transfers between devices  66.8 us (15%)
  local copies, waits for them, and re-layouts  33.3 us (7%)
  blocking collectives  30.4 us (7%)
  other arithmetic  7.35 us (2%)
    all_to_all x8, waiting for transfers between devices, exchange(): lax.all_to_all(buffer, 'panel', split_axis=0, concat_axis=0, tiled=True)  95 us
    ppermute x12, waiting for transfers between devices, shift_leaf(): return lax.ppermute(block, 'leaf', pairs)  51.4 us
    dot_general x7, matrix products, body(): jnp.einsum('nrw,nwv->nrv', rhs - incoming, diag_inverse, precision=main)  46.3 us
    all_to_all x8, starting transfers between devices, exchange(): lax.all_to_all(buffer, 'panel', split_axis=0, concat_axis=0, tiled=True)  43.4 us
    dot_general x6, matrix products, body(): lowered = jnp.einsum('nrv,nvw->nrw', picked, couple_t, precision=main)  39 us
    dot_general x7, matrix products, body(): jnp.einsum('nrw,nwv->nrv', source, inverse_t, precision=main)  38.1 us
    all_to_all x2, blocking collectives, exchange(): lax.all_to_all(buffer, 'panel', split_axis=0, concat_axis=0, tiled=True)  30.4 us
    dot_general x6, matrix products, body(): jnp.einsum('nrw,nwv->nrv', forward_part, couple_block, precision=main)  29 us
  transfers between devices with their start and end apart: 20, of which 13 were waited for; matrix products, arithmetic and copies ran while one was open for 15% of the time, Pallas kernels for 0%

profile of v7, /device:TPU:1, one launch (start us, length us, event | category | flops | bytes accessed | tf_op | source)
XLA Modules:
  0.0 451.0 jit_solution(8885985132651071667)
XLA Ops:
  3.8 8.6 %all-to-all-start = ((f32[32,2,1]{1,2,0:T(1,128)}), f32[32,2,1]{1,2,0:T(1,128)S(1)}, u32[]{:S(2)}, u32[]{:S(2)}) async-start(f32[32,2,1]{1,2,0:T(1,128)} %bitcast.5), calls=%async_computation | async-start | bytes 32768 | tf_op jit(solution)/shard_map/all_to_all | solution.py:16
  14.1 6.8 %fusion.22 = f32[32,8,256]{2,1,0:T(8,128)S(1)} fusion(f32[1,32,256,256]{3,2,1,0:T(8,128)} %param.6, f32[32,8,256]{2,0,1:T(8,128)S(1)} %select_bitcast_fusion), kind=kOutput, calls=%fused_computation.22 | convolution fusion | flops 201326592 | bytes 8912896 | tf_op jit(solution)/shard_map/nrw,nwv->nrv/dot_general | solution.py:77
  26.6 7.4 %all-to-all-start.1 = ((f32[64,8,256]{2,1,0:T(8,128)}), f32[64,8,256]{2,1,0:T(8,128)S(1)}, u32[]{:S(2)}, u32[]{:S(2)}) async-start(f32[64,8,256]{2,1,0:T(8,128)} %copy.186), calls=%async_computation.1 | async-start | bytes 1048576 | tf_op jit(solution)/shard_map/all_to_all | solution.py:16
  35.3 10.3 %all-to-all-done.1 = f32[64,8,256]{2,1,0:T(8,128)S(1)} async-done(((f32[64,8,256]{2,1,0:T(8,128)}), f32[64,8,256]{2,1,0:T(8,128)S(1)}, u32[]{:S(2)}, u32[]{:S(2)}) %all-to-all-start.1) | async-done | bytes 524320 | tf_op jit(solution)/shard_map/all_to_all | solution.py:16
  49.8 9.1 %copy.180 = f32[1,32,256,256]{2,3,1,0:T(8,128)} copy(f32[1,32,256,256]{3,2,1,0:T(8,128)} %param.6) | data formatting | bytes 16777216 | tf_op args[1]
  58.9 9.0 %copy.183 = f32[1,32,256,256]{2,3,1,0:T(8,128)} copy(f32[1,32,256,256]{3,2,1,0:T(8,128)} %param.7) | data formatting | bytes 16777216 | tf_op args[2]
  81.8 15.3 %all_to_all.54 = f32[64,8,256]{2,1,0:T(8,128)S(1)} all-to-all(f32[64,8,256]{2,1,0:T(8,128)S(1)} %copy.192), channel_id=1, replica_groups=mesh['leaf'=4,'panel'=32] {'panel'}, dimensions={0} | all-to-all | bytes 1048576 | tf_op jit(solution)/shard_map/all_to_all | solution.py:16
  118.9 15.2 %all_to_all.55 = f32[64,8,256]{2,1,0:T(8,128)S(1)} all-to-all(f32[64,8,256]{2,1,0:T(8,128)S(1)} %copy.198), channel_id=1, replica_groups=mesh['leaf'=4,'panel'=32] {'panel'}, dimensions={0} | all-to-all | bytes 1048576 | tf_op jit(solution)/shard_map/all_to_all | solution.py:16
  144.9 6.6 %select_select_fusion.7 = (f32[32,8,256]{2,1,0:T(8,128)S(1)}, f32[32,8,256]{2,1,0:T(8,128)S(1)}) fusion(f32[32,8,256]{2,1,0:T(8,128)S(1)} %fusion.18, f32[32,8,256]{2,1,0:T(8,128)S(1)} %fusion.20, f32[32,8,256]{2,1,0:T(8,128)S(1)} %fusion.22, pred[]{:T(512)S(6)} %eq.371, pred[]{:T(512)S(6)} %eq.370, pred[]{:T(512)S(6)} %eq.369, pred[]{:T(512)S(6)} %eq.368, ...), kind=kOutput, calls=%fused_computation.147 | convolution fusion | flops 201588736 | bytes 9961476 | tf_op jit(solution)/shard_map/nrw,nwv->nrv/dot_general | solution.py:77
  171.0 17.0 %all-to-all-done.4 = f32[64,16,256]{2,1,0:T(8,128)} async-done(((f32[64,16,256]{2,1,0:T(8,128)}), f32[64,16,256]{2,1,0:T(8,128)}, u32[]{:S(2)}, u32[]{:S(2)}) %all-to-all-start.4) | async-done | bytes 1048608 | tf_op jit(solution)/shard_map/all_to_all | solution.py:16
  201.6 6.6 %fusion.14 = f32[32,8,256]{2,1,0:T(8,128)S(1)} fusion(f32[1,32,256,256]{3,2,1,0:T(8,128)} %param.6, f32[32,8,256]{2,0,1:T(8,128)S(1)} %bitcast_subtract_fusion.3), kind=kOutput, calls=%fused_computation.14 | convolution fusion | flops 201326592 | bytes 8912896 | tf_op jit(solution)/shard_map/nrw,nwv->nrv/dot_general | solution.py:77
  224.8 17.0 %all-to-all-done.5 = f32[64,16,256]{2,1,0:T(8,128)} async-done(((f32[64,16,256]{2,1,0:T(8,128)}), f32[64,16,256]{2,1,0:T(8,128)}, u32[]{:S(2)}, u32[]{:S(2)}) %all-to-all-start.5) | async-done | bytes 1048608 | tf_op jit(solution)/shard_map/all_to_all | solution.py:16
  245.0 6.6 %fusion.68 = f32[32,8,256]{2,1,0:T(8,128)S(1)} fusion(f32[32,256,256]{2,1,0:T(8,128)} %bitcast.159, f32[32,8,256]{2,0,1:T(8,128)S(1)} %fusion.31), kind=kOutput, calls=%fused_computation.80 | convolution fusion | flops 201326592 | bytes 8912896 | tf_op jit(solution)/shard_map/nrv,nvw->nrw/dot_general | solution.py:84
  251.9 6.7 %broadcast_select_fusion.3 = (f32[32,8,256]{2,1,0:T(8,128)S(1)}, f32[32,8,256]{2,1,0:T(8,128)S(1)}, f32[32,8,256]{2,1,0:T(8,128)S(1)}, f32[32,8,256]{2,1,0:T(8,128)S(1)}, f32[32,8,256]{2,1,0:T(8,128)S(1)}) fusion(pred[]{:T(512)S(6)} %eq.399, f32[32,8,256]{2,1,0:T(8,128)S(1)} %fusion.14, f32[32,8,256]{2,1,0:T(8,128)S(1)} %get-tuple-element.14, ...), kind=kOutput, calls=%fused_computation.164 | convolution fusion | flops 201850880 | bytes 11272200 | tf_op jit(solution)/shard_map/nrw,nwv->nrv/dot_general | solution.py:77
  269.1 13.9 %collective-permute-done.7 = f32[32,8,256]{2,1,0:T(8,128)S(1)} collective-permute-done((f32[32,8,256]{2,1,0:T(8,128)S(1)}, f32[32,8,256]{2,1,0:T(8,128)S(1)}, u32[]{:S(2)}, u32[]{:S(2)}) %collective-permute-start.7) | collective-permute-done | bytes 262176 | tf_op jit(solution)/shard_map/ppermute | solution.py:12
  289.8 17.0 %all-to-all-done.6 = f32[64,16,256]{2,1,0:T(8,128)S(1)} async-done(((f32[64,16,256]{2,1,0:T(8,128)}), f32[64,16,256]{2,1,0:T(8,128)S(1)}, u32[]{:S(2)}, u32[]{:S(2)}) %all-to-all-start.6) | async-done | bytes 1048608 | tf_op jit(solution)/shard_map/all_to_all | solution.py:16
  308.6 6.6 %fusion.63 = f32[32,8,256]{2,1,0:T(8,128)S(1)} fusion(f32[32,256,256]{2,1,0:T(8,128)} %bitcast.160, f32[32,8,256]{2,0,1:T(8,128)S(1)} %fusion.27), kind=kOutput, calls=%fused_computation.75 | convolution fusion | flops 201326592 | bytes 8912896 | tf_op jit(solution)/shard_map/nrv,nvw->nrw/dot_general | solution.py:84
  315.6 6.6 %broadcast_select_fusion.11 = (f32[32,8,256]{2,1,0:T(8,128)S(1)}, f32[32,8,256]{2,1,0:T(8,128)S(1)}, f32[32,8,256]{2,1,0:T(8,128)S(1)}, f32[32,8,256]{2,1,0:T(8,128)S(1)}) fusion(f32[32,8,256]{2,1,0:T(8,128)S(1)} %get-tuple-element.21, pred[]{:T(512)S(6)} %eq.335, f32[32,8,256]{2,1,0:T(8,128)S(1)} %copy-done.4, pred[]{:T(512)S(6)} %eq.402, ...), kind=kOutput, calls=%fused_computation.181 | convolution fusion | flops 201588736 | bytes 10747908 | tf_op jit(solution)/shard_map/nrw,nwv->nrv/dot_general | solution.py:77
  327.6 8.3 %collective-permute-done.9 = f32[32,8,256]{2,1,0:T(8,128)S(1)} collective-permute-done((f32[32,8,256]{2,1,0:T(8,128)S(1)}, f32[32,8,256]{2,1,0:T(8,128)S(1)}, u32[]{:S(2)}, u32[]{:S(2)}) %collective-permute-start.9) | collective-permute-done | bytes 262176 | tf_op jit(solution)/shard_map/ppermute | solution.py:12
  342.4 11.6 %all-to-all-done.7 = f32[64,8,256]{2,1,0:T(8,128)S(1)} async-done(((f32[64,8,256]{2,1,0:T(8,128)}), f32[64,8,256]{2,1,0:T(8,128)S(1)}, u32[]{:S(2)}, u32[]{:S(2)}) %all-to-all-start.7) | async-done | bytes 524320 | tf_op jit(solution)/shard_map/all_to_all | solution.py:16
  368.6 8.7 %collective-permute-done.10 = f32[32,8,256]{2,1,0:T(8,128)S(1)} collective-permute-done((f32[32,8,256]{2,1,0:T(8,128)S(1)}, f32[32,8,256]{2,1,0:T(8,128)S(1)}, u32[]{:S(2)}, u32[]{:S(2)}) %collective-permute-start.10) | collective-permute-done | bytes 262176 | tf_op jit(solution)/shard_map/ppermute | solution.py:12
  383.1 11.7 %all-to-all-done.8 = f32[64,8,256]{2,1,0:T(8,128)S(1)} async-done(((f32[64,8,256]{2,1,0:T(8,128)}), f32[64,8,256]{2,1,0:T(8,128)S(1)}, u32[]{:S(2)}, u32[]{:S(2)}) %all-to-all-start.8) | async-done | bytes 524320 | tf_op jit(solution)/shard_map/all_to_all | solution.py:16
  409.4 8.7 %collective-permute-done.11 = f32[32,8,256]{2,1,0:T(8,128)S(1)} collective-permute-done((f32[32,8,256]{2,1,0:T(8,128)S(1)}, f32[32,8,256]{2,1,0:T(8,128)S(1)}, u32[]{:S(2)}, u32[]{:S(2)}) %collective-permute-start.11) | collective-permute-done | bytes 262176 | tf_op jit(solution)/shard_map/ppermute | solution.py:12
  425.4 10.4 %all-to-all-done.9 = f32[64,8,256]{2,1,0:T(8,128)S(1)} async-done(((f32[64,8,256]{2,1,0:T(8,128)}), f32[64,8,256]{2,1,0:T(8,128)S(1)}, u32[]{:S(2)}, u32[]{:S(2)}) %all-to-all-start.9) | async-done | bytes 524320 | tf_op jit(solution)/shard_map/all_to_all | solution.py:16
  (147 shorter events, 203.2 us)
Async XLA Ops:
  3.8 22.8 %all-to-all-start = ((f32[32,2,1]{1,2,0:T(1,128)}), f32[32,2,1]{1,2,0:T(1,128)S(1)}, u32[]{:S(2)}, u32[]{:S(2)}) async-start(f32[32,2,1]{1,2,0:T(1,128)} %bitcast.5), calls=%async_computation | async-start | bytes 32768 | tf_op jit(solution)/shard_map/all_to_all | solution.py:16
  26.6 19.0 %all-to-all-start.1 = ((f32[64,8,256]{2,1,0:T(8,128)}), f32[64,8,256]{2,1,0:T(8,128)S(1)}, u32[]{:S(2)}, u32[]{:S(2)}) async-start(f32[64,8,256]{2,1,0:T(8,128)} %copy.186), calls=%async_computation.1 | async-start | bytes 1048576 | tf_op jit(solution)/shard_map/all_to_all | solution.py:16
  46.1 21.8 %collective-permute-start = (f32[32,8,256]{2,0,1:T(8,128)S(1)}, f32[32,8,256]{2,0,1:T(8,128)S(1)}, u32[]{:S(2)}, u32[]{:S(2)}) collective-permute-start(f32[32,8,256]{2,0,1:T(8,128)S(1)} %fusion.49), channel_id=1, source_target_pairs={{0,32},{1,33},{2,34},{3,35},{4,36},{5,37},{6,38},{7,39},{8,40},{9,... | collective-permute-start | bytes 786440 | tf_op jit(solution)/shard_map/ppermute | solution.py:12
  97.6 7.4 %collective-permute-start.1 = (f32[32,8,256]{2,0,1:T(8,128)S(1)}, f32[32,8,256]{2,0,1:T(8,128)S(1)}, u32[]{:S(2)}, u32[]{:S(2)}) collective-permute-start(f32[32,8,256]{2,0,1:T(8,128)S(1)} %fusion.47), channel_id=1, source_target_pairs={{0,32},{32,64},{1,33},{33,65},{2,34},{34,66},{3,35},{35,67},{4,36}... | collective-permute-start | bytes 786440 | tf_op jit(solution)/shard_map/ppermute | solution.py:12
  134.6 10.0 %collective-permute-start.2 = (f32[32,8,256]{2,0,1:T(8,128)S(1)}, f32[32,8,256]{2,0,1:T(8,128)S(1)}, u32[]{:S(2)}, u32[]{:S(2)}) collective-permute-start(f32[32,8,256]{2,0,1:T(8,128)S(1)} %fusion.45), channel_id=1, source_target_pairs={{0,32},{32,64},{64,96},{1,33},{33,65},{65,97},{2,34},{34,66},{66,9... | collective-permute-start | bytes 786440 | tf_op jit(solution)/shard_map/ppermute | solution.py:12
  144.9 14.4 %slice-start.6 = ((s8[8388608]{0:T(1024)(128)(4,1)}), s8[4194304]{0:T(1024)(128)(4,1)S(1)}, s32[]{:S(2)}) async-start(s8[8388608]{0:T(1024)(128)(4,1)} %bitcast.152), calls=%async_computation.16 | async-start | bytes 8388608
  158.2 5.7 %collective-permute-start.3 = (f32[32,8,256]{2,1,0:T(8,128)S(1)}, f32[32,8,256]{2,1,0:T(8,128)S(1)}, u32[]{:S(2)}, u32[]{:S(2)}) collective-permute-start(f32[32,8,256]{2,1,0:T(8,128)S(1)} %fusion.124), channel_id=1, source_target_pairs={{96,64},{97,65},{98,66},{99,67},{100,68},{101,69},{102,70},{103,71... | collective-permute-start | bytes 786440 | tf_op jit(solution)/shard_map/ppermute | solution.py:12
  166.1 21.9 %all-to-all-start.4 = ((f32[64,16,256]{2,1,0:T(8,128)}), f32[64,16,256]{2,1,0:T(8,128)}, u32[]{:S(2)}, u32[]{:S(2)}) async-start(f32[64,16,256]{2,1,0:T(8,128)} %copy.205), calls=%async_computation.4 | async-start | bytes 2097152 | tf_op jit(solution)/shard_map/all_to_all | solution.py:16
  190.2 18.0 %slice-start = ((s8[8388608]{0:T(1024)(128)(4,1)}), s8[4194304]{0:T(1024)(128)(4,1)S(1)}, s32[]{:S(2)}) async-start(s8[8388608]{0:T(1024)(128)(4,1)} %bitcast.143), calls=%async_computation.10 | async-start | bytes 8388608
  190.2 11.0 %collective-permute-start.4 = (f32[32,8,256]{2,0,1:T(8,128)S(1)}, f32[32,8,256]{2,0,1:T(8,128)S(1)}, u32[]{:S(2)}, u32[]{:S(2)}) collective-permute-start(f32[32,8,256]{2,0,1:T(8,128)S(1)} %fusion.37), channel_id=1, source_target_pairs={{0,32},{32,64},{64,96},{1,33},{33,65},{65,97},{2,34},{34,66},{66,9... | collective-permute-start | bytes 786440 | tf_op jit(solution)/shard_map/ppermute | solution.py:12
  212.4 5.5 %collective-permute-start.5 = (f32[32,8,256]{2,1,0:T(8,128)S(1)}, f32[32,8,256]{2,1,0:T(8,128)S(1)}, u32[]{:S(2)}, u32[]{:S(2)}) collective-permute-start(f32[32,8,256]{2,1,0:T(8,128)S(1)} %fusion.119), channel_id=1, source_target_pairs={{64,32},{96,64},{65,33},{97,65},{66,34},{98,66},{67,35},{99,67},{6... | collective-permute-start | bytes 786440 | tf_op jit(solution)/shard_map/ppermute | solution.py:12
  220.1 21.7 %all-to-all-start.5 = ((f32[64,16,256]{2,1,0:T(8,128)}), f32[64,16,256]{2,1,0:T(8,128)}, u32[]{:S(2)}, u32[]{:S(2)}) async-start(f32[64,16,256]{2,1,0:T(8,128)} %copy.214), calls=%async_computation.5 | async-start | bytes 2097152 | tf_op jit(solution)/shard_map/all_to_all | solution.py:16
  244.0 7.6 %collective-permute-start.6 = (f32[32,8,256]{2,0,1:T(8,128)S(1)}, f32[32,8,256]{2,0,1:T(8,128)S(1)}, u32[]{:S(2)}, u32[]{:S(2)}) collective-permute-start(f32[32,8,256]{2,0,1:T(8,128)S(1)} %fusion.33), channel_id=1, source_target_pairs={{32,64},{64,96},{33,65},{65,97},{34,66},{66,98},{35,67},{67,99},{3... | collective-permute-start | bytes 786440 | tf_op jit(solution)/shard_map/ppermute | solution.py:12
  244.9 13.7 %slice-start.2 = ((s8[8388608]{0:T(1024)(128)(4,1)}), s8[4194304]{0:T(1024)(128)(4,1)S(1)}, s32[]{:S(2)}) async-start(s8[8388608]{0:T(1024)(128)(4,1)} %bitcast.146), calls=%async_computation.12 | async-start | bytes 8388608
  262.8 20.2 %collective-permute-start.7 = (f32[32,8,256]{2,1,0:T(8,128)S(1)}, f32[32,8,256]{2,1,0:T(8,128)S(1)}, u32[]{:S(2)}, u32[]{:S(2)}) collective-permute-start(f32[32,8,256]{2,1,0:T(8,128)S(1)} %fusion.114), channel_id=1, source_target_pairs={{32,0},{64,32},{96,64},{33,1},{65,33},{97,65},{34,2},{66,34},{98,6... | collective-permute-start | bytes 786440 | tf_op jit(solution)/shard_map/ppermute | solution.py:12
  285.2 21.6 %all-to-all-start.6 = ((f32[64,16,256]{2,1,0:T(8,128)}), f32[64,16,256]{2,1,0:T(8,128)S(1)}, u32[]{:S(2)}, u32[]{:S(2)}) async-start(f32[64,16,256]{2,1,0:T(8,128)} %copy.223), calls=%async_computation.6 | async-start | bytes 2097152 | tf_op jit(solution)/shard_map/all_to_all | solution.py:16
  307.8 7.5 %collective-permute-start.8 = (f32[32,8,256]{2,0,1:T(8,128)S(1)}, f32[32,8,256]{2,0,1:T(8,128)S(1)}, u32[]{:S(2)}, u32[]{:S(2)}) collective-permute-start(f32[32,8,256]{2,0,1:T(8,128)S(1)} %fusion.29), channel_id=1, source_target_pairs={{64,96},{65,97},{66,98},{67,99},{68,100},{69,101},{70,102},{71,103... | collective-permute-start | bytes 786440 | tf_op jit(solution)/shard_map/ppermute | solution.py:12
  308.6 13.6 %slice-start.4 = ((s8[8388608]{0:T(1024)(128)(4,1)}), s8[4194304]{0:T(1024)(128)(4,1)S(1)}, s32[]{:S(2)}) async-start(s8[8388608]{0:T(1024)(128)(4,1)} %bitcast.149), calls=%async_computation.14 | async-start | bytes 8388608
  326.4 9.6 %collective-permute-start.9 = (f32[32,8,256]{2,1,0:T(8,128)S(1)}, f32[32,8,256]{2,1,0:T(8,128)S(1)}, u32[]{:S(2)}, u32[]{:S(2)}) collective-permute-start(f32[32,8,256]{2,1,0:T(8,128)S(1)} %fusion.100), channel_id=1, source_target_pairs={{32,0},{64,32},{96,64},{33,1},{65,33},{97,65},{34,2},{66,34},{98,6... | collective-permute-start | bytes 786440 | tf_op jit(solution)/shard_map/ppermute | solution.py:12
  337.6 16.4 %all-to-all-start.7 = ((f32[64,8,256]{2,1,0:T(8,128)}), f32[64,8,256]{2,1,0:T(8,128)S(1)}, u32[]{:S(2)}, u32[]{:S(2)}) async-start(f32[64,8,256]{2,1,0:T(8,128)} %copy.230), calls=%async_computation.7 | async-start | bytes 1048576 | tf_op jit(solution)/shard_map/all_to_all | solution.py:16
  367.3 10.0 %collective-permute-start.10 = (f32[32,8,256]{2,1,0:T(8,128)S(1)}, f32[32,8,256]{2,1,0:T(8,128)S(1)}, u32[]{:S(2)}, u32[]{:S(2)}) collective-permute-start(f32[32,8,256]{2,1,0:T(8,128)S(1)} %fusion.98), channel_id=1, source_target_pairs={{32,0},{64,32},{33,1},{65,33},{34,2},{66,34},{35,3},{67,35},{36,4}... | collective-permute-start | bytes 786440 | tf_op jit(solution)/shard_map/ppermute | solution.py:12
  379.0 15.8 %all-to-all-start.8 = ((f32[64,8,256]{2,1,0:T(8,128)}), f32[64,8,256]{2,1,0:T(8,128)S(1)}, u32[]{:S(2)}, u32[]{:S(2)}) async-start(f32[64,8,256]{2,1,0:T(8,128)} %copy.234), calls=%async_computation.8 | async-start | bytes 1048576 | tf_op jit(solution)/shard_map/all_to_all | solution.py:16
  408.1 10.0 %collective-permute-start.11 = (f32[32,8,256]{2,1,0:T(8,128)S(1)}, f32[32,8,256]{2,1,0:T(8,128)S(1)}, u32[]{:S(2)}, u32[]{:S(2)}) collective-permute-start(f32[32,8,256]{2,1,0:T(8,128)S(1)} %fusion.96), channel_id=1, source_target_pairs={{32,0},{33,1},{34,2},{35,3},{36,4},{37,5},{38,6},{39,7},{40,8},{41... | collective-permute-start | bytes 786440 | tf_op jit(solution)/shard_map/ppermute | solution.py:12
  419.8 16.1 %all-to-all-start.9 = ((f32[64,8,256]{2,1,0:T(8,128)}), f32[64,8,256]{2,1,0:T(8,128)S(1)}, u32[]{:S(2)}, u32[]{:S(2)}) async-start(f32[64,8,256]{2,1,0:T(8,128)} %copy.238), calls=%async_computation.9 | async-start | bytes 1048576 | tf_op jit(solution)/shard_map/all_to_all | solution.py:16
  (13 other events, 116.9 us)

commit v8 on v7

--- a/solution.py
+++ b/solution.py
@@ -98,13 +98,15 @@
             fwd_arrived, bwd_arrived = arrived[:, :rows], arrived[:, rows:]
         elif senders:
             fwd_arrived = exchange(fwd_buffer)
+            if turn == 0:
+                fwd_arrived, inverse_t = lax.optimization_barrier((fwd_arrived, inverse_t))
         elif down:
             bwd_arrived = exchange(bwd_buffer)
         if senders:
             summed = jnp.einsum("st,trw->srw", recv_onehot, fwd_arrived, precision=highest)
             incoming = shift_leaf(summed, [(l, l + 1) for l in senders])
             if turn == 0:
-                incoming, inverse_t, couple_t = lax.optimization_barrier((incoming, inverse_t, couple_t))
+                incoming, couple_t = lax.optimization_barrier((incoming, couple_t))
         else:
             incoming = zero_chunk
         if down:

time: 459 us -> 453 us (0.987)
  waiting for transfers between devices: 146 us -> 138 us
    all_to_all x8, waiting for transfers between devices: 95 us -> 85.7 us  [exchange(): lax.all_to_all(buffer, 'panel', split_axis=0, concat_axis=0, tiled=True)]
where the time goes in v8:
time: 453 us; the launch traced here: 445 us
  matrix products  165 us (36%)
  waiting for transfers between devices  138 us (30%)
  starting transfers between devices  66.3 us (15%)
  local copies, waits for them, and re-layouts  33.3 us (7%)
  blocking collectives  33 us (7%)
  other arithmetic  7.35 us (2%)
    all_to_all x8, waiting for transfers between devices, exchange(): lax.all_to_all(buffer, 'panel', split_axis=0, concat_axis=0, tiled=True)  85.7 us
    ppermute x12, waiting for transfers between devices, shift_leaf(): return lax.ppermute(block, 'leaf', pairs)  52.2 us
    dot_general x7, matrix products, body(): jnp.einsum('nrw,nwv->nrv', rhs - incoming, diag_inverse, precision=main)  46.3 us
    all_to_all x8, starting transfers between devices, exchange(): lax.all_to_all(buffer, 'panel', split_axis=0, concat_axis=0, tiled=True)  43.8 us
    dot_general x6, matrix products, body(): lowered = jnp.einsum('nrv,nvw->nrw', picked, couple_t, precision=main)  39 us
    dot_general x7, matrix products, body(): jnp.einsum('nrw,nwv->nrv', source, inverse_t, precision=main)  38.1 us
    all_to_all x2, blocking collectives, exchange(): lax.all_to_all(buffer, 'panel', split_axis=0, concat_axis=0, tiled=True)  33 us
    dot_general x6, matrix products, body(): jnp.einsum('nrw,nwv->nrv', forward_part, couple_block, precision=main)  29 us
  transfers between devices with their start and end apart: 20, of which 13 were waited for; matrix products, arithmetic and copies ran while one was open for 15% of the time, Pallas kernels for 0%

profile of v8, /device:TPU:1, one launch (start us, length us, event | category | flops | bytes accessed | tf_op | source)
XLA Modules:
  0.0 444.7 jit_solution(17937297145313639138)
XLA Ops:
  3.8 8.6 %all-to-all-start = ((f32[32,2,1]{1,2,0:T(1,128)}), f32[32,2,1]{1,2,0:T(1,128)S(1)}, u32[]{:S(2)}, u32[]{:S(2)}) async-start(f32[32,2,1]{1,2,0:T(1,128)} %bitcast.5), calls=%async_computation | async-start | bytes 32768 | tf_op jit(solution)/shard_map/all_to_all | solution.py:16
  14.1 6.8 %fusion.22 = f32[32,8,256]{2,1,0:T(8,128)S(1)} fusion(f32[1,32,256,256]{3,2,1,0:T(8,128)} %param.6, f32[32,8,256]{2,0,1:T(8,128)S(1)} %select_bitcast_fusion), kind=kOutput, calls=%fused_computation.22 | convolution fusion | flops 201326592 | bytes 8912896 | tf_op jit(solution)/shard_map/nrw,nwv->nrv/dot_general | solution.py:77
  26.6 7.4 %all-to-all-start.1 = ((f32[64,8,256]{2,1,0:T(8,128)}), f32[64,8,256]{2,1,0:T(8,128)S(1)}, u32[]{:S(2)}, u32[]{:S(2)}) async-start(f32[64,8,256]{2,1,0:T(8,128)} %copy.186), calls=%async_computation.1 | async-start | bytes 1048576 | tf_op jit(solution)/shard_map/all_to_all | solution.py:16
  34.0 9.1 %copy.180 = f32[1,32,256,256]{2,3,1,0:T(8,128)} copy(f32[1,32,256,256]{3,2,1,0:T(8,128)} %param.6) | data formatting | bytes 16777216 | tf_op args[1]
  49.8 9.0 %copy.183 = f32[1,32,256,256]{2,3,1,0:T(8,128)} copy(f32[1,32,256,256]{3,2,1,0:T(8,128)} %param.7) | data formatting | bytes 16777216 | tf_op args[2]
  72.8 17.9 %all_to_all.54 = f32[64,8,256]{2,1,0:T(8,128)S(1)} all-to-all(f32[64,8,256]{2,1,0:T(8,128)S(1)} %copy.192), channel_id=1, replica_groups=mesh['leaf'=4,'panel'=32] {'panel'}, dimensions={0} | all-to-all | bytes 1048576 | tf_op jit(solution)/shard_map/all_to_all | solution.py:16
  112.4 15.2 %all_to_all.55 = f32[64,8,256]{2,1,0:T(8,128)S(1)} all-to-all(f32[64,8,256]{2,1,0:T(8,128)S(1)} %copy.198), channel_id=1, replica_groups=mesh['leaf'=4,'panel'=32] {'panel'}, dimensions={0} | all-to-all | bytes 1048576 | tf_op jit(solution)/shard_map/all_to_all | solution.py:16
  138.4 6.6 %select_select_fusion.7 = (f32[32,8,256]{2,1,0:T(8,128)S(1)}, f32[32,8,256]{2,1,0:T(8,128)S(1)}) fusion(f32[32,8,256]{2,1,0:T(8,128)S(1)} %fusion.18, f32[32,8,256]{2,1,0:T(8,128)S(1)} %fusion.20, f32[32,8,256]{2,1,0:T(8,128)S(1)} %fusion.22, pred[]{:T(512)S(6)} %eq.371, pred[]{:T(512)S(6)} %eq.370, pred[]{:T(512)S(6)} %eq.369, pred[]{:T(512)S(6)} %eq.368, ...), kind=kOutput, calls=%fused_computation.147 | convolution fusion | flops 201588736 | bytes 9961476 | tf_op jit(solution)/shard_map/nrw,nwv->nrv/dot_general | solution.py:77
  145.2 6.6 %fusion.124 = f32[32,8,256]{2,1,0:T(8,128)S(1)} fusion(f32[32,256,256]{2,1,0:T(8,128)} %bitcast.139, f32[32,8,256]{2,1,0:T(8,128)S(1)} %get-tuple-element.31, f32[32,8,256]{2,1,0:T(8,128)S(1)} %get-tuple-element.18, f32[32,8,256]{2,1,0:T(8,128)S(1)} %get-tuple-element.17, f32[32,8,256]{2,1,0:T(8,128)S(1)} %get-tuple-element.16, pred[]{:T(512)S(6)} %eq.377, ...), kind=kOutput, calls=%fused_computation.140 | convolution fusion | flops 201523200 | bytes 9699331 | tf_op jit(solution)/shard_map/nrw,nwv->nrv/dot_general | solution.py:86
  164.4 16.9 %all-to-all-done.4 = f32[64,16,256]{2,1,0:T(8,128)} async-done(((f32[64,16,256]{2,1,0:T(8,128)}), f32[64,16,256]{2,1,0:T(8,128)}, u32[]{:S(2)}, u32[]{:S(2)}) %all-to-all-start.4) | async-done | bytes 1048608 | tf_op jit(solution)/shard_map/all_to_all | solution.py:16
  194.7 6.6 %fusion.14 = f32[32,8,256]{2,1,0:T(8,128)S(1)} fusion(f32[1,32,256,256]{3,2,1,0:T(8,128)} %param.6, f32[32,8,256]{2,0,1:T(8,128)S(1)} %bitcast_subtract_fusion.3), kind=kOutput, calls=%fused_computation.14 | convolution fusion | flops 201326592 | bytes 8912896 | tf_op jit(solution)/shard_map/nrw,nwv->nrv/dot_general | solution.py:77
  217.9 17.0 %all-to-all-done.5 = f32[64,16,256]{2,1,0:T(8,128)} async-done(((f32[64,16,256]{2,1,0:T(8,128)}), f32[64,16,256]{2,1,0:T(8,128)}, u32[]{:S(2)}, u32[]{:S(2)}) %all-to-all-start.5) | async-done | bytes 1048608 | tf_op jit(solution)/shard_map/all_to_all | solution.py:16
  238.0 6.6 %fusion.68 = f32[32,8,256]{2,1,0:T(8,128)S(1)} fusion(f32[32,256,256]{2,1,0:T(8,128)} %bitcast.159, f32[32,8,256]{2,0,1:T(8,128)S(1)} %fusion.31), kind=kOutput, calls=%fused_computation.80 | convolution fusion | flops 201326592 | bytes 8912896 | tf_op jit(solution)/shard_map/nrv,nvw->nrw/dot_general | solution.py:84
  245.0 6.7 %broadcast_select_fusion.3 = (f32[32,8,256]{2,1,0:T(8,128)S(1)}, f32[32,8,256]{2,1,0:T(8,128)S(1)}, f32[32,8,256]{2,1,0:T(8,128)S(1)}, f32[32,8,256]{2,1,0:T(8,128)S(1)}, f32[32,8,256]{2,1,0:T(8,128)S(1)}) fusion(pred[]{:T(512)S(6)} %eq.399, f32[32,8,256]{2,1,0:T(8,128)S(1)} %fusion.14, f32[32,8,256]{2,1,0:T(8,128)S(1)} %get-tuple-element.16, ...), kind=kOutput, calls=%fused_computation.164 | convolution fusion | flops 201850880 | bytes 11272200 | tf_op jit(solution)/shard_map/nrw,nwv->nrv/dot_general | solution.py:77
  262.2 14.4 %collective-permute-done.7 = f32[32,8,256]{2,1,0:T(8,128)S(1)} collective-permute-done((f32[32,8,256]{2,1,0:T(8,128)S(1)}, f32[32,8,256]{2,1,0:T(8,128)S(1)}, u32[]{:S(2)}, u32[]{:S(2)}) %collective-permute-start.7) | collective-permute-done | bytes 262176 | tf_op jit(solution)/shard_map/ppermute | solution.py:12
  283.4 17.0 %all-to-all-done.6 = f32[64,16,256]{2,1,0:T(8,128)S(1)} async-done(((f32[64,16,256]{2,1,0:T(8,128)}), f32[64,16,256]{2,1,0:T(8,128)S(1)}, u32[]{:S(2)}, u32[]{:S(2)}) %all-to-all-start.6) | async-done | bytes 1048608 | tf_op jit(solution)/shard_map/all_to_all | solution.py:16
  302.3 6.6 %fusion.63 = f32[32,8,256]{2,1,0:T(8,128)S(1)} fusion(f32[32,256,256]{2,1,0:T(8,128)} %bitcast.160, f32[32,8,256]{2,0,1:T(8,128)S(1)} %fusion.27), kind=kOutput, calls=%fused_computation.75 | convolution fusion | flops 201326592 | bytes 8912896 | tf_op jit(solution)/shard_map/nrv,nvw->nrw/dot_general | solution.py:84
  309.3 6.6 %broadcast_select_fusion.11 = (f32[32,8,256]{2,1,0:T(8,128)S(1)}, f32[32,8,256]{2,1,0:T(8,128)S(1)}, f32[32,8,256]{2,1,0:T(8,128)S(1)}, f32[32,8,256]{2,1,0:T(8,128)S(1)}) fusion(f32[32,8,256]{2,1,0:T(8,128)S(1)} %get-tuple-element.23, pred[]{:T(512)S(6)} %eq.335, f32[32,8,256]{2,1,0:T(8,128)S(1)} %copy-done.4, pred[]{:T(512)S(6)} %eq.402, ...), kind=kOutput, calls=%fused_computation.181 | convolution fusion | flops 201588736 | bytes 10747908 | tf_op jit(solution)/shard_map/nrw,nwv->nrv/dot_general | solution.py:77
  321.3 8.3 %collective-permute-done.9 = f32[32,8,256]{2,1,0:T(8,128)S(1)} collective-permute-done((f32[32,8,256]{2,1,0:T(8,128)S(1)}, f32[32,8,256]{2,1,0:T(8,128)S(1)}, u32[]{:S(2)}, u32[]{:S(2)}) %collective-permute-start.9) | collective-permute-done | bytes 262176 | tf_op jit(solution)/shard_map/ppermute | solution.py:12
  336.1 11.6 %all-to-all-done.7 = f32[64,8,256]{2,1,0:T(8,128)S(1)} async-done(((f32[64,8,256]{2,1,0:T(8,128)}), f32[64,8,256]{2,1,0:T(8,128)S(1)}, u32[]{:S(2)}, u32[]{:S(2)}) %all-to-all-start.7) | async-done | bytes 524320 | tf_op jit(solution)/shard_map/all_to_all | solution.py:16
  362.3 8.7 %collective-permute-done.10 = f32[32,8,256]{2,1,0:T(8,128)S(1)} collective-permute-done((f32[32,8,256]{2,1,0:T(8,128)S(1)}, f32[32,8,256]{2,1,0:T(8,128)S(1)}, u32[]{:S(2)}, u32[]{:S(2)}) %collective-permute-start.10) | collective-permute-done | bytes 262176 | tf_op jit(solution)/shard_map/ppermute | solution.py:12
  376.8 11.7 %all-to-all-done.8 = f32[64,8,256]{2,1,0:T(8,128)S(1)} async-done(((f32[64,8,256]{2,1,0:T(8,128)}), f32[64,8,256]{2,1,0:T(8,128)S(1)}, u32[]{:S(2)}, u32[]{:S(2)}) %all-to-all-start.8) | async-done | bytes 524320 | tf_op jit(solution)/shard_map/all_to_all | solution.py:16
  403.1 8.8 %collective-permute-done.11 = f32[32,8,256]{2,1,0:T(8,128)S(1)} collective-permute-done((f32[32,8,256]{2,1,0:T(8,128)S(1)}, f32[32,8,256]{2,1,0:T(8,128)S(1)}, u32[]{:S(2)}, u32[]{:S(2)}) %collective-permute-start.11) | collective-permute-done | bytes 262176 | tf_op jit(solution)/shard_map/ppermute | solution.py:12
  419.1 10.4 %all-to-all-done.9 = f32[64,8,256]{2,1,0:T(8,128)S(1)} async-done(((f32[64,8,256]{2,1,0:T(8,128)}), f32[64,8,256]{2,1,0:T(8,128)S(1)}, u32[]{:S(2)}, u32[]{:S(2)}) %all-to-all-start.9) | async-done | bytes 524320 | tf_op jit(solution)/shard_map/all_to_all | solution.py:16
  (147 shorter events, 197.6 us)
Async XLA Ops:
  3.8 22.8 %all-to-all-start = ((f32[32,2,1]{1,2,0:T(1,128)}), f32[32,2,1]{1,2,0:T(1,128)S(1)}, u32[]{:S(2)}, u32[]{:S(2)}) async-start(f32[32,2,1]{1,2,0:T(1,128)} %bitcast.5), calls=%async_computation | async-start | bytes 32768 | tf_op jit(solution)/shard_map/all_to_all | solution.py:16
  26.6 19.0 %all-to-all-start.1 = ((f32[64,8,256]{2,1,0:T(8,128)}), f32[64,8,256]{2,1,0:T(8,128)S(1)}, u32[]{:S(2)}, u32[]{:S(2)}) async-start(f32[64,8,256]{2,1,0:T(8,128)} %copy.186), calls=%async_computation.1 | async-start | bytes 1048576 | tf_op jit(solution)/shard_map/all_to_all | solution.py:16
  46.1 12.8 %collective-permute-start = (f32[32,8,256]{2,0,1:T(8,128)S(1)}, f32[32,8,256]{2,0,1:T(8,128)S(1)}, u32[]{:S(2)}, u32[]{:S(2)}) collective-permute-start(f32[32,8,256]{2,0,1:T(8,128)S(1)} %fusion.49), channel_id=1, source_target_pairs={{0,32},{1,33},{2,34},{3,35},{4,36},{5,37},{6,38},{7,39},{8,40},{9,... | collective-permute-start | bytes 786440 | tf_op jit(solution)/shard_map/ppermute | solution.py:12
  91.1 7.4 %collective-permute-start.1 = (f32[32,8,256]{2,0,1:T(8,128)S(1)}, f32[32,8,256]{2,0,1:T(8,128)S(1)}, u32[]{:S(2)}, u32[]{:S(2)}) collective-permute-start(f32[32,8,256]{2,0,1:T(8,128)S(1)} %fusion.47), channel_id=1, source_target_pairs={{0,32},{32,64},{1,33},{33,65},{2,34},{34,66},{3,35},{35,67},{4,36}... | collective-permute-start | bytes 786440 | tf_op jit(solution)/shard_map/ppermute | solution.py:12
  128.1 10.0 %collective-permute-start.2 = (f32[32,8,256]{2,0,1:T(8,128)S(1)}, f32[32,8,256]{2,0,1:T(8,128)S(1)}, u32[]{:S(2)}, u32[]{:S(2)}) collective-permute-start(f32[32,8,256]{2,0,1:T(8,128)S(1)} %fusion.45), channel_id=1, source_target_pairs={{0,32},{32,64},{64,96},{1,33},{33,65},{65,97},{2,34},{34,66},{66,9... | collective-permute-start | bytes 786440 | tf_op jit(solution)/shard_map/ppermute | solution.py:12
  138.4 14.0 %slice-start.6 = ((s8[8388608]{0:T(1024)(128)(4,1)}), s8[4194304]{0:T(1024)(128)(4,1)S(1)}, s32[]{:S(2)}) async-start(s8[8388608]{0:T(1024)(128)(4,1)} %bitcast.152), calls=%async_computation.16 | async-start | bytes 8388608
  151.7 5.3 %collective-permute-start.3 = (f32[32,8,256]{2,1,0:T(8,128)S(1)}, f32[32,8,256]{2,1,0:T(8,128)S(1)}, u32[]{:S(2)}, u32[]{:S(2)}) collective-permute-start(f32[32,8,256]{2,1,0:T(8,128)S(1)} %fusion.124), channel_id=1, source_target_pairs={{96,64},{97,65},{98,66},{99,67},{100,68},{101,69},{102,70},{103,71... | collective-permute-start | bytes 786440 | tf_op jit(solution)/shard_map/ppermute | solution.py:12
  159.2 22.1 %all-to-all-start.4 = ((f32[64,16,256]{2,1,0:T(8,128)}), f32[64,16,256]{2,1,0:T(8,128)}, u32[]{:S(2)}, u32[]{:S(2)}) async-start(f32[64,16,256]{2,1,0:T(8,128)} %copy.205), calls=%async_computation.4 | async-start | bytes 2097152 | tf_op jit(solution)/shard_map/all_to_all | solution.py:16
  183.5 17.8 %slice-start = ((s8[8388608]{0:T(1024)(128)(4,1)}), s8[4194304]{0:T(1024)(128)(4,1)S(1)}, s32[]{:S(2)}) async-start(s8[8388608]{0:T(1024)(128)(4,1)} %bitcast.143), calls=%async_computation.10 | async-start | bytes 8388608
  183.5 10.8 %collective-permute-start.4 = (f32[32,8,256]{2,0,1:T(8,128)S(1)}, f32[32,8,256]{2,0,1:T(8,128)S(1)}, u32[]{:S(2)}, u32[]{:S(2)}) collective-permute-start(f32[32,8,256]{2,0,1:T(8,128)S(1)} %fusion.37), channel_id=1, source_target_pairs={{0,32},{32,64},{64,96},{1,33},{33,65},{65,97},{2,34},{34,66},{66,9... | collective-permute-start | bytes 786440 | tf_op jit(solution)/shard_map/ppermute | solution.py:12
  205.5 5.5 %collective-permute-start.5 = (f32[32,8,256]{2,1,0:T(8,128)S(1)}, f32[32,8,256]{2,1,0:T(8,128)S(1)}, u32[]{:S(2)}, u32[]{:S(2)}) collective-permute-start(f32[32,8,256]{2,1,0:T(8,128)S(1)} %fusion.119), channel_id=1, source_target_pairs={{64,32},{96,64},{65,33},{97,65},{66,34},{98,66},{67,35},{99,67},{6... | collective-permute-start | bytes 786440 | tf_op jit(solution)/shard_map/ppermute | solution.py:12
  213.1 21.7 %all-to-all-start.5 = ((f32[64,16,256]{2,1,0:T(8,128)}), f32[64,16,256]{2,1,0:T(8,128)}, u32[]{:S(2)}, u32[]{:S(2)}) async-start(f32[64,16,256]{2,1,0:T(8,128)} %copy.214), calls=%async_computation.5 | async-start | bytes 2097152 | tf_op jit(solution)/shard_map/all_to_all | solution.py:16
  237.1 7.6 %collective-permute-start.6 = (f32[32,8,256]{2,0,1:T(8,128)S(1)}, f32[32,8,256]{2,0,1:T(8,128)S(1)}, u32[]{:S(2)}, u32[]{:S(2)}) collective-permute-start(f32[32,8,256]{2,0,1:T(8,128)S(1)} %fusion.33), channel_id=1, source_target_pairs={{32,64},{64,96},{33,65},{65,97},{34,66},{66,98},{35,67},{67,99},{3... | collective-permute-start | bytes 786440 | tf_op jit(solution)/shard_map/ppermute | solution.py:12
  238.0 13.7 %slice-start.2 = ((s8[8388608]{0:T(1024)(128)(4,1)}), s8[4194304]{0:T(1024)(128)(4,1)S(1)}, s32[]{:S(2)}) async-start(s8[8388608]{0:T(1024)(128)(4,1)} %bitcast.146), calls=%async_computation.12 | async-start | bytes 8388608
  255.9 20.8 %collective-permute-start.7 = (f32[32,8,256]{2,1,0:T(8,128)S(1)}, f32[32,8,256]{2,1,0:T(8,128)S(1)}, u32[]{:S(2)}, u32[]{:S(2)}) collective-permute-start(f32[32,8,256]{2,1,0:T(8,128)S(1)} %fusion.114), channel_id=1, source_target_pairs={{32,0},{64,32},{96,64},{33,1},{65,33},{97,65},{34,2},{66,34},{98,6... | collective-permute-start | bytes 786440 | tf_op jit(solution)/shard_map/ppermute | solution.py:12
  278.8 21.6 %all-to-all-start.6 = ((f32[64,16,256]{2,1,0:T(8,128)}), f32[64,16,256]{2,1,0:T(8,128)S(1)}, u32[]{:S(2)}, u32[]{:S(2)}) async-start(f32[64,16,256]{2,1,0:T(8,128)} %copy.223), calls=%async_computation.6 | async-start | bytes 2097152 | tf_op jit(solution)/shard_map/all_to_all | solution.py:16
  301.4 7.5 %collective-permute-start.8 = (f32[32,8,256]{2,0,1:T(8,128)S(1)}, f32[32,8,256]{2,0,1:T(8,128)S(1)}, u32[]{:S(2)}, u32[]{:S(2)}) collective-permute-start(f32[32,8,256]{2,0,1:T(8,128)S(1)} %fusion.29), channel_id=1, source_target_pairs={{64,96},{65,97},{66,98},{67,99},{68,100},{69,101},{70,102},{71,103... | collective-permute-start | bytes 786440 | tf_op jit(solution)/shard_map/ppermute | solution.py:12
  302.3 13.6 %slice-start.4 = ((s8[8388608]{0:T(1024)(128)(4,1)}), s8[4194304]{0:T(1024)(128)(4,1)S(1)}, s32[]{:S(2)}) async-start(s8[8388608]{0:T(1024)(128)(4,1)} %bitcast.149), calls=%async_computation.14 | async-start | bytes 8388608
  320.0 9.6 %collective-permute-start.9 = (f32[32,8,256]{2,1,0:T(8,128)S(1)}, f32[32,8,256]{2,1,0:T(8,128)S(1)}, u32[]{:S(2)}, u32[]{:S(2)}) collective-permute-start(f32[32,8,256]{2,1,0:T(8,128)S(1)} %fusion.100), channel_id=1, source_target_pairs={{32,0},{64,32},{96,64},{33,1},{65,33},{97,65},{34,2},{66,34},{98,6... | collective-permute-start | bytes 786440 | tf_op jit(solution)/shard_map/ppermute | solution.py:12
  331.3 16.4 %all-to-all-start.7 = ((f32[64,8,256]{2,1,0:T(8,128)}), f32[64,8,256]{2,1,0:T(8,128)S(1)}, u32[]{:S(2)}, u32[]{:S(2)}) async-start(f32[64,8,256]{2,1,0:T(8,128)} %copy.230), calls=%async_computation.7 | async-start | bytes 1048576 | tf_op jit(solution)/shard_map/all_to_all | solution.py:16
  361.0 10.0 %collective-permute-start.10 = (f32[32,8,256]{2,1,0:T(8,128)S(1)}, f32[32,8,256]{2,1,0:T(8,128)S(1)}, u32[]{:S(2)}, u32[]{:S(2)}) collective-permute-start(f32[32,8,256]{2,1,0:T(8,128)S(1)} %fusion.98), channel_id=1, source_target_pairs={{32,0},{64,32},{33,1},{65,33},{34,2},{66,34},{35,3},{67,35},{36,4}... | collective-permute-start | bytes 786440 | tf_op jit(solution)/shard_map/ppermute | solution.py:12
  372.6 15.9 %all-to-all-start.8 = ((f32[64,8,256]{2,1,0:T(8,128)}), f32[64,8,256]{2,1,0:T(8,128)S(1)}, u32[]{:S(2)}, u32[]{:S(2)}) async-start(f32[64,8,256]{2,1,0:T(8,128)} %copy.234), calls=%async_computation.8 | async-start | bytes 1048576 | tf_op jit(solution)/shard_map/all_to_all | solution.py:16
  401.8 10.0 %collective-permute-start.11 = (f32[32,8,256]{2,1,0:T(8,128)S(1)}, f32[32,8,256]{2,1,0:T(8,128)S(1)}, u32[]{:S(2)}, u32[]{:S(2)}) collective-permute-start(f32[32,8,256]{2,1,0:T(8,128)S(1)} %fusion.96), channel_id=1, source_target_pairs={{32,0},{33,1},{34,2},{35,3},{36,4},{37,5},{38,6},{39,7},{40,8},{41... | collective-permute-start | bytes 786440 | tf_op jit(solution)/shard_map/ppermute | solution.py:12
  413.4 16.1 %all-to-all-start.9 = ((f32[64,8,256]{2,1,0:T(8,128)}), f32[64,8,256]{2,1,0:T(8,128)S(1)}, u32[]{:S(2)}, u32[]{:S(2)}) async-start(f32[64,8,256]{2,1,0:T(8,128)} %copy.238), calls=%async_computation.9 | async-start | bytes 1048576 | tf_op jit(solution)/shard_map/all_to_all | solution.py:16
  (13 other events, 116.4 us)

commit v9 on v5

--- a/solution.py
+++ b/solution.py
@@ -48,9 +48,7 @@
     slot_iota = jnp.arange(slot_count, dtype=jnp.int32)
     send_onehot = (slot_iota[:, None] == dest_slot[None, :]).astype(jnp.float32)
     send_ids = jnp.dot(send_onehot, (positions + 1).astype(jnp.float32), precision=highest) - 1.0
-    arrived_ids = exchange(send_ids)
     node_float = node_iota.astype(jnp.float32)
-    recv_onehot = (arrived_ids[None, :] == node_float[:, None]).astype(jnp.float32)
 
     chunks = CHUNKS
     rows = total_cols // chunks
@@ -96,6 +94,11 @@
         if senders and down:
             arrived = exchange(jnp.concatenate([fwd_buffer, bwd_buffer], axis=1))
             fwd_arrived, bwd_arrived = arrived[:, :rows], arrived[:, rows:]
+        elif turn == 0:
+            id_rows = jnp.broadcast_to(send_ids[:, None, None], (slot_count, 8, width))
+            arrived = exchange(jnp.concatenate([fwd_buffer, id_rows], axis=1))
+            fwd_arrived = arrived[:, :rows]
+            recv_onehot = (arrived[:, rows, 0][None, :] == node_float[:, None]).astype(jnp.float32)
         elif senders:
             fwd_arrived = exchange(fwd_buffer)
         elif down:

time: 448 us -> 446 us (level)
  starting transfers between devices: 66.4 us -> 59 us
  waiting for transfers between devices: 135 us -> 142 us
    all_to_all x8 -> x7, starting transfers between devices: 43.2 us -> 35.9 us  [exchange(): lax.all_to_all(buffer, 'panel', split_axis=0, concat_axis=0, tiled=True)]
    all_to_all x8 -> x7, waiting for transfers between devices: 85.9 us -> 92.5 us  [exchange(): lax.all_to_all(buffer, 'panel', split_axis=0, concat_axis=0, tiled=True)]
    unnamed x34 -> x36, local copies, waits for them, and re-layouts: 18 us -> 18.1 us
  transfers between devices with their start and end apart: 20 -> 19, of which waited for: 13 -> 13; matrix products, arithmetic and copies ran while one was open for 16% -> 12% of each run, Pallas kernels for 0% -> 0%
where the time goes in v9:
time: 446 us; the launch traced here: 438 us
  matrix products  163 us (37%)
  waiting for transfers between devices  142 us (32%)
  starting transfers between devices  59 us (13%)
  local copies, waits for them, and re-layouts  33.1 us (7%)
  blocking collectives  31.6 us (7%)
  other arithmetic  7.14 us (2%)
    all_to_all x7, waiting for transfers between devices, exchange(): lax.all_to_all(buffer, 'panel', split_axis=0, concat_axis=0, tiled=True)  92.5 us
    ppermute x12, waiting for transfers between devices, shift_leaf(): return lax.ppermute(block, 'leaf', pairs)  49 us
    dot_general x7, matrix products, body(): jnp.einsum('nrw,nwv->nrv', rhs - incoming, diag_inverse, precision=main)  45.9 us
    dot_general x6, matrix products, body(): lowered = jnp.einsum('nrv,nvw->nrw', picked, couple_t, precision=main)  39 us
    all_to_all x7, starting transfers between devices, exchange(): lax.all_to_all(buffer, 'panel', split_axis=0, concat_axis=0, tiled=True)  35.9 us
    dot_general x7, matrix products, body(): jnp.einsum('nrw,nwv->nrv', source, inverse_t, precision=main)  35.7 us
    all_to_all x2, blocking collectives, exchange(): lax.all_to_all(buffer, 'panel', split_axis=0, concat_axis=0, tiled=True)  31.6 us
    dot_general x6, matrix products, body(): jnp.einsum('nrw,nwv->nrv', forward_part, couple_block, precision=main)  31.3 us
  transfers between devices with their start and end apart: 19, of which 13 were waited for; matrix products, arithmetic and copies ran while one was open for 12% of the time, Pallas kernels for 0%

profile of v9, /device:TPU:1, one launch (start us, length us, event | category | flops | bytes accessed | tf_op | source)
XLA Modules:
  0.0 438.0 jit_solution(8522333933917571196)
XLA Ops:
  17.4 8.6 %all-to-all-start = ((f32[64,16,256]{2,1,0:T(8,128)}), f32[64,16,256]{2,1,0:T(8,128)S(1)}, u32[]{:S(2)}, u32[]{:S(2)}) async-start(f32[64,16,256]{2,1,0:T(8,128)} %copy.161), calls=%async_computation | async-start | bytes 2097152 | tf_op jit(solution)/shard_map/all_to_all | solution.py:16
  26.0 16.9 %all-to-all-done = f32[64,16,256]{2,1,0:T(8,128)S(1)} async-done(((f32[64,16,256]{2,1,0:T(8,128)}), f32[64,16,256]{2,1,0:T(8,128)S(1)}, u32[]{:S(2)}, u32[]{:S(2)}) %all-to-all-start) | async-done | bytes 1048608 | tf_op jit(solution)/shard_map/all_to_all | solution.py:16
  67.0 15.8 %all_to_all.45 = f32[64,8,256]{2,1,0:T(8,128)S(1)} all-to-all(f32[64,8,256]{2,1,0:T(8,128)S(1)} %copy.167), channel_id=1, replica_groups=mesh['leaf'=4,'panel'=32] {'panel'}, dimensions={0} | all-to-all | bytes 1048576 | tf_op jit(solution)/shard_map/all_to_all | solution.py:16
  107.3 15.7 %all_to_all.46 = f32[64,8,256]{2,1,0:T(8,128)S(1)} all-to-all(f32[64,8,256]{2,1,0:T(8,128)S(1)} %copy.173), channel_id=1, replica_groups=mesh['leaf'=4,'panel'=32] {'panel'}, dimensions={0} | all-to-all | bytes 1048576 | tf_op jit(solution)/shard_map/all_to_all | solution.py:16
  127.7 9.0 %copy.155 = f32[1,32,256,256]{2,3,1,0:T(8,128)} copy(f32[1,32,256,256]{3,2,1,0:T(8,128)} %param.6) | data formatting | bytes 16777216 | tf_op args[1]
  137.0 6.6 %select_select_fusion.7 = (f32[32,8,256]{2,1,0:T(8,128)S(1)}, f32[32,8,256]{2,1,0:T(8,128)S(1)}) fusion(f32[32,8,256]{2,1,0:T(8,128)S(1)} %fusion.44, f32[32,8,256]{2,1,0:T(8,128)S(1)} %fusion.46, f32[32,8,256]{2,1,0:T(8,128)S(1)} %fusion.48, pred[]{:T(512)S(6)} %eq.371, pred[]{:T(512)S(6)} %eq.370, pred[]{:T(512)S(6)} %eq.369, pred[]{:T(512)S(6)} %eq.368, ...), kind=kOutput, calls=%fused_computation.161 | convolution fusion | flops 201588736 | bytes 9961476 | tf_op jit(solution)/shard_map/nrw,nwv->nrv/dot_general | solution.py:75
  162.2 9.0 %copy.158 = f32[1,32,256,256]{2,3,1,0:T(8,128)} copy(f32[1,32,256,256]{3,2,1,0:T(8,128)} %param.7) | data formatting | bytes 16777216 | tf_op args[2]
  171.2 7.9 %all-to-all-done.3 = f32[64,16,256]{2,1,0:T(8,128)} async-done(((f32[64,16,256]{2,1,0:T(8,128)}), f32[64,16,256]{2,1,0:T(8,128)}, u32[]{:S(2)}, u32[]{:S(2)}) %all-to-all-start.3) | async-done | bytes 1048608 | tf_op jit(solution)/shard_map/all_to_all | solution.py:16
  183.6 6.5 %fusion.8 = f32[32,8,256]{2,1,0:T(8,128)S(1)} fusion(f32[1,32,256,256]{2,3,1,0:T(8,128)} %copy.158, f32[32,8,256]{2,0,1:T(8,128)S(1)} %fusion.61), kind=kOutput, calls=%fused_computation.8 | convolution fusion | flops 201326592 | bytes 8912896 | tf_op jit(solution)/shard_map/nrv,nvw->nrw/dot_general | solution.py:82
  190.4 6.6 %fusion.40 = f32[32,8,256]{2,1,0:T(8,128)S(1)} fusion(f32[1,32,256,256]{3,2,1,0:T(8,128)} %param.6, f32[32,8,256]{2,0,1:T(8,128)S(1)} %bitcast_subtract_fusion.3), kind=kOutput, calls=%fused_computation.40 | convolution fusion | flops 201326592 | bytes 8912896 | tf_op jit(solution)/shard_map/nrw,nwv->nrv/dot_general | solution.py:75
  213.6 17.0 %all-to-all-done.4 = f32[64,16,256]{2,1,0:T(8,128)} async-done(((f32[64,16,256]{2,1,0:T(8,128)}), f32[64,16,256]{2,1,0:T(8,128)}, u32[]{:S(2)}, u32[]{:S(2)}) %all-to-all-start.4) | async-done | bytes 1048608 | tf_op jit(solution)/shard_map/all_to_all | solution.py:16
  233.7 6.6 %fusion.6 = f32[32,8,256]{2,1,0:T(8,128)S(1)} fusion(f32[1,32,256,256]{2,3,1,0:T(8,128)} %copy.158, f32[32,8,256]{2,0,1:T(8,128)S(1)} %fusion.57), kind=kOutput, calls=%fused_computation.6 | convolution fusion | flops 201326592 | bytes 8912896 | tf_op jit(solution)/shard_map/nrv,nvw->nrw/dot_general | solution.py:82
  240.7 6.7 %broadcast_select_fusion.3 = (f32[32,8,256]{2,1,0:T(8,128)S(1)}, f32[32,8,256]{2,1,0:T(8,128)S(1)}, f32[32,8,256]{2,1,0:T(8,128)S(1)}, f32[32,8,256]{2,1,0:T(8,128)S(1)}, f32[32,8,256]{2,1,0:T(8,128)S(1)}) fusion(pred[]{:T(512)S(6)} %eq.399, f32[32,8,256]{2,1,0:T(8,128)S(1)} %fusion.40, f32[32,8,256]{2,1,0:T(8,128)S(1)} %get-tuple-element.8, ...), kind=kOutput, calls=%fused_computation.178 | convolution fusion | flops 201850880 | bytes 11272200 | tf_op jit(solution)/shard_map/nrw,nwv->nrv/dot_general | solution.py:75
  257.9 12.0 %collective-permute-done.7 = f32[32,8,256]{2,1,0:T(8,128)S(1)} collective-permute-done((f32[32,8,256]{2,1,0:T(8,128)S(1)}, f32[32,8,256]{2,1,0:T(8,128)S(1)}, u32[]{:S(2)}, u32[]{:S(2)}) %collective-permute-start.7) | collective-permute-done | bytes 262176 | tf_op jit(solution)/shard_map/ppermute | solution.py:12
  276.7 17.0 %all-to-all-done.5 = f32[64,16,256]{2,1,0:T(8,128)S(1)} async-done(((f32[64,16,256]{2,1,0:T(8,128)}), f32[64,16,256]{2,1,0:T(8,128)S(1)}, u32[]{:S(2)}, u32[]{:S(2)}) %all-to-all-start.5) | async-done | bytes 1048608 | tf_op jit(solution)/shard_map/all_to_all | solution.py:16
  295.5 6.6 %fusion.4 = f32[32,8,256]{2,1,0:T(8,128)S(1)} fusion(f32[1,32,256,256]{2,3,1,0:T(8,128)} %copy.158, f32[32,8,256]{2,0,1:T(8,128)S(1)} %fusion.53), kind=kOutput, calls=%fused_computation.4 | convolution fusion | flops 201326592 | bytes 8912896 | tf_op jit(solution)/shard_map/nrv,nvw->nrw/dot_general | solution.py:82
  302.5 6.6 %broadcast_select_fusion.11 = (f32[32,8,256]{2,1,0:T(8,128)S(1)}, f32[32,8,256]{2,1,0:T(8,128)S(1)}, f32[32,8,256]{2,1,0:T(8,128)S(1)}, f32[32,8,256]{2,1,0:T(8,128)S(1)}) fusion(f32[32,8,256]{2,1,0:T(8,128)S(1)} %get-tuple-element.15, pred[]{:T(512)S(6)} %eq.335, f32[32,8,256]{2,1,0:T(8,128)S(1)} %copy-done.5, pred[]{:T(512)S(6)} %eq.402, ...), kind=kOutput, calls=%fused_computation.195 | convolution fusion | flops 201588736 | bytes 10747908 | tf_op jit(solution)/shard_map/nrw,nwv->nrv/dot_general | solution.py:75
  314.6 8.3 %collective-permute-done.9 = f32[32,8,256]{2,1,0:T(8,128)S(1)} collective-permute-done((f32[32,8,256]{2,1,0:T(8,128)S(1)}, f32[32,8,256]{2,1,0:T(8,128)S(1)}, u32[]{:S(2)}, u32[]{:S(2)}) %collective-permute-start.9) | collective-permute-done | bytes 262176 | tf_op jit(solution)/shard_map/ppermute | solution.py:12
  329.4 11.6 %all-to-all-done.6 = f32[64,8,256]{2,1,0:T(8,128)S(1)} async-done(((f32[64,8,256]{2,1,0:T(8,128)}), f32[64,8,256]{2,1,0:T(8,128)S(1)}, u32[]{:S(2)}, u32[]{:S(2)}) %all-to-all-start.6) | async-done | bytes 524320 | tf_op jit(solution)/shard_map/all_to_all | solution.py:16
  341.4 6.5 %fusion.2 = f32[32,8,256]{2,1,0:T(8,128)S(1)} fusion(f32[1,32,256,256]{2,3,1,0:T(8,128)} %copy.158, f32[32,8,256]{2,0,1:T(8,128)S(1)} %fusion.71), kind=kOutput, calls=%fused_computation.2 | convolution fusion | flops 201326592 | bytes 8912896 | tf_op jit(solution)/shard_map/nrv,nvw->nrw/dot_general | solution.py:82
  355.5 8.7 %collective-permute-done.10 = f32[32,8,256]{2,1,0:T(8,128)S(1)} collective-permute-done((f32[32,8,256]{2,1,0:T(8,128)S(1)}, f32[32,8,256]{2,1,0:T(8,128)S(1)}, u32[]{:S(2)}, u32[]{:S(2)}) %collective-permute-start.10) | collective-permute-done | bytes 262176 | tf_op jit(solution)/shard_map/ppermute | solution.py:12
  370.0 11.7 %all-to-all-done.7 = f32[64,8,256]{2,1,0:T(8,128)S(1)} async-done(((f32[64,8,256]{2,1,0:T(8,128)}), f32[64,8,256]{2,1,0:T(8,128)S(1)}, u32[]{:S(2)}, u32[]{:S(2)}) %all-to-all-start.7) | async-done | bytes 524320 | tf_op jit(solution)/shard_map/all_to_all | solution.py:16
  396.3 8.7 %collective-permute-done.11 = f32[32,8,256]{2,1,0:T(8,128)S(1)} collective-permute-done((f32[32,8,256]{2,1,0:T(8,128)S(1)}, f32[32,8,256]{2,1,0:T(8,128)S(1)}, u32[]{:S(2)}, u32[]{:S(2)}) %collective-permute-start.11) | collective-permute-done | bytes 262176 | tf_op jit(solution)/shard_map/ppermute | solution.py:12
  412.3 10.4 %all-to-all-done.8 = f32[64,8,256]{2,1,0:T(8,128)S(1)} async-done(((f32[64,8,256]{2,1,0:T(8,128)}), f32[64,8,256]{2,1,0:T(8,128)S(1)}, u32[]{:S(2)}, u32[]{:S(2)}) %all-to-all-start.8) | async-done | bytes 524320 | tf_op jit(solution)/shard_map/all_to_all | solution.py:16
  (144 shorter events, 194.7 us)
Async XLA Ops:
  17.4 25.5 %all-to-all-start = ((f32[64,16,256]{2,1,0:T(8,128)}), f32[64,16,256]{2,1,0:T(8,128)S(1)}, u32[]{:S(2)}, u32[]{:S(2)}) async-start(f32[64,16,256]{2,1,0:T(8,128)} %copy.161), calls=%async_computation | async-start | bytes 2097152 | tf_op jit(solution)/shard_map/all_to_all | solution.py:16
  43.9 9.1 %collective-permute-start = (f32[32,8,256]{2,0,1:T(8,128)S(1)}, f32[32,8,256]{2,0,1:T(8,128)S(1)}, u32[]{:S(2)}, u32[]{:S(2)}) collective-permute-start(f32[32,8,256]{2,0,1:T(8,128)S(1)} %fusion.65), channel_id=1, source_target_pairs={{0,32},{1,33},{2,34},{3,35},{4,36},{5,37},{6,38},{7,39},{8,40},{9,... | collective-permute-start | bytes 786440 | tf_op jit(solution)/shard_map/ppermute | solution.py:12
  83.3 10.0 %collective-permute-start.1 = (f32[32,8,256]{2,0,1:T(8,128)S(1)}, f32[32,8,256]{2,0,1:T(8,128)S(1)}, u32[]{:S(2)}, u32[]{:S(2)}) collective-permute-start(f32[32,8,256]{2,0,1:T(8,128)S(1)} %fusion.75), channel_id=1, source_target_pairs={{0,32},{32,64},{1,33},{33,65},{2,34},{34,66},{3,35},{35,67},{4,36}... | collective-permute-start | bytes 786440 | tf_op jit(solution)/shard_map/ppermute | solution.py:12
  123.5 13.2 %collective-permute-start.2 = (f32[32,8,256]{2,0,1:T(8,128)S(1)}, f32[32,8,256]{2,0,1:T(8,128)S(1)}, u32[]{:S(2)}, u32[]{:S(2)}) collective-permute-start(f32[32,8,256]{2,0,1:T(8,128)S(1)} %fusion.73), channel_id=1, source_target_pairs={{0,32},{32,64},{64,96},{1,33},{33,65},{65,97},{2,34},{34,66},{66,9... | collective-permute-start | bytes 786440 | tf_op jit(solution)/shard_map/ppermute | solution.py:12
  147.9 7.6 %collective-permute-start.3 = (f32[32,8,256]{2,1,0:T(8,128)S(1)}, f32[32,8,256]{2,1,0:T(8,128)S(1)}, u32[]{:S(2)}, u32[]{:S(2)}) collective-permute-start(f32[32,8,256]{2,1,0:T(8,128)S(1)} %fusion.22), channel_id=1, source_target_pairs={{96,64},{97,65},{98,66},{99,67},{100,68},{101,69},{102,70},{103,71... | collective-permute-start | bytes 786440 | tf_op jit(solution)/shard_map/ppermute | solution.py:12
  157.6 21.5 %all-to-all-start.3 = ((f32[64,16,256]{2,1,0:T(8,128)}), f32[64,16,256]{2,1,0:T(8,128)}, u32[]{:S(2)}, u32[]{:S(2)}) async-start(f32[64,16,256]{2,1,0:T(8,128)} %copy.180), calls=%async_computation.3 | async-start | bytes 2097152 | tf_op jit(solution)/shard_map/all_to_all | solution.py:16
  181.4 15.6 %slice-start = ((s8[8388608]{0:T(1024)(128)(4,1)}), s8[4194304]{0:T(1024)(128)(4,1)S(1)}, s32[]{:S(2)}) async-start(s8[8388608]{0:T(1024)(128)(4,1)} %bitcast.152), calls=%async_computation.9 | async-start | bytes 8388608
  181.4 8.7 %collective-permute-start.4 = (f32[32,8,256]{2,0,1:T(8,128)S(1)}, f32[32,8,256]{2,0,1:T(8,128)S(1)}, u32[]{:S(2)}, u32[]{:S(2)}) collective-permute-start(f32[32,8,256]{2,0,1:T(8,128)S(1)} %fusion.63), channel_id=1, source_target_pairs={{0,32},{32,64},{64,96},{1,33},{33,65},{65,97},{2,34},{34,66},{66,9... | collective-permute-start | bytes 786440 | tf_op jit(solution)/shard_map/ppermute | solution.py:12
  201.2 5.5 %collective-permute-start.5 = (f32[32,8,256]{2,1,0:T(8,128)S(1)}, f32[32,8,256]{2,1,0:T(8,128)S(1)}, u32[]{:S(2)}, u32[]{:S(2)}) collective-permute-start(f32[32,8,256]{2,1,0:T(8,128)S(1)} %fusion.20), channel_id=1, source_target_pairs={{64,32},{96,64},{65,33},{97,65},{66,34},{98,66},{67,35},{99,67},{6... | collective-permute-start | bytes 786440 | tf_op jit(solution)/shard_map/ppermute | solution.py:12
  208.8 21.7 %all-to-all-start.4 = ((f32[64,16,256]{2,1,0:T(8,128)}), f32[64,16,256]{2,1,0:T(8,128)}, u32[]{:S(2)}, u32[]{:S(2)}) async-start(f32[64,16,256]{2,1,0:T(8,128)} %copy.189), calls=%async_computation.4 | async-start | bytes 2097152 | tf_op jit(solution)/shard_map/all_to_all | solution.py:16
  232.8 7.6 %collective-permute-start.6 = (f32[32,8,256]{2,0,1:T(8,128)S(1)}, f32[32,8,256]{2,0,1:T(8,128)S(1)}, u32[]{:S(2)}, u32[]{:S(2)}) collective-permute-start(f32[32,8,256]{2,0,1:T(8,128)S(1)} %fusion.59), channel_id=1, source_target_pairs={{32,64},{64,96},{33,65},{65,97},{34,66},{66,98},{35,67},{67,99},{3... | collective-permute-start | bytes 786440 | tf_op jit(solution)/shard_map/ppermute | solution.py:12
  233.7 13.7 %slice-start.2 = ((s8[8388608]{0:T(1024)(128)(4,1)}), s8[4194304]{0:T(1024)(128)(4,1)S(1)}, s32[]{:S(2)}) async-start(s8[8388608]{0:T(1024)(128)(4,1)} %bitcast.154), calls=%async_computation.11 | async-start | bytes 8388608
  240.3 13.0 %slice-start.8 = ((s8[8388608]{0:T(1024)(128)(4,1)}), s8[4194304]{0:T(1024)(128)(4,1)S(1)}, s32[]{:S(2)}) async-start(s8[8388608]{0:T(1024)(128)(4,1)} %bitcast.160), calls=%async_computation.17 | async-start | bytes 8388608
  240.7 12.6 %slice-start.9 = ((s8[8388608]{0:T(1024)(128)(4,1)}), s8[4194304]{0:T(1024)(128)(4,1)S(1)}, s32[]{:S(2)}) async-start(s8[8388608]{0:T(1024)(128)(4,1)} %bitcast.160), calls=%async_computation.18 | async-start | bytes 8388608
  251.6 18.3 %collective-permute-start.7 = (f32[32,8,256]{2,1,0:T(8,128)S(1)}, f32[32,8,256]{2,1,0:T(8,128)S(1)}, u32[]{:S(2)}, u32[]{:S(2)}) collective-permute-start(f32[32,8,256]{2,1,0:T(8,128)S(1)} %fusion.18), channel_id=1, source_target_pairs={{32,0},{64,32},{96,64},{33,1},{65,33},{97,65},{34,2},{66,34},{98,6... | collective-permute-start | bytes 786440 | tf_op jit(solution)/shard_map/ppermute | solution.py:12
  272.1 21.6 %all-to-all-start.5 = ((f32[64,16,256]{2,1,0:T(8,128)}), f32[64,16,256]{2,1,0:T(8,128)S(1)}, u32[]{:S(2)}, u32[]{:S(2)}) async-start(f32[64,16,256]{2,1,0:T(8,128)} %copy.198), calls=%async_computation.5 | async-start | bytes 2097152 | tf_op jit(solution)/shard_map/all_to_all | solution.py:16
  294.7 7.5 %collective-permute-start.8 = (f32[32,8,256]{2,0,1:T(8,128)S(1)}, f32[32,8,256]{2,0,1:T(8,128)S(1)}, u32[]{:S(2)}, u32[]{:S(2)}) collective-permute-start(f32[32,8,256]{2,0,1:T(8,128)S(1)} %fusion.55), channel_id=1, source_target_pairs={{64,96},{65,97},{66,98},{67,99},{68,100},{69,101},{70,102},{71,103... | collective-permute-start | bytes 786440 | tf_op jit(solution)/shard_map/ppermute | solution.py:12
  295.5 13.6 %slice-start.4 = ((s8[8388608]{0:T(1024)(128)(4,1)}), s8[4194304]{0:T(1024)(128)(4,1)S(1)}, s32[]{:S(2)}) async-start(s8[8388608]{0:T(1024)(128)(4,1)} %bitcast.156), calls=%async_computation.13 | async-start | bytes 8388608
  313.3 9.6 %collective-permute-start.9 = (f32[32,8,256]{2,1,0:T(8,128)S(1)}, f32[32,8,256]{2,1,0:T(8,128)S(1)}, u32[]{:S(2)}, u32[]{:S(2)}) collective-permute-start(f32[32,8,256]{2,1,0:T(8,128)S(1)} %fusion.16), channel_id=1, source_target_pairs={{32,0},{64,32},{96,64},{33,1},{65,33},{97,65},{34,2},{66,34},{98,6... | collective-permute-start | bytes 786440 | tf_op jit(solution)/shard_map/ppermute | solution.py:12
  324.5 16.4 %all-to-all-start.6 = ((f32[64,8,256]{2,1,0:T(8,128)}), f32[64,8,256]{2,1,0:T(8,128)S(1)}, u32[]{:S(2)}, u32[]{:S(2)}) async-start(f32[64,8,256]{2,1,0:T(8,128)} %copy.205), calls=%async_computation.6 | async-start | bytes 1048576 | tf_op jit(solution)/shard_map/all_to_all | solution.py:16
  354.3 10.0 %collective-permute-start.10 = (f32[32,8,256]{2,1,0:T(8,128)S(1)}, f32[32,8,256]{2,1,0:T(8,128)S(1)}, u32[]{:S(2)}, u32[]{:S(2)}) collective-permute-start(f32[32,8,256]{2,1,0:T(8,128)S(1)} %fusion.14), channel_id=1, source_target_pairs={{32,0},{64,32},{33,1},{65,33},{34,2},{66,34},{35,3},{67,35},{36,4}... | collective-permute-start | bytes 786440 | tf_op jit(solution)/shard_map/ppermute | solution.py:12
  365.9 15.8 %all-to-all-start.7 = ((f32[64,8,256]{2,1,0:T(8,128)}), f32[64,8,256]{2,1,0:T(8,128)S(1)}, u32[]{:S(2)}, u32[]{:S(2)}) async-start(f32[64,8,256]{2,1,0:T(8,128)} %copy.209), calls=%async_computation.7 | async-start | bytes 1048576 | tf_op jit(solution)/shard_map/all_to_all | solution.py:16
  395.1 10.0 %collective-permute-start.11 = (f32[32,8,256]{2,1,0:T(8,128)S(1)}, f32[32,8,256]{2,1,0:T(8,128)S(1)}, u32[]{:S(2)}, u32[]{:S(2)}) collective-permute-start(f32[32,8,256]{2,1,0:T(8,128)S(1)} %fusion.12), channel_id=1, source_target_pairs={{32,0},{33,1},{34,2},{35,3},{36,4},{37,5},{38,6},{39,7},{40,8},{41... | collective-permute-start | bytes 786440 | tf_op jit(solution)/shard_map/ppermute | solution.py:12
  406.7 16.1 %all-to-all-start.8 = ((f32[64,8,256]{2,1,0:T(8,128)}), f32[64,8,256]{2,1,0:T(8,128)S(1)}, u32[]{:S(2)}, u32[]{:S(2)}) async-start(f32[64,8,256]{2,1,0:T(8,128)} %copy.213), calls=%async_computation.8 | async-start | bytes 1048576 | tf_op jit(solution)/shard_map/all_to_all | solution.py:16
  (12 other events, 103.1 us)
